TPU v7x, 32 devices: a whole 2x2x4 slice. The times are simulated.
32 devices in a mesh: member: 2 (over x), row: 16 (over z, y, core).
Axes of the slice: x: 2, y: 2, z: 4, core: 2. Of those that a mesh axis runs over, the one named last changes fastest.
Arguments:
- coarse: bfloat16 [384, 128, 128], P('row', 'member'), parts along dimension 1, may hold values from -6 to 6
- skip_field: bfloat16 [192, 256, 256], P(None, ('member', 'row')), parts along dimension 1, may hold values from -6 to 6
- up_weight: bfloat16 [4, 4, 384, 192], replicated, may hold values from -0.15625 to 0.15625
- up_bias: float32 [192], replicated, may hold values from -3 to 3
- conv_weight: bfloat16 [3, 3, 384, 192], replicated, may hold values from -0.109375 to 0.109375
- conv_bias: float32 [192], replicated, may hold values from -3 to 3
Outputs:
- decoded: bfloat16 [192, 256, 256], P(None, ('member', 'row')), parts along dimension 1
There are 2 independent parts, one for each index of `member`. A program takes and returns all parts, laid end to end along the dimension named above; an argument that names none is the same for every part. Nothing has to cross between parts.
All inputs are finite; a program needn't handle non-finite values.
Results may differ from a plain program's by a relative error of at most 0.0055.
Values may be sent and summed in bfloat16 or wider, within the bound.
No kernel may reach another device: no remote copies, remote signals or barrier semaphores. Data moves between devices by JAX's collectives and lax.ppermute only.
A program may use at most 64 MiB of HBM per device.

v0:
```python
import jax
import jax.numpy as jnp
from jax import lax
from jax.sharding import PartitionSpec as P

TAP_TABLE = (((0, 3), (1, 1)), ((1, 2), (2, 0)))


def extended(x, sides, width):
    for axis, dim in sides:
        peers, length = (lax.axis_size(axis), x.shape[dim])
        up = [(i, (i + 1) % peers) for i in range(peers - 1)]
        down = [(j, i) for i, j in up]
        last = lax.slice_in_dim(x, length - width, length, axis=dim)
        initial = lax.slice_in_dim(x, 0, width, axis=dim)
        before = lax.ppermute(last, axis, up)
        after = lax.ppermute(initial, axis, down)
        x = jnp.concatenate([before, x, after], axis=dim)
    return x


def upsample(padded, weight):
    span_rows = padded.shape[1] - 2
    span_cols = padded.shape[2] - 2
    outputs = weight.shape[3]
    row_parts = []
    for row_par in range(2):
        col_parts = []
        for col_par in range(2):
            summed = jnp.zeros((outputs, span_rows, span_cols), jnp.float32)
            for row_off, row_tap in TAP_TABLE[row_par]:
                for col_off, col_tap in TAP_TABLE[col_par]:
                    window = padded[:, row_off : row_off + span_rows, col_off : col_off + span_cols]
                    summed = summed + jnp.einsum(
                        "chw,co->ohw",
                        window,
                        weight[row_tap, col_tap],
                        preferred_element_type=jnp.float32,
                    )
            col_parts.append(summed)
        row_parts.append(jnp.stack(col_parts, axis=-1))
    stacked = jnp.stack(row_parts, axis=2)
    return stacked.reshape(outputs, 2 * span_rows, 2 * span_cols)


def conv_taps(padded, weight):
    span_rows = padded.shape[1] - 2
    span_cols = padded.shape[2] - 2
    summed = jnp.zeros((weight.shape[3], span_rows, span_cols), jnp.float32)
    for row_tap in range(3):
        for col_tap in range(3):
            window = padded[:, row_tap : row_tap + span_rows, col_tap : col_tap + span_cols]
            summed = summed + jnp.einsum(
                "chw,co->ohw", window, weight[row_tap, col_tap], preferred_element_type=jnp.float32
            )
    return summed


def shards(coarse, skip_field, up_weight, up_bias, conv_weight, conv_bias):
    tiled_rows = lax.all_to_all(coarse, "row", split_axis=1, concat_axis=0, tiled=True)
    rimmed = extended(tiled_rows, (("row", 1),), 1)
    raised = upsample(jnp.pad(rimmed, ((0, 0), (0, 0), (1, 1))), up_weight)
    upsampled = (raised + up_bias[:, None, None]).astype(jnp.bfloat16)
    joined = jnp.concatenate([skip_field, upsampled], axis=0)
    rimmed_fine = extended(joined, (("row", 1),), 1)
    pre = conv_taps(jnp.pad(rimmed_fine, ((0, 0), (0, 0), (1, 1))), conv_weight)
    pre = pre + conv_bias[:, None, None]
    return jax.nn.silu(pre).astype(jnp.bfloat16)


def solution(mesh):
    in_specs = (P("row", "member", None), P(None, ("member", "row"), None), P(), P(), P(), P())
    out_specs = P(None, ("member", "row"), None)
    return jax.shard_map(shards, mesh=mesh, in_specs=in_specs, out_specs=out_specs, check_vma=False)
```

profile of v0, /device:TPU:13, one launch (start us, length us, event | category | flops | bytes accessed | tf_op | source)
XLA Modules:
  0.0 64.4 jit_solution(7071694644316420056)
XLA Ops:
  0.0 2.0 %copy.15 = bf16[24,64,128]{2,0,1:T(8,128)(2,1)} copy(bf16[24,64,128]{2,1,0:T(8,128)(2,1)} %param.6) | data formatting | bytes 786432 | tf_op args[0]
  2.0 6.6 %all-to-all-start = ((bf16[24,64,128]{2,0,1:T(8,128)(2,1)}), bf16[24,64,128]{2,0,1:T(8,128)(2,1)S(1)}, u32[]{:S(2)}, u32[]{:S(2)}) async-start(bf16[24,64,128]{2,0,1:T(8,128)(2,1)} %copy.15), calls=%async_computation | async-start | bytes 786432 | tf_op jit(solution)/shard_map/all_to_all | solution.py:60
  8.6 1.4 %copy.19 = bf16[192,8,256]{2,0,1:T(8,128)(2,1)S(1)} copy(bf16[192,8,256]{2,1,0:T(8,128)(2,1)} %param.7) | data formatting | bytes 1572864 | tf_op args[1]
  10.0 9.3 %all-to-all-done = bf16[24,64,128]{2,0,1:T(8,128)(2,1)S(1)} async-done(((bf16[24,64,128]{2,0,1:T(8,128)(2,1)}), bf16[24,64,128]{2,0,1:T(8,128)(2,1)S(1)}, u32[]{:S(2)}, u32[]{:S(2)}) %all-to-all-start) | async-done | bytes 393248 | tf_op jit(solution)/shard_map/all_to_all | solution.py:60
  20.2 3.7 %collective-permute-start = (bf16[384,1,128]{2,0,1:T(8,128)(2,1)S(1)}, bf16[384,1,128]{2,0,1:T(8,128)(2,1)S(1)}, u32[]{:S(2)}, u32[]{:S(2)}) collective-permute-start(bf16[384,1,128]{2,0,1:T(8,128)(2,1)S(1)} %get-tuple-element.7), channel_id=1, source_target_pairs={{0,1},{1,2},{2,3},{3,4},{4,5},{5,6},{6,7},{7,8},{8,9},{9,10},{10,1... | collective-permute-start | bytes 294920 | tf_op jit(solution)/shard_map/ppermute | solution.py:16
  23.9 1.9 %collective-permute-start.1 = (bf16[384,1,128]{2,0,1:T(8,128)(2,1)S(1)}, bf16[384,1,128]{2,0,1:T(8,128)(2,1)S(1)}, u32[]{:S(2)}, u32[]{:S(2)}) collective-permute-start(bf16[384,1,128]{2,0,1:T(8,128)(2,1)S(1)} %get-tuple-element.8), channel_id=1, source_target_pairs={{1,0},{2,1},{3,2},{4,3},{5,4},{6,5},{7,6},{8,7},{9,8},{10,9},{11,1... | collective-permute-start | bytes 294920 | tf_op jit(solution)/shard_map/ppermute | solution.py:17
  26.1 4.6 %collective-permute-done.1 = bf16[384,1,128]{2,0,1:T(8,128)(2,1)S(1)} collective-permute-done((bf16[384,1,128]{2,0,1:T(8,128)(2,1)S(1)}, bf16[384,1,128]{2,0,1:T(8,128)(2,1)S(1)}, u32[]{:S(2)}, u32[]{:S(2)}) %collective-permute-start.1) | collective-permute-done | bytes 98336 | tf_op jit(solution)/shard_map/ppermute | solution.py:17
  30.7 0.6 fusion.48
  35.2 1.3 %pad_maximum_fusion.8 = f32[192,4,2,128,2]{3,0,1,4,2:T(8,128)} fusion(f32[192,4,1,128,2]{3,0,1,4,2:T(8,128)S(1)} %get-tuple-element.10, f32[192,4,1,128,2]{3,0,1,4,2:T(8,128)S(1)} %get-tuple-element.9), kind=kLoop, calls=%fused_computation.31 | loop fusion | flops 393216 | bytes 3145728 | tf_op jit(solution)/shard_map/stack | solution.py:42
  36.5 2.8 %copy.17 = f32[192,4,2,128,2]{0,4,3,2,1:T(2,128)S(1)} copy(f32[192,4,2,128,2]{3,0,1,4,2:T(8,128)} %pad_maximum_fusion.8) | data formatting | bytes 3145728 | tf_op jit(solution)/shard_map/stack | solution.py:42
  39.3 2.5 %reshape.5 = f32[192,8,256]{0,2,1:T(8,128)} reshape(f32[192,4,2,128,2]{0,4,3,2,1:T(2,128)S(1)} %copy.17) | data formatting | bytes 3145728 | tf_op jit(solution)/shard_map/reshape | solution.py:43
  41.7 1.9 %copy.18 = f32[192,8,256]{2,0,1:T(8,128)S(1)} copy(f32[192,8,256]{0,2,1:T(8,128)} %reshape.5) | data formatting | bytes 3145728 | tf_op jit(solution)/shard_map/reshape | solution.py:43
  43.9 2.1 %collective-permute-start.2 = (bf16[384,1,256]{2,0,1:T(8,128)(2,1)S(1)}, bf16[384,1,256]{2,0,1:T(8,128)(2,1)S(1)}, u32[]{:S(2)}, u32[]{:S(2)}) collective-permute-start(bf16[384,1,256]{2,0,1:T(8,128)(2,1)S(1)} %get-tuple-element.5), channel_id=1, source_target_pairs={{0,1},{1,2},{2,3},{3,4},{4,5},{5,6},{6,7},{7,8},{8,9},{9,10},{10,1... | collective-permute-start | bytes 589832 | tf_op jit(solution)/shard_map/ppermute | solution.py:16
  45.9 2.6 %collective-permute-start.3 = (bf16[384,1,256]{2,0,1:T(8,128)(2,1)S(1)}, bf16[384,1,256]{2,0,1:T(8,128)(2,1)S(1)}, u32[]{:S(2)}, u32[]{:S(2)}) collective-permute-start(bf16[384,1,256]{2,0,1:T(8,128)(2,1)S(1)} %get-tuple-element.6), channel_id=1, source_target_pairs={{1,0},{2,1},{3,2},{4,3},{5,4},{6,5},{7,6},{8,7},{9,8},{10,9},{11,1... | collective-permute-start | bytes 589832 | tf_op jit(solution)/shard_map/ppermute | solution.py:17
  48.5 0.6 fusion.21
  49.1 4.7 %collective-permute-done.3 = bf16[384,1,256]{2,0,1:T(8,128)(2,1)S(1)} collective-permute-done((bf16[384,1,256]{2,0,1:T(8,128)(2,1)S(1)}, bf16[384,1,256]{2,0,1:T(8,128)(2,1)S(1)}, u32[]{:S(2)}, u32[]{:S(2)}) %collective-permute-start.3) | collective-permute-done | bytes 196640 | tf_op jit(solution)/shard_map/ppermute | solution.py:17
  53.8 3.5 %select_maximum_fusion = bf16[384,10,258]{2,0,1:T(8,128)(2,1)S(1)} fusion(bf16[384,1,256]{2,0,1:T(8,128)(2,1)S(1)} %collective-permute-done.3, bf16[384,1,256]{2,0,1:T(8,128)(2,1)S(1)} %collective-permute-done.2, bf16[192,8,256]{2,0,1:T(8,128)(2,1)S(1)} %add_convert_fusion, bf16[192,8,256]{2,0,1:T(8,128)(2,1)S(1)} %copy.19), kind=kLoop, calls=%fused_computation.5 | loop fusion | flops 14860800 | bytes 3947520 | tf_op jit(solution)/shard_map/concatenate | solution.py:18
  57.9 0.7 %fusion.11 = f32[8,256,192]{1,2,0:T(8,128)S(1)} fusion(bf16[384,10,258]{2,0,1:T(8,128)(2,1)S(1)} %select_maximum_fusion, bf16[3,3,384,192]{2,3,1,0:T(8,128)(2,1)S(1)} %copy-done.1), kind=kOutput, calls=%fused_computation.19 | convolution fusion | flops 301989888 | bytes 3293184 | tf_op jit(solution)/shard_map/chw,co->ohw/dot_general | solution.py:53
  58.6 0.6 fusion.13
  59.2 0.7 %fusion.15 = f32[8,256,192]{1,2,0:T(8,128)S(1)} fusion(bf16[384,10,258]{2,0,1:T(8,128)(2,1)S(1)} %select_maximum_fusion, bf16[3,3,384,192]{2,3,1,0:T(8,128)(2,1)S(1)} %copy-done.1), kind=kOutput, calls=%fused_computation.23 | convolution fusion | flops 301989888 | bytes 3293184 | tf_op jit(solution)/shard_map/chw,co->ohw/dot_general | solution.py:53
  60.5 0.6 fusion.7
  61.1 0.6 fusion.17
  61.7 1.4 %fusion.28 = bf16[192,8,256]{2,0,1:T(8,128)(2,1)S(1)} fusion(f32[8,256,192]{1,2,0:T(8,128)S(1)} %fusion.7, f32[8,256,192]{1,2,0:T(8,128)S(1)} %fusion.9, f32[8,256,192]{1,2,0:T(8,128)S(1)} %fusion.11, f32[8,256,192]{1,2,0:T(8,128)S(1)} %fusion.21, f32[8,256,192]{1,2,0:T(8,128)S(1)} %fusion.13, f32[8,256,192]{1,2,0:T(8,128)S(1)} %fusion.15, ...), kind=kOutput, calls=%fused_computation.42 | convolution fusion | flops 307494912 | bytes 15090688 | tf_op jit(solution)/shard_map/chw,co->ohw/dot_general | solution.py:53
  63.1 1.3 %copy.20 = bf16[192,8,256]{2,1,0:T(8,128)(2,1)} copy(bf16[192,8,256]{2,0,1:T(8,128)(2,1)S(1)} %fusion.28) | data formatting | bytes 1572864 | tf_op jit(solution)/shard_map/convert_element_type | solution.py:68
  (33 shorter events, 6.3 us)
Async XLA Ops:
  2.0 17.3 %all-to-all-start = ((bf16[24,64,128]{2,0,1:T(8,128)(2,1)}), bf16[24,64,128]{2,0,1:T(8,128)(2,1)S(1)}, u32[]{:S(2)}, u32[]{:S(2)}) async-start(bf16[24,64,128]{2,0,1:T(8,128)(2,1)} %copy.15), calls=%async_computation | async-start | bytes 786432 | tf_op jit(solution)/shard_map/all_to_all | solution.py:60
  8.6 10.8 %copy-start = (bf16[4,4,384,192]{2,3,1,0:T(8,128)(2,1)S(1)}, bf16[4,4,384,192]{2,3,1,0:T(8,128)(2,1)}, u32[]{:S(2)}) copy-start(bf16[4,4,384,192]{2,3,1,0:T(8,128)(2,1)} %param.8) | copy-start | bytes 7077892
  20.2 5.9 %collective-permute-start = (bf16[384,1,128]{2,0,1:T(8,128)(2,1)S(1)}, bf16[384,1,128]{2,0,1:T(8,128)(2,1)S(1)}, u32[]{:S(2)}, u32[]{:S(2)}) collective-permute-start(bf16[384,1,128]{2,0,1:T(8,128)(2,1)S(1)} %get-tuple-element.7), channel_id=1, source_target_pairs={{0,1},{1,2},{2,3},{3,4},{4,5},{5,6},{6,7},{7,8},{8,9},{9,10},{10,1... | collective-permute-start | bytes 294920 | tf_op jit(solution)/shard_map/ppermute | solution.py:16
  23.9 6.8 %collective-permute-start.1 = (bf16[384,1,128]{2,0,1:T(8,128)(2,1)S(1)}, bf16[384,1,128]{2,0,1:T(8,128)(2,1)S(1)}, u32[]{:S(2)}, u32[]{:S(2)}) collective-permute-start(bf16[384,1,128]{2,0,1:T(8,128)(2,1)S(1)} %get-tuple-element.8), channel_id=1, source_target_pairs={{1,0},{2,1},{3,2},{4,3},{5,4},{6,5},{7,6},{8,7},{9,8},{10,9},{11,1... | collective-permute-start | bytes 294920 | tf_op jit(solution)/shard_map/ppermute | solution.py:17
  41.7 1.9 %copy-start.2 = (f32[192]{0:T(256)S(1)}, f32[192]{0:T(256)}, u32[]{:S(2)}) copy-start(f32[192]{0:T(256)} %param.9) | copy-start | bytes 2308
  43.8 4.7 %copy-start.1 = (bf16[3,3,384,192]{2,3,1,0:T(8,128)(2,1)S(1)}, bf16[3,3,384,192]{2,3,1,0:T(8,128)(2,1)}, u32[]{:S(2)}) copy-start(bf16[3,3,384,192]{2,3,1,0:T(8,128)(2,1)} %param.10) | copy-start | bytes 3981316
  43.9 5.2 %collective-permute-start.2 = (bf16[384,1,256]{2,0,1:T(8,128)(2,1)S(1)}, bf16[384,1,256]{2,0,1:T(8,128)(2,1)S(1)}, u32[]{:S(2)}, u32[]{:S(2)}) collective-permute-start(bf16[384,1,256]{2,0,1:T(8,128)(2,1)S(1)} %get-tuple-element.5), channel_id=1, source_target_pairs={{0,1},{1,2},{2,3},{3,4},{4,5},{5,6},{6,7},{7,8},{8,9},{9,10},{10,1... | collective-permute-start | bytes 589832 | tf_op jit(solution)/shard_map/ppermute | solution.py:16
  45.9 7.9 %collective-permute-start.3 = (bf16[384,1,256]{2,0,1:T(8,128)(2,1)S(1)}, bf16[384,1,256]{2,0,1:T(8,128)(2,1)S(1)}, u32[]{:S(2)}, u32[]{:S(2)}) collective-permute-start(bf16[384,1,256]{2,0,1:T(8,128)(2,1)S(1)} %get-tuple-element.6), channel_id=1, source_target_pairs={{1,0},{2,1},{3,2},{4,3},{5,4},{6,5},{7,6},{8,7},{9,8},{10,9},{11,1... | collective-permute-start | bytes 589832 | tf_op jit(solution)/shard_map/ppermute | solution.py:17
  61.1 0.7 %copy-start.3 = (f32[192]{0:T(256)S(1)}, f32[192]{0:T(256)}, u32[]{:S(2)}) copy-start(f32[192]{0:T(256)} %param.11) | copy-start | bytes 2308
where the time goes:
time: 64.9 us; the launch traced here: 64.4 us
  waiting for transfers between devices  18.6 us (29%)
  starting transfers between devices  16.8 us (26%)
  local copies, waits for them, and re-layouts  12 us (18%)
  matrix products  10.9 us (17%)
  other arithmetic  5.71 us (9%)
    ppermute x2, waiting for transfers between devices, extended(): after = lax.ppermute(initial, axis, down)  9.32 us
    all_to_all x1, waiting for transfers between devices, shards(): lax.all_to_all(coarse, 'row', split_axis=1, concat_axis=0, tiled=True)  9.31 us
    all_to_all x1, starting transfers between devices, shards(): lax.all_to_all(coarse, 'row', split_axis=1, concat_axis=0, tiled=True)  6.55 us
    dot_general x9, matrix products, conv_taps(): jnp.einsum('chw,co->ohw', window, weight[row_tap, col_tap], preferred_ele...  6.21 us
    ppermute x2, starting transfers between devices, extended(): before = lax.ppermute(last, axis, up)  5.72 us
    dot_general x16, matrix products, upsample(): jnp.einsum('chw,co->ohw', window, weight[row_tap, col_tap], preferred_ele...  4.71 us
    ppermute x2, starting transfers between devices, extended(): after = lax.ppermute(initial, axis, down)  4.51 us
    reshape x2, local copies, waits for them, and re-layouts, upsample(): return stacked.reshape(outputs, 2 * span_rows, 2 * span_cols)  4.37 us
  transfers between devices with their start and end apart: 5, of which 3 were waited for; matrix products, arithmetic and copies ran while one was open for 4% of the time, Pallas kernels for 0%

commit v1 on v0

v1 whole, which is shorter than its diff:
```python
import jax
import jax.numpy as jnp
from jax import lax
from jax.sharding import PartitionSpec as P

CHW = ("NCHW", "HWIO", "NCHW")


def coarse_windows(coarse, peers):
    groups, rows, cols = coarse.shape
    tile = rows // peers
    padded = jnp.pad(coarse, ((0, 0), (1, tile - 1), (0, 0)))
    blocks = padded.reshape(groups, peers + 1, tile, cols)
    windows = jnp.concatenate([blocks[:, :peers], blocks[:, 1:, :2]], axis=2)
    windows = jnp.transpose(windows, (1, 0, 2, 3))
    gathered = lax.all_to_all(windows, "row", 0, 0, tiled=True)
    return gathered.reshape(peers * groups, tile + 2, cols)


def skip_rim(skip, peers):
    up = [(i, i + 1) for i in range(peers - 1)]
    down = [(j, i) for i, j in up]
    before = lax.ppermute(skip[:, -1:], "row", up)
    after = lax.ppermute(skip[:, :1], "row", down)
    return jnp.concatenate([before, skip, after], axis=1)


def upsample(window, up_weight, up_bias):
    kernel = up_weight[::-1, ::-1]
    raised = lax.conv_general_dilated(
        window[None],
        kernel,
        window_strides=(1, 1),
        padding=((1, 1), (2, 2)),
        lhs_dilation=(2, 2),
        dimension_numbers=CHW,
        preferred_element_type=jnp.float32,
    )[0]
    return raised + up_bias[:, None, None]


def conv3(field, weight):
    return lax.conv_general_dilated(
        field[None],
        weight,
        window_strides=(1, 1),
        padding=((0, 0), (1, 1)),
        dimension_numbers=CHW,
        preferred_element_type=jnp.float32,
    )[0]


def shards(coarse, skip_field, up_weight, up_bias, conv_weight, conv_bias):
    peers = lax.axis_size("row")
    me = lax.axis_index("row")
    skip_ext = skip_rim(skip_field, peers)
    window = coarse_windows(coarse, peers)
    raised = upsample(window, up_weight, up_bias)
    fine = raised.shape[1]
    row = lax.broadcasted_iota(jnp.int32, (1, fine, 1), 1)
    outside = ((row == 0) & (me == 0)) | ((row == fine - 1) & (me == peers - 1))
    upsampled = jnp.where(outside, 0.0, raised).astype(jnp.bfloat16)
    skips = skip_field.shape[0]
    pre = conv3(skip_ext, conv_weight[:, :, :skips]) + conv3(upsampled, conv_weight[:, :, skips:])
    pre = pre + conv_bias[:, None, None]
    return jax.nn.silu(pre).astype(jnp.bfloat16)


def solution(mesh):
    in_specs = (P("row", "member", None), P(None, ("member", "row"), None), P(), P(), P(), P())
    out_specs = P(None, ("member", "row"), None)
    return jax.shard_map(shards, mesh=mesh, in_specs=in_specs, out_specs=out_specs, check_vma=False)
```

time: 64.9 us -> 59 us (0.909)
  local copies, waits for them, and re-layouts: 12 us -> 22.9 us
  waiting for transfers between devices: 18.6 us -> 7.84 us
  starting transfers between devices: 16.8 us -> 13 us
  matrix products: 10.9 us -> 9.26 us
    dot_general x25 -> x0, matrix products: 10.9 us -> none  [the longest x9 6.21 us: conv_taps(): jnp.einsum('chw,co->ohw', window, weight[row_tap, col_tap], preferred_ele...]
    conv_general_dilated x0 -> x8, local copies, waits for them, and re-layouts: none -> 10.2 us  [the longest x5 8.55 us: conv3(): lax.conv_general_dilated(field[None], weight, window_strides=(1, 1), padd...]
    all_to_all x1, waiting for transfers between devices: 9.31 us -> 0.01 us  [coarse_windows(): gathered = lax.all_to_all(windows, 'row', 0, 0, tiled=True)]
    conv_general_dilated x0 -> x3, matrix products: none -> 9.26 us  [the longest x2 6.09 us: conv3(): lax.conv_general_dilated(field[None], weight, window_strides=(1, 1), padd...]
    reshape x2 -> x0, local copies, waits for them, and re-layouts: 4.37 us -> none  [upsample(): return stacked.reshape(outputs, 2 * span_rows, 2 * span_cols)]
    concatenate x2 -> x0, other arithmetic: 4.1 us -> none  [extended(): x = jnp.concatenate([before, x, after], axis=dim)]
    ppermute x4 -> x2, starting transfers between devices: 10.2 us -> 6.46 us  [the longest x1 4.19 us: skip_rim(): before = lax.ppermute(skip[:, -1:], 'row', up)]
    broadcast_in_dim x0 -> x1, other arithmetic: none -> 3.42 us  [conv3(): field[None]]
  transfers between devices with their start and end apart: 5 -> 3, of which waited for: 3 -> 1; matrix products, arithmetic and copies ran while one was open for 4% -> 37% of each run, Pallas kernels for 0% -> 0%
where the time goes in v1:
time: 59 us; the launch traced here: 58.4 us
  local copies, waits for them, and re-layouts  22.9 us (39%)
  starting transfers between devices  13 us (22%)
  matrix products  9.26 us (16%)
  waiting for transfers between devices  7.84 us (13%)
  other arithmetic  5.11 us (9%)
    conv_general_dilated x5, local copies, waits for them, and re-layouts, conv3(): lax.conv_general_dilated(field[None], weight, window_strides=(1, 1), padd...  8.55 us
    ppermute x1, waiting for transfers between devices, skip_rim(): after = lax.ppermute(skip[:, :1], 'row', down)  7.84 us
    all_to_all x1, starting transfers between devices, coarse_windows(): gathered = lax.all_to_all(windows, 'row', 0, 0, tiled=True)  6.55 us
    conv_general_dilated x2, matrix products, conv3(): lax.conv_general_dilated(field[None], weight, window_strides=(1, 1), padd...  6.09 us
    unnamed x21, local copies, waits for them, and re-layouts  4.96 us
    ppermute x1, starting transfers between devices, skip_rim(): before = lax.ppermute(skip[:, -1:], 'row', up)  4.19 us
    broadcast_in_dim x1, other arithmetic, conv3(): field[None]  3.42 us
    conv_general_dilated x1, matrix products, upsample(): lax.conv_general_dilated(window[None], kernel, window_strides=(1, 1), pad...  3.17 us
  transfers between devices with their start and end apart: 3, of which 1 were waited for; matrix products, arithmetic and copies ran while one was open for 37% of the time, Pallas kernels for 0%

profile of v1, /device:TPU:13, one launch (start us, length us, event | category | flops | bytes accessed | tf_op | source)
XLA Modules:
  0.0 58.4 jit_solution(8797126773264021774)
XLA Ops:
  0.0 1.4 %copy.31 = bf16[24,64,128]{2,0,1:T(8,128)(2,1)S(1)} copy(bf16[24,64,128]{2,1,0:T(8,128)(2,1)} %param.6) | data formatting | bytes 786432 | tf_op args[0]
  1.5 0.9 %maximum_bitcast_fusion.1 = bf16[16,24,6,128]{3,1,2,0:T(8,128)(2,1)} fusion(bf16[24,16,2,128]{3,0,2,1:T(8,128)(2,1)S(1)} %slice.33, bf16[24,16,4,128]{3,0,2,1:T(8,128)(2,1)S(1)} %slice.32), kind=kLoop, calls=%fused_computation.40 | loop fusion | flops 294912 | bytes 1179648 | tf_op jit(solution)/shard_map/transpose | solution.py:15
  2.4 6.6 %all-to-all-start = ((bf16[16,24,6,128]{3,1,2,0:T(8,128)(2,1)}), bf16[16,24,6,128]{3,1,2,0:T(8,128)(2,1)S(1)}, u32[]{:S(2)}, u32[]{:S(2)}) async-start(bf16[16,24,6,128]{3,1,2,0:T(8,128)(2,1)} %maximum_bitcast_fusion.1), calls=%async_computation | async-start | bytes 1179648 | tf_op jit(solution)/shard_map/all_to_all | solution.py:16
  9.0 1.7 %fusion.47 = (bf16[192,1,256]{2,1,0:T(2,128)(2,1)S(1)}, bf16[192,1,256]{2,1,0:T(2,128)(2,1)S(1)}) fusion(bf16[192,8,256]{2,1,0:T(8,128)(2,1)} %param.7), kind=kLoop, calls=%fused_computation.54 | loop fusion | bytes 393216 | tf_op jit(solution)/shard_map/slice | solution.py:23
  10.7 2.3 %collective-permute-start.1 = (bf16[192,1,256]{2,0,1:T(8,128)(2,1)S(1)}, bf16[192,1,256]{2,0,1:T(8,128)(2,1)S(1)}, u32[]{:S(2)}, u32[]{:S(2)}) collective-permute-start(bf16[192,1,256]{2,0,1:T(8,128)(2,1)S(1)} %copy.40), channel_id=1, source_target_pairs={{1,0},{2,1},{3,2},{4,3},{5,4},{6,5},{7,6},{8,7},{9,8},{10,9},{11,1... | collective-permute-start | bytes 294920 | tf_op jit(solution)/shard_map/ppermute | solution.py:24
  13.0 4.2 %collective-permute-start = (bf16[192,1,256]{2,0,1:T(8,128)(2,1)S(1)}, bf16[192,1,256]{2,0,1:T(8,128)(2,1)S(1)}, u32[]{:S(2)}, u32[]{:S(2)}) collective-permute-start(bf16[192,1,256]{2,0,1:T(8,128)(2,1)S(1)} %copy.39), channel_id=1, source_target_pairs={{0,1},{1,2},{2,3},{3,4},{4,5},{5,6},{6,7},{7,8},{8,9},{9,10},{10,1... | collective-permute-start | bytes 294920 | tf_op jit(solution)/shard_map/ppermute | solution.py:23
  17.2 7.8 %collective-permute-done.1 = bf16[192,1,256]{2,0,1:T(8,128)(2,1)S(1)} collective-permute-done((bf16[192,1,256]{2,0,1:T(8,128)(2,1)S(1)}, bf16[192,1,256]{2,0,1:T(8,128)(2,1)S(1)}, u32[]{:S(2)}, u32[]{:S(2)}) %collective-permute-start.1) | collective-permute-done | bytes 98336 | tf_op jit(solution)/shard_map/ppermute | solution.py:24
  25.2 0.2 copy.24
  25.4 3.4 %maximum_bitcast_fusion = bf16[192,10,1,256]{3,1,0,2:T(8,128)(2,1)} fusion(bf16[192,1,256]{2,1,0:T(2,128)(2,1)S(1)} %copy.25, bf16[192,8,256]{2,1,0:T(8,128)(2,1)} %param.7, bf16[192,1,256]{2,1,0:T(2,128)(2,1)S(1)} %copy.24), kind=kLoop, calls=%fused_computation.11 | loop fusion | flops 2949120 | bytes 1966080 | tf_op jit(solution)/shard_map/broadcast_in_dim | solution.py:44
  28.8 2.9 %copy.43 = bf16[192,10,1,256]{0,3,1,2:T(8,128)(2,1)} copy(bf16[192,10,1,256]{3,1,0,2:T(8,128)(2,1)} %maximum_bitcast_fusion) | data formatting | bytes 1966080
  31.7 2.8 %pad.5.clone = bf16[192,10,1,264]{0,3,1,2:T(8,128)(2,1)} pad(bf16[192,10,1,256]{0,3,1,2:T(8,128)(2,1)} %copy.43, bf16[]{:T(256)} %constant.16.clone.1), padding=0_0x0_0x0_0x1_7 | pad | bytes 1996802 | tf_op jit(solution)/shard_map/broadcast_in_dim | solution.py:44
  34.4 3.4 %reshape.24 = bf16[192,10,1,8,33]{0,4,3,1,2:T(8,128)(2,1)} reshape(bf16[192,10,1,264]{0,3,1,2:T(8,128)(2,1)} %pad.5.clone) | data formatting | bytes 2027520 | tf_op jit(solution)/shard_map/conv_general_dilated | solution.py:43
  37.8 1.8 %copy.28 = bf16[192,10,1,8,33]{0,3,4,1,2:T(8,128)(2,1)S(1)} copy(bf16[192,10,1,8,33]{0,4,3,1,2:T(8,128)(2,1)} %reshape.24) | data formatting | bytes 2027520 | tf_op jit(solution)/shard_map/conv_general_dilated | solution.py:43
  39.7 3.0 %convolution_select_fusion = f32[8,8,33,192]{3,1,2,0:T(8,128)S(1)} fusion(bf16[192,10,1,7,2]{0,3,4,1,2:T(8,128)(2,1)S(1)} %slice.30, bf16[192,10,1,8,33]{0,3,4,1,2:T(8,128)(2,1)S(1)} %copy.28, pred[8,33]{0,1:T(8,128)(4,1)S(1)} %copy-done.7, bf16[3,3,384,192]{2,3,1,0:T(8,128)(2,1)S(1)} %copy-done.3), kind=kOutput, calls=%fused_computation.13 | convolution fusion | flops 1405052928 | bytes 3945472 | tf_op jit(solution)/shard_map/conv_general_dilated | solution.py:43
  42.7 2.0 %copy.30 = f32[8,8,33,192]{3,0,2,1:T(8,128)} copy(f32[8,8,33,192]{3,1,2,0:T(8,128)S(1)} %convolution_select_fusion) | data formatting | bytes 3244032 | tf_op jit(solution)/shard_map/conv_general_dilated | solution.py:43
  44.8 0.3 copy.44
  45.2 1.0 %pad.7.clone = bf16[384,6,1,136]{0,3,1,2:T(8,128)(2,1)} pad(bf16[384,6,1,128]{0,3,1,2:T(8,128)(2,1)S(1)} %copy.44, bf16[]{:T(256)} %constant.16.clone.1), padding=0_0x0_0x0_0x1_7 | pad | bytes 1216514 | tf_op jit(solution)/shard_map/broadcast_in_dim;reshape | solution.py:31
  46.1 1.5 %reshape.29 = bf16[384,6,1,8,17]{0,4,3,1,2:T(8,128)(2,1)S(1)} reshape(bf16[384,6,1,136]{0,3,1,2:T(8,128)(2,1)} %pad.7.clone) | data formatting | bytes 1253376 | tf_op jit(solution)/shard_map/conv_general_dilated | solution.py:30
  47.8 3.2 %fusion.17 = bf16[10,1,8,34,192]{4,2,3,0,1:T(8,128)(2,1)S(1)} fusion(bf16[4,4,384,192]{2,3,1,0:T(8,128)(2,1)S(1)} %copy-done, f32[192]{0:T(256)S(1)} %copy-done.5, pred[10]{0:T(512)(128)(4,1)S(1)} %and_or_fusion, pred[8,34]{0,1:T(8,128)(4,1)S(1)} %copy-done.6, bf16[384,6,1,7,2]{0,3,4,1,2:T(8,128)(2,1)S(1)} %slice.34, bf16[384,6,1,8,17]{0,3,4,1,2:T(8,128)(2,1)S(1)} %copy.35), kind=kOutput, calls=%fused_computation.23 | convolution fusion | flops 1609033728 | bytes 4096026 | tf_op jit(solution)/shard_map/conv_general_dilated | solution.py:30
  51.0 3.1 %fusion.8 = f32[8,8,34,192]{3,1,2,0:T(8,128)S(1)} fusion(bf16[10,1,7,1,192]{4,2,3,0,1:T(8,128)(2,1)S(1)} %get-tuple-element.6, bf16[10,1,7,1,192]{4,2,3,0,1:T(8,128)(2,1)S(1)} %get-tuple-element.5, bf16[10,1,8,34,192]{4,2,3,0,1:T(8,128)(2,1)S(1)} %fusion.17, bf16[3,3,384,192]{2,3,1,0:T(8,128)(2,1)S(1)} %copy-done.4), kind=kOutput, calls=%fused_computation.16 | convolution fusion | flops 1449418752 | bytes 4030464 | tf_op jit(solution)/shard_map/conv_general_dilated | solution.py:43
  54.1 1.3 %copy.37 = f32[8,8,34,192]{3,0,2,1:T(8,128)S(1)} copy(f32[8,8,34,192]{3,1,2,0:T(8,128)S(1)} %fusion.8) | data formatting | bytes 3342336 | tf_op jit(solution)/shard_map/conv_general_dilated | solution.py:43
  55.4 0.3 copy-done.1
  55.7 0.8 %multiply_convert_fusion = bf16[192,8,256]{0,1,2:T(8,128)(2,1)S(1)} fusion(f32[8,1,272,192]{3,0,2,1:T(8,128)S(1)} %bitcast.36, f32[8,1,264,192]{3,0,2,1:T(8,128)S(1)} %bitcast.37, f32[192]{0:T(256)S(1)} %copy-done.2), kind=kLoop, calls=%fused_computation.10 | loop fusion | flops 2752512 | bytes 3932928 | tf_op jit(solution)/shard_map/convert_element_type | solution.py:66
  56.5 1.9 %copy.38 = bf16[192,8,256]{2,1,0:T(8,128)(2,1)} copy(bf16[192,8,256]{0,1,2:T(8,128)(2,1)S(1)} %multiply_convert_fusion) | data formatting | bytes 1572864 | tf_op jit(solution)/shard_map/convert_element_type | solution.py:66
  (29 shorter events, 0.5 us)
Async XLA Ops:
  0.0 47.8 %copy-start = (bf16[4,4,384,192]{2,3,1,0:T(8,128)(2,1)S(1)}, bf16[4,4,384,192]{2,3,1,0:T(8,128)(2,1)}, u32[]{:S(2)}) copy-start(bf16[4,4,384,192]{2,3,1,0:T(8,128)(2,1)} %param.8) | copy-start | bytes 7077892
  2.4 42.3 %all-to-all-start = ((bf16[16,24,6,128]{3,1,2,0:T(8,128)(2,1)}), bf16[16,24,6,128]{3,1,2,0:T(8,128)(2,1)S(1)}, u32[]{:S(2)}, u32[]{:S(2)}) async-start(bf16[16,24,6,128]{3,1,2,0:T(8,128)(2,1)} %maximum_bitcast_fusion.1), calls=%async_computation | async-start | bytes 1179648 | tf_op jit(solution)/shard_map/all_to_all | solution.py:16
  10.7 14.4 %collective-permute-start.1 = (bf16[192,1,256]{2,0,1:T(8,128)(2,1)S(1)}, bf16[192,1,256]{2,0,1:T(8,128)(2,1)S(1)}, u32[]{:S(2)}, u32[]{:S(2)}) collective-permute-start(bf16[192,1,256]{2,0,1:T(8,128)(2,1)S(1)} %copy.40), channel_id=1, source_target_pairs={{1,0},{2,1},{3,2},{4,3},{5,4},{6,5},{7,6},{8,7},{9,8},{10,9},{11,1... | collective-permute-start | bytes 294920 | tf_op jit(solution)/shard_map/ppermute | solution.py:24
  13.0 12.2 %collective-permute-start = (bf16[192,1,256]{2,0,1:T(8,128)(2,1)S(1)}, bf16[192,1,256]{2,0,1:T(8,128)(2,1)S(1)}, u32[]{:S(2)}, u32[]{:S(2)}) collective-permute-start(bf16[192,1,256]{2,0,1:T(8,128)(2,1)S(1)} %copy.39), channel_id=1, source_target_pairs={{0,1},{1,2},{2,3},{3,4},{4,5},{5,6},{6,7},{7,8},{8,9},{9,10},{10,1... | collective-permute-start | bytes 294920 | tf_op jit(solution)/shard_map/ppermute | solution.py:23
  37.8 1.9 %copy-start.3 = (bf16[3,3,384,192]{2,3,1,0:T(8,128)(2,1)S(1)}, bf16[3,3,384,192]{2,3,1,0:T(8,128)(2,1)}, u32[]{:S(2)}) copy-start(bf16[3,3,384,192]{2,3,1,0:T(8,128)(2,1)} %param.10) | copy-start | bytes 3981316
  37.8 1.9 %copy-start.7 = (pred[8,33]{0,1:T(8,128)(4,1)S(1)}, pred[8,33]{0,1:T(8,128)(4,1)}, u32[]{:S(2)}) copy-start(pred[8,33]{0,1:T(8,128)(4,1)} %constant.33) | copy-start | bytes 796
  45.1 2.6 %copy-start.5 = (f32[192]{0:T(256)S(1)}, f32[192]{0:T(256)}, u32[]{:S(2)}) copy-start(f32[192]{0:T(256)} %param.9) | copy-start | bytes 2308
  45.1 2.6 %copy-start.6 = (pred[8,34]{0,1:T(8,128)(4,1)S(1)}, pred[8,34]{0,1:T(8,128)(4,1)}, u32[]{:S(2)}) copy-start(pred[8,34]{0,1:T(8,128)(4,1)} %constant.34) | copy-start | bytes 820
  47.8 3.2 %copy-start.4 = (bf16[3,3,384,192]{2,3,1,0:T(8,128)(2,1)S(1)}, bf16[3,3,384,192]{2,3,1,0:T(8,128)(2,1)}, u32[]{:S(2)}) copy-start(bf16[3,3,384,192]{2,3,1,0:T(8,128)(2,1)} %param.10) | copy-start | bytes 3981316
  54.1 1.6 %copy-start.1 = (f32[8,8,33,192]{3,0,2,1:T(8,128)S(1)}, f32[8,8,33,192]{3,0,2,1:T(8,128)}, u32[]{:S(2)}) copy-start(f32[8,8,33,192]{3,0,2,1:T(8,128)} %copy.30) | copy-start | bytes 4866052
  54.1 1.6 %copy-start.2 = (f32[192]{0:T(256)S(1)}, f32[192]{0:T(256)}, u32[]{:S(2)}) copy-start(f32[192]{0:T(256)} %param.11) | copy-start | bytes 2308

commit v2 on v1

v2 whole, which is shorter than its diff:
```python
import jax
import jax.numpy as jnp
from jax import lax
from jax.experimental import pallas as pl
from jax.experimental.pallas import tpu as pltpu
from jax.sharding import PartitionSpec as P


def coarse_windows(coarse, peers):
    groups, rows, cols = coarse.shape
    tile = rows // peers
    padded = jnp.pad(coarse, ((0, 0), (1, tile - 1), (0, 0)))
    blocks = padded.reshape(groups, peers + 1, tile, cols)
    windows = jnp.concatenate([blocks[:, :peers], blocks[:, 1:, :2]], axis=2)
    windows = jnp.transpose(windows, (1, 2, 0, 3))
    gathered = lax.all_to_all(windows, "row", 0, 2, tiled=True)
    return gathered.reshape(tile + 2, peers * groups, cols)


def skip_rows(skip, peers):
    up = [(i, i + 1) for i in range(peers - 1)]
    down = [(j, i) for i, j in up]
    before = lax.ppermute(skip[:, -1:], "row", up)
    after = lax.ppermute(skip[:, :1], "row", down)
    rimmed = jnp.concatenate([before, skip, after], axis=1)
    return jnp.transpose(rimmed, (1, 0, 2))


def lane_shift(v, period, step):
    lane = lax.broadcasted_iota(jnp.int32, v.shape, 1) % period
    edge = 0 if step > 0 else period - 1
    return jnp.where(lane == edge, 0.0, pltpu.roll(v, step % v.shape[1], 1))


def decoder_kernel(flags, xw_ref, sk_ref, wu_ref, bu_ref, w3_ref, b3_ref, out_ref):
    nwin, cin, cw = xw_ref.shape
    nfine, cout, fw = sk_ref.shape
    nout = nfine - 2
    span = (nwin - 1) * cw
    f32 = jnp.float32

    def dot(a, b):
        return jnp.dot(a, b, preferred_element_type=f32)

    wide = jnp.concatenate([xw_ref[i] for i in range(nwin)], axis=1)
    later, earlier = wide[:, cw:], wide[:, :span]
    parity = []
    for first, second in ((0, 2), (1, 3)):
        z = dot(wu_ref[first], later) + dot(wu_ref[second], earlier)
        taps = [z[k * cout : (k + 1) * cout] for k in range(4)]
        even = taps[1] + lane_shift(taps[3], cw, 1) + bu_ref[...]
        odd = taps[2] + lane_shift(taps[0], cw, -1) + bu_ref[...]
        parity.append((even.astype(jnp.bfloat16), odd.astype(jnp.bfloat16)))

    col = lax.broadcasted_iota(jnp.int32, (cw, fw), 0)
    pos = lax.broadcasted_iota(jnp.int32, (cw, fw), 1)
    put_even = (pos == 2 * col).astype(jnp.bfloat16)
    put_odd = (pos == 2 * col + 1).astype(jnp.bfloat16)

    joined = []
    for t in range(nfine):
        even, odd = parity[t % 2]
        q = t // 2
        row = dot(even[:, q * cw : (q + 1) * cw], put_even) + dot(odd[:, q * cw : (q + 1) * cw], put_odd)
        if t == 0:
            row = jnp.where(flags[0] == 1, 0.0, row)
        if t == nfine - 1:
            row = jnp.where(flags[1] == 1, 0.0, row)
        joined.append(jnp.concatenate([sk_ref[t], row.astype(jnp.bfloat16)], axis=0))
    field = jnp.concatenate(joined, axis=1)

    total = None
    for ky in range(3):
        part = dot(w3_ref[ky], field[:, ky * fw : (ky + nout) * fw])
        total = part if total is None else total + part
    pre = total[cout : 2 * cout]
    pre = pre + lane_shift(total[:cout], fw, 1) + lane_shift(total[2 * cout :], fw, -1)
    pre = pre + b3_ref[...]
    act = (pre / (1.0 + jnp.exp(-pre))).astype(out_ref.dtype)
    for y in range(nout):
        out_ref[y] = act[:, y * fw : (y + 1) * fw]


def decode(flags, xw, sk, wu, bu, w3, b3):
    nfine, cout, fw = sk.shape
    vmem = pl.BlockSpec(memory_space=pltpu.VMEM)
    return pl.pallas_call(
        decoder_kernel,
        out_shape=jax.ShapeDtypeStruct((nfine - 2, cout, fw), jnp.bfloat16),
        in_specs=[pl.BlockSpec(memory_space=pltpu.SMEM)] + [vmem] * 6,
        out_specs=vmem,
        compiler_params=pltpu.CompilerParams(vmem_limit_bytes=48 * 1024 * 1024),
    )(flags, xw, sk, wu, bu, w3, b3)


def shards(coarse, skip_field, up_weight, up_bias, conv_weight, conv_bias):
    peers = lax.axis_size("row")
    me = lax.axis_index("row")
    flags = jnp.stack([me == 0, me == peers - 1]).astype(jnp.int32)
    sk = skip_rows(skip_field, peers)
    xw = coarse_windows(coarse, peers)
    cout = up_weight.shape[3]
    wu = jnp.transpose(up_weight, (0, 1, 3, 2)).reshape(4, 4 * cout, -1)
    w3 = jnp.transpose(conv_weight, (0, 1, 3, 2)).reshape(3, 3 * cout, -1)
    out = decode(flags, xw, sk, wu, up_bias[:, None], w3, conv_bias[:, None])
    return jnp.transpose(out, (1, 0, 2))


def solution(mesh):
    in_specs = (P("row", "member", None), P(None, ("member", "row"), None), P(), P(), P(), P())
    out_specs = P(None, ("member", "row"), None)
    return jax.shard_map(shards, mesh=mesh, in_specs=in_specs, out_specs=out_specs, check_vma=False)
```

time: 59 us -> 37 us (0.63)
  local copies, waits for them, and re-layouts: 22.9 us -> 4.23 us
  matrix products: 9.26 us -> 0 us
  Pallas kernels: 0 us -> 8.82 us
  other arithmetic: 5.11 us -> 1.07 us
  waiting for transfers between devices: 7.84 us -> 10.1 us
  starting transfers between devices: 13 us -> 11.9 us
    conv_general_dilated x8 -> x0, local copies, waits for them, and re-layouts: 10.2 us -> none  [the longest x5 8.55 us: conv3(): lax.conv_general_dilated(field[None], weight, window_strides=(1, 1), padd...]
    conv_general_dilated x3 -> x0, matrix products: 9.26 us -> none  [the longest x2 6.09 us: conv3(): lax.conv_general_dilated(field[None], weight, window_strides=(1, 1), padd...]
    pallas_call x0 -> x1, Pallas kernels: none -> 8.82 us  [decode(): pl.pallas_call(decoder_kernel, out_shape=jax.ShapeDtypeStruct((nfine - 2,...]
    unnamed x21 -> x10, local copies, waits for them, and re-layouts: 4.96 us -> 1.43 us
    broadcast_in_dim x1 -> x0, other arithmetic: 3.42 us -> none  [conv3(): field[None]]
    broadcast_in_dim x1 -> x2, local copies, waits for them, and re-layouts: 2.77 us -> 0.23 us  [shards(): out = decode(flags, xw, sk, wu, up_bias[:, None], w3, conv_bias[:, None])]
    ppermute x2, waiting for transfers between devices: 7.84 us -> 10.1 us  [the longest x1 8.44 us: skip_rows(): before = lax.ppermute(skip[:, -1:], 'row', up)]
    convert_element_type x2 -> x0, local copies, waits for them, and re-layouts: 1.9 us -> none  [the longest x1 1.89 us: shards(): return jax.nn.silu(pre).astype(jnp.bfloat16)]
  transfers between devices with their start and end apart: 3 -> 3, of which waited for: 1 -> 2; matrix products, arithmetic and copies ran while one was open for 37% -> 2% of each run, Pallas kernels for 0% -> 0%
where the time goes in v2:
time: 37 us; the launch traced here: 36.3 us
  starting transfers between devices  11.9 us (32%)
  waiting for transfers between devices  10.1 us (27%)
  Pallas kernels  8.82 us (24%)
  local copies, waits for them, and re-layouts  4.23 us (11%)
  other arithmetic  1.07 us (3%)
    pallas_call x1, Pallas kernels, decode(): pl.pallas_call(decoder_kernel, out_shape=jax.ShapeDtypeStruct((nfine - 2,...  8.82 us
    ppermute x1, waiting for transfers between devices, skip_rows(): before = lax.ppermute(skip[:, -1:], 'row', up)  8.44 us
    all_to_all x1, starting transfers between devices, coarse_windows(): gathered = lax.all_to_all(windows, 'row', 0, 2, tiled=True)  6.55 us
    ppermute x1, starting transfers between devices, skip_rows(): before = lax.ppermute(skip[:, -1:], 'row', up)  3.47 us
    ppermute x1, starting transfers between devices, skip_rows(): after = lax.ppermute(skip[:, :1], 'row', down)  1.92 us
    ppermute x1, waiting for transfers between devices, skip_rows(): after = lax.ppermute(skip[:, :1], 'row', down)  1.67 us
    unnamed x10, local copies, waits for them, and re-layouts  1.43 us
    transpose x1, local copies, waits for them, and re-layouts, shards(): return jnp.transpose(out, (1, 0, 2))  1.32 us
  transfers between devices with their start and end apart: 3, of which 2 were waited for; matrix products, arithmetic and copies ran while one was open for 2% of the time, Pallas kernels for 0%

profile of v2, /device:TPU:13, one launch (start us, length us, event | category | flops | bytes accessed | tf_op | source)
XLA Modules:
  0.0 36.3 jit_solution(17587544224704796499)
XLA Ops:
  0.0 1.3 %copy.13 = bf16[24,64,128]{2,0,1:T(8,128)(2,1)S(1)} copy(bf16[24,64,128]{2,1,0:T(8,128)(2,1)} %param.6) | data formatting | bytes 786432 | tf_op args[0]
  1.3 0.0 copy-start.1
  1.4 0.0 copy-start.2
  1.4 0.0 copy-start.3
  1.4 0.9 %maximum_bitcast_fusion.1 = bf16[16,6,24,128]{3,2,1,0:T(8,128)(2,1)} fusion(bf16[24,16,2,128]{3,0,2,1:T(8,128)(2,1)S(1)} %slice.17, bf16[24,16,4,128]{3,0,2,1:T(8,128)(2,1)S(1)} %slice.16), kind=kLoop, calls=%fused_computation.1 | loop fusion | flops 294912 | bytes 1179648 | tf_op jit(solution)/shard_map/transpose | solution.py:15
  2.3 6.6 %all-to-all-start = ((bf16[16,6,24,128]{3,2,1,0:T(8,128)(2,1)}), bf16[16,6,24,128]{3,2,1,0:T(8,128)(2,1)}, u32[]{:S(2)}, u32[]{:S(2)}) async-start(bf16[16,6,24,128]{3,2,1,0:T(8,128)(2,1)} %maximum_bitcast_fusion.1), calls=%async_computation | async-start | bytes 1179648 | tf_op jit(solution)/shard_map/all_to_all | solution.py:16
  8.8 0.0 copy-done.1
  8.8 0.0 copy-start
  8.9 0.2 copy.15
  9.0 3.5 %collective-permute-start = (bf16[192,1,256]{2,0,1:T(8,128)(2,1)S(1)}, bf16[192,1,256]{2,0,1:T(8,128)(2,1)S(1)}, u32[]{:S(2)}, u32[]{:S(2)}) collective-permute-start(bf16[192,1,256]{2,0,1:T(8,128)(2,1)S(1)} %get-tuple-element.5), channel_id=1, source_target_pairs={{0,1},{1,2},{2,3},{3,4},{4,5},{5,6},{6,7},{7,8},{8,9},{9,10},{10,1... | collective-permute-start | bytes 294920 | tf_op jit(solution)/shard_map/ppermute | solution.py:23
  12.5 1.9 %collective-permute-start.1 = (bf16[192,1,256]{2,0,1:T(8,128)(2,1)S(1)}, bf16[192,1,256]{2,0,1:T(8,128)(2,1)S(1)}, u32[]{:S(2)}, u32[]{:S(2)}) collective-permute-start(bf16[192,1,256]{2,0,1:T(8,128)(2,1)S(1)} %get-tuple-element.6), channel_id=1, source_target_pairs={{1,0},{2,1},{3,2},{4,3},{5,4},{6,5},{7,6},{8,7},{9,8},{10,9},{11,1... | collective-permute-start | bytes 294920 | tf_op jit(solution)/shard_map/ppermute | solution.py:24
  14.5 0.0 copy-done.2
  14.5 0.1 copy.18.bu_ref
  14.6 0.0 copy-done.3
  14.6 0.1 copy.19.b3_ref
  14.7 0.1 add_convert_fusion.flags
  14.8 8.4 %collective-permute-done = bf16[192,1,256]{2,0,1:T(8,128)(2,1)S(1)} collective-permute-done((bf16[192,1,256]{2,0,1:T(8,128)(2,1)S(1)}, bf16[192,1,256]{2,0,1:T(8,128)(2,1)S(1)}, u32[]{:S(2)}, u32[]{:S(2)}) %collective-permute-start) | collective-permute-done | bytes 98336 | tf_op jit(solution)/shard_map/ppermute | solution.py:23
  23.2 1.7 %collective-permute-done.1 = bf16[192,1,256]{2,0,1:T(8,128)(2,1)S(1)} collective-permute-done((bf16[192,1,256]{2,0,1:T(8,128)(2,1)S(1)}, bf16[192,1,256]{2,0,1:T(8,128)(2,1)S(1)}, u32[]{:S(2)}, u32[]{:S(2)}) %collective-permute-start.1) | collective-permute-done | bytes 98336 | tf_op jit(solution)/shard_map/ppermute | solution.py:24
  24.9 0.1 maximum_bitcast_fusion.sk_ref
  25.0 0.0 all-to-all-done
  25.1 1.1 %copy.14 = bf16[1,6,16,24,128]{4,3,2,1,0:T(8,128)(2,1)S(1)} copy(bf16[1,6,16,24,128]{4,3,1,2,0:T(8,128)(2,1)} %bitcast.5) | data formatting | bytes 1179648 | tf_op jit(solution)/shard_map/all_to_all | solution.py:16
  26.2 0.0 copy-done
  26.2 8.8 %shard_map.64 = bf16[8,192,256]{2,1,0:T(8,128)(2,1)S(1)} custom-call(s32[2]{0:T(128)S(1)} %add_convert_fusion.flags, bf16[6,384,128]{2,1,0:T(8,128)(2,1)S(1)} %bitcast.21, bf16[10,192,256]{2,1,0:T(8,128)(2,1)S(1)} %maximum_bitcast_fusion.sk_ref, bf16[4,768,384]{2,1,0:T(8,128)(2,1)} %bitcast.25, f32[192,1]{1,0:T(8,128)S(1)} %copy.18.bu_ref, ...), custom_call_target="tpu_custom_call" | custom-call | tf_op jit(solution)/shard_map/pallas_call | solution.py:87
  35.0 1.3 %copy.20 = bf16[192,8,256]{2,1,0:T(8,128)(2,1)} copy(bf16[192,8,256]{2,0,1:T(8,128)(2,1)S(1)} %bitcast.20) | data formatting | bytes 1572864 | tf_op jit(solution)/shard_map/transpose | solution.py:106
  (4 shorter events, 0.1 us)
Async XLA Ops:
  1.3 7.6 %copy-start.1 = (bf16[192,8,256]{2,1,0:T(8,128)(2,1)S(1)}, bf16[192,8,256]{2,1,0:T(8,128)(2,1)}, u32[]{:S(2)}) copy-start(bf16[192,8,256]{2,1,0:T(8,128)(2,1)} %param.7) | copy-start | bytes 2359300
  1.4 13.1 %copy-start.2 = (f32[192]{0:T(256)S(1)}, f32[192]{0:T(256)}, u32[]{:S(2)}) copy-start(f32[192]{0:T(256)} %param.9) | copy-start | bytes 2308
  1.4 13.2 %copy-start.3 = (f32[192]{0:T(256)S(1)}, f32[192]{0:T(256)}, u32[]{:S(2)}) copy-start(f32[192]{0:T(256)} %param.11) | copy-start | bytes 2308
  2.3 22.8 %all-to-all-start = ((bf16[16,6,24,128]{3,2,1,0:T(8,128)(2,1)}), bf16[16,6,24,128]{3,2,1,0:T(8,128)(2,1)}, u32[]{:S(2)}, u32[]{:S(2)}) async-start(bf16[16,6,24,128]{3,2,1,0:T(8,128)(2,1)} %maximum_bitcast_fusion.1), calls=%async_computation | async-start | bytes 1179648 | tf_op jit(solution)/shard_map/all_to_all | solution.py:16
  8.8 17.3 %copy-start = (bf16[3,3,384,192]{2,3,1,0:T(8,128)(2,1)S(1)}, bf16[3,3,384,192]{2,3,1,0:T(8,128)(2,1)}, u32[]{:S(2)}) copy-start(bf16[3,3,384,192]{2,3,1,0:T(8,128)(2,1)} %param.10) | copy-start | bytes 3981316
  9.0 14.2 %collective-permute-start = (bf16[192,1,256]{2,0,1:T(8,128)(2,1)S(1)}, bf16[192,1,256]{2,0,1:T(8,128)(2,1)S(1)}, u32[]{:S(2)}, u32[]{:S(2)}) collective-permute-start(bf16[192,1,256]{2,0,1:T(8,128)(2,1)S(1)} %get-tuple-element.5), channel_id=1, source_target_pairs={{0,1},{1,2},{2,3},{3,4},{4,5},{5,6},{6,7},{7,8},{8,9},{9,10},{10,1... | collective-permute-start | bytes 294920 | tf_op jit(solution)/shard_map/ppermute | solution.py:23
  12.5 12.4 %collective-permute-start.1 = (bf16[192,1,256]{2,0,1:T(8,128)(2,1)S(1)}, bf16[192,1,256]{2,0,1:T(8,128)(2,1)S(1)}, u32[]{:S(2)}, u32[]{:S(2)}) collective-permute-start(bf16[192,1,256]{2,0,1:T(8,128)(2,1)S(1)} %get-tuple-element.6), channel_id=1, source_target_pairs={{1,0},{2,1},{3,2},{4,3},{5,4},{6,5},{7,6},{8,7},{9,8},{10,9},{11,1... | collective-permute-start | bytes 294920 | tf_op jit(solution)/shard_map/ppermute | solution.py:24

commit v3 on v2

--- a/solution.py
+++ b/solution.py
@@ -32,10 +32,26 @@
     return jnp.where(lane == edge, 0.0, pltpu.roll(v, step % v.shape[1], 1))
 
 
-def decoder_kernel(flags, xw_ref, sk_ref, wu_ref, bu_ref, w3_ref, b3_ref, out_ref):
+def conv_rows(field, w_ref, nout, fw):
+    total = None
+    for ky in range(3):
+        part = jnp.dot(w_ref[ky], field[:, ky * fw : (ky + nout) * fw], preferred_element_type=jnp.float32)
+        total = part if total is None else total + part
+    cout = total.shape[0] // 3
+    mid = total[cout : 2 * cout]
+    return mid + lane_shift(total[:cout], fw, 1) + lane_shift(total[2 * cout :], fw, -1)
+
+
+def skip_kernel(sk_ref, w_ref, b_ref, out_ref):
+    nfine, _, fw = sk_ref.shape
+    field = jnp.concatenate([sk_ref[t] for t in range(nfine)], axis=1)
+    out_ref[...] = conv_rows(field, w_ref, nfine - 2, fw) + b_ref[...]
+
+
+def decoder_kernel(flags, xw_ref, wu_ref, bu_ref, w3_ref, part_ref, out_ref):
     nwin, cin, cw = xw_ref.shape
-    nfine, cout, fw = sk_ref.shape
-    nout = nfine - 2
+    cout, nout, fw = out_ref.shape
+    nfine = nout + 2
     span = (nwin - 1) * cw
     f32 = jnp.float32
 
@@ -57,7 +73,7 @@
     put_even = (pos == 2 * col).astype(jnp.bfloat16)
     put_odd = (pos == 2 * col + 1).astype(jnp.bfloat16)
 
-    joined = []
+    rows = []
     for t in range(nfine):
         even, odd = parity[t % 2]
         q = t // 2
@@ -66,31 +82,40 @@
             row = jnp.where(flags[0] == 1, 0.0, row)
         if t == nfine - 1:
             row = jnp.where(flags[1] == 1, 0.0, row)
-        joined.append(jnp.concatenate([sk_ref[t], row.astype(jnp.bfloat16)], axis=0))
-    field = jnp.concatenate(joined, axis=1)
+        rows.append(row.astype(jnp.bfloat16))
+    field = jnp.concatenate(rows, axis=1)
 
-    total = None
-    for ky in range(3):
-        part = dot(w3_ref[ky], field[:, ky * fw : (ky + nout) * fw])
-        total = part if total is None else total + part
-    pre = total[cout : 2 * cout]
-    pre = pre + lane_shift(total[:cout], fw, 1) + lane_shift(total[2 * cout :], fw, -1)
-    pre = pre + b3_ref[...]
+    pre = conv_rows(field, w3_ref, nout, fw) + part_ref[...]
     act = (pre / (1.0 + jnp.exp(-pre))).astype(out_ref.dtype)
     for y in range(nout):
-        out_ref[y] = act[:, y * fw : (y + 1) * fw]
+        out_ref[:, y, :] = act[:, y * fw : (y + 1) * fw]
 
 
-def decode(flags, xw, sk, wu, bu, w3, b3):
+def skip_conv(sk, w3s, b3):
     nfine, cout, fw = sk.shape
+    nout = nfine - 2
+    vmem = pl.BlockSpec(memory_space=pltpu.VMEM)
+    flops = 2 * 3 * w3s.shape[1] * w3s.shape[2] * nout * fw
+    return pl.pallas_call(
+        skip_kernel,
+        out_shape=jax.ShapeDtypeStruct((cout, nout * fw), jnp.float32),
+        in_specs=[vmem] * 3,
+        out_specs=vmem,
+        compiler_params=pltpu.CompilerParams(vmem_limit_bytes=48 * 1024 * 1024),
+        cost_estimate=pl.CostEstimate(flops=flops, transcendentals=0, bytes_accessed=sk.size * 2 + w3s.size * 2 + cout * nout * fw * 4),
+    )(sk, w3s, b3)
+
+
+def decode(flags, xw, wu, bu, w3u, part, nout, fw):
+    cout = bu.shape[0]
     vmem = pl.BlockSpec(memory_space=pltpu.VMEM)
     return pl.pallas_call(
         decoder_kernel,
-        out_shape=jax.ShapeDtypeStruct((nfine - 2, cout, fw), jnp.bfloat16),
-        in_specs=[pl.BlockSpec(memory_space=pltpu.SMEM)] + [vmem] * 6,
+        out_shape=jax.ShapeDtypeStruct((cout, nout, fw), jnp.bfloat16),
+        in_specs=[pl.BlockSpec(memory_space=pltpu.SMEM)] + [vmem] * 5,
         out_specs=vmem,
         compiler_params=pltpu.CompilerParams(vmem_limit_bytes=48 * 1024 * 1024),
-    )(flags, xw, sk, wu, bu, w3, b3)
+    )(flags, xw, wu, bu, w3u, part)
 
 
 def shards(coarse, skip_field, up_weight, up_bias, conv_weight, conv_bias):
@@ -102,8 +127,10 @@
     cout = up_weight.shape[3]
     wu = jnp.transpose(up_weight, (0, 1, 3, 2)).reshape(4, 4 * cout, -1)
     w3 = jnp.transpose(conv_weight, (0, 1, 3, 2)).reshape(3, 3 * cout, -1)
-    out = decode(flags, xw, sk, wu, up_bias[:, None], w3, conv_bias[:, None])
-    return jnp.transpose(out, (1, 0, 2))
+    skips = skip_field.shape[0]
+    part = skip_conv(sk, w3[:, :, :skips], conv_bias[:, None])
+    nout, fw = skip_field.shape[1], skip_field.shape[2]
+    return decode(flags, xw, wu, up_bias[:, None], w3[:, :, skips:], part, nout, fw)
 
 
 def solution(mesh):

time: 37 us -> 40.5 us (1.095)
  local copies, waits for them, and re-layouts: 4.23 us -> 5.86 us
  Pallas kernels: 8.82 us -> 10.2 us
  other arithmetic: 1.07 us -> 1.96 us
    unnamed x10 -> x16, local copies, waits for them, and re-layouts: 1.43 us -> 3.99 us
    pallas_call x1 -> x2, Pallas kernels: 8.82 us -> 10.2 us  [the longest x1 7.93 us: decode(): pl.pallas_call(decoder_kernel, out_shape=jax.ShapeDtypeStruct((cout, nout...]
    transpose x1 -> x0, local copies, waits for them, and re-layouts: 1.32 us -> none  [shards(): return jnp.transpose(out, (1, 0, 2))]
    transpose x1, other arithmetic: 0.12 us -> 1.02 us  [skip_rows(): return jnp.transpose(rimmed, (1, 0, 2))]
  transfers between devices with their start and end apart: 3 -> 3, of which waited for: 2 -> 2; matrix products, arithmetic and copies ran while one was open for 2% -> 5% of each run, Pallas kernels for 0% -> 6%
where the time goes in v3:
time: 40.5 us; the launch traced here: 40.1 us
  starting transfers between devices  11.9 us (29%)
  Pallas kernels  10.2 us (25%)
  waiting for transfers between devices  9.95 us (25%)
  local copies, waits for them, and re-layouts  5.86 us (14%)
  other arithmetic  1.96 us (5%)
    ppermute x1, waiting for transfers between devices, skip_rows(): before = lax.ppermute(skip[:, -1:], 'row', up)  8.17 us
    pallas_call x1, Pallas kernels, decode(): pl.pallas_call(decoder_kernel, out_shape=jax.ShapeDtypeStruct((cout, nout...  7.93 us
    all_to_all x1, starting transfers between devices, coarse_windows(): gathered = lax.all_to_all(windows, 'row', 0, 2, tiled=True)  6.69 us
    unnamed x16, local copies, waits for them, and re-layouts  3.99 us
    ppermute x1, starting transfers between devices, skip_rows(): before = lax.ppermute(skip[:, -1:], 'row', up)  3.34 us
    pallas_call x1, Pallas kernels, skip_conv(): pl.pallas_call(skip_kernel, out_shape=jax.ShapeDtypeStruct((cout, nout *...  2.31 us
    ppermute x1, starting transfers between devices, skip_rows(): after = lax.ppermute(skip[:, :1], 'row', down)  1.92 us
    ppermute x1, waiting for transfers between devices, skip_rows(): after = lax.ppermute(skip[:, :1], 'row', down)  1.78 us
  transfers between devices with their start and end apart: 3, of which 2 were waited for; matrix products, arithmetic and copies ran while one was open for 5% of the time, Pallas kernels for 6%

profile of v3, /device:TPU:13, one launch (start us, length us, event | category | flops | bytes accessed | tf_op | source)
XLA Modules:
  0.0 40.1 jit_solution(4713871970095109788)
XLA Ops:
  0.0 1.3 %copy.12 = bf16[24,64,128]{2,0,1:T(8,128)(2,1)S(1)} copy(bf16[24,64,128]{2,1,0:T(8,128)(2,1)} %param.6) | data formatting | bytes 786432 | tf_op args[0]
  1.3 0.0 copy-start.4
  1.4 0.9 %maximum_bitcast_fusion.1 = bf16[16,6,24,128]{3,2,1,0:T(8,128)(2,1)} fusion(bf16[24,16,2,128]{3,0,2,1:T(8,128)(2,1)S(1)} %slice.25, bf16[24,16,4,128]{3,0,2,1:T(8,128)(2,1)S(1)} %slice.24), kind=kLoop, calls=%fused_computation.1 | loop fusion | flops 294912 | bytes 1179648 | tf_op jit(solution)/shard_map/transpose | solution.py:15
  2.3 6.7 %all-to-all-start = ((bf16[16,6,24,128]{3,2,1,0:T(8,128)(2,1)}), bf16[16,6,24,128]{3,2,1,0:T(8,128)(2,1)}, u32[]{:S(2)}, u32[]{:S(2)}) async-start(bf16[16,6,24,128]{3,2,1,0:T(8,128)(2,1)} %maximum_bitcast_fusion.1), calls=%async_computation | async-start | bytes 1179648 | tf_op jit(solution)/shard_map/all_to_all | solution.py:16
  9.0 0.0 copy-done.4
  9.0 0.2 copy.14
  9.1 3.3 %collective-permute-start = (bf16[192,1,256]{2,0,1:T(8,128)(2,1)S(1)}, bf16[192,1,256]{2,0,1:T(8,128)(2,1)S(1)}, u32[]{:S(2)}, u32[]{:S(2)}) collective-permute-start(bf16[192,1,256]{2,0,1:T(8,128)(2,1)S(1)} %get-tuple-element.7), channel_id=1, source_target_pairs={{0,1},{1,2},{2,3},{3,4},{4,5},{5,6},{6,7},{7,8},{8,9},{9,10},{10,1... | collective-permute-start | bytes 294920 | tf_op jit(solution)/shard_map/ppermute | solution.py:23
  12.5 1.9 %collective-permute-start.1 = (bf16[192,1,256]{2,0,1:T(8,128)(2,1)S(1)}, bf16[192,1,256]{2,0,1:T(8,128)(2,1)}, u32[]{:S(2)}, u32[]{:S(2)}) collective-permute-start(bf16[192,1,256]{2,0,1:T(8,128)(2,1)S(1)} %get-tuple-element.8), channel_id=1, source_target_pairs={{1,0},{2,1},{3,2},{4,3},{5,4},{6,5},{7,6},{8,7},{9,8},{10,9},{11,1... | collective-permute-start | bytes 294920 | tf_op jit(solution)/shard_map/ppermute | solution.py:24
  14.4 0.0 copy-done.5
  14.4 0.1 copy.17.b_ref
  14.6 0.1 copy.18.bu_ref
  14.7 0.4 fusion
  15.1 0.1 add_convert_fusion.flags
  15.2 8.2 %collective-permute-done = bf16[192,1,256]{2,0,1:T(8,128)(2,1)S(1)} collective-permute-done((bf16[192,1,256]{2,0,1:T(8,128)(2,1)S(1)}, bf16[192,1,256]{2,0,1:T(8,128)(2,1)S(1)}, u32[]{:S(2)}, u32[]{:S(2)}) %collective-permute-start) | collective-permute-done | bytes 98336 | tf_op jit(solution)/shard_map/ppermute | solution.py:23
  23.4 1.8 %collective-permute-done.1 = bf16[192,1,256]{2,0,1:T(8,128)(2,1)} collective-permute-done((bf16[192,1,256]{2,0,1:T(8,128)(2,1)S(1)}, bf16[192,1,256]{2,0,1:T(8,128)(2,1)}, u32[]{:S(2)}, u32[]{:S(2)}) %collective-permute-start.1) | collective-permute-done | bytes 98336 | tf_op jit(solution)/shard_map/ppermute | solution.py:24
  25.1 1.0 %maximum_bitcast_fusion.sk_ref = bf16[10,192,256]{2,1,0:T(8,128)(2,1)S(1)} fusion(bf16[192,1,256]{2,0,1:T(8,128)(2,1)} %collective-permute-done.1, bf16[192,8,256]{2,0,1:T(8,128)(2,1)S(1)} %copy.14, bf16[192,1,256]{2,0,1:T(8,128)(2,1)S(1)} %collective-permute-done), kind=kLoop, calls=%fused_computation | loop fusion | flops 983040 | bytes 1966080 | tf_op jit(solution)/shard_map/transpose | solution.py:26
  26.2 0.0 copy-start
  26.2 2.3 %shard_map.64.part_ref = f32[192,2048]{1,0:T(8,128)S(1)} custom-call(bf16[10,192,256]{2,1,0:T(8,128)(2,1)S(1)} %maximum_bitcast_fusion.sk_ref, bf16[3,576,192]{2,1,0:T(8,128)(2,1)S(1)} %get-tuple-element.5.w_ref, f32[192,1]{1,0:T(8,128)S(1)} %copy.17.b_ref), custom_call_target="tpu_custom_call" | custom-call | flops 1358954496 | bytes 3219456 | tf_op jit(solution)/shard_map/pallas_call | solution.py:99
  28.5 0.0 copy-start.1
  28.5 1.2 %copy-done.1 = f32[192,2048]{1,0:T(8,128)} copy-done((f32[192,2048]{1,0:T(8,128)}, f32[192,2048]{1,0:T(8,128)S(1)}, u32[]{:S(2)}) %copy-start.1) | copy-done | bytes 1572888
  29.7 0.0 all-to-all-done
  29.7 1.1 %copy.13 = bf16[1,6,16,24,128]{4,3,2,1,0:T(8,128)(2,1)S(1)} copy(bf16[1,6,16,24,128]{4,3,1,2,0:T(8,128)(2,1)} %bitcast.5) | data formatting | bytes 1179648 | tf_op jit(solution)/shard_map/all_to_all | solution.py:16
  30.8 1.4 %copy-done.2 = f32[192,2048]{1,0:T(8,128)S(1)} copy-done((f32[192,2048]{1,0:T(8,128)S(1)}, f32[192,2048]{1,0:T(8,128)}, u32[]{:S(2)}) %copy-start.2) | copy-done | bytes 1572888
  32.2 7.9 %shard_map.65 = bf16[192,8,256]{2,1,0:T(8,128)(2,1)} custom-call(s32[2]{0:T(128)S(1)} %add_convert_fusion.flags, bf16[6,384,128]{2,1,0:T(8,128)(2,1)S(1)} %bitcast.19, bf16[4,768,384]{2,1,0:T(8,128)(2,1)S(1)} %bitcast.20, f32[192,1]{1,0:T(8,128)S(1)} %copy.18.bu_ref, bf16[3,576,192]{2,1,0:T(8,128)(2,1)S(1)} %get-tuple-element.6.w3_ref, f32[192,2048]{1,0:T(8,128)S(1)} %copy-done.2), custom_call_target="tpu_custom_call" | custom-call | tf_op jit(solution)/shard_map/pallas_call | solution.py:112
  (11 shorter events, 0.1 us)
Async XLA Ops:
  1.3 7.7 %copy-start.4 = (bf16[192,8,256]{2,1,0:T(8,128)(2,1)S(1)}, bf16[192,8,256]{2,1,0:T(8,128)(2,1)}, u32[]{:S(2)}) copy-start(bf16[192,8,256]{2,1,0:T(8,128)(2,1)} %param.7) | copy-start | bytes 2359300
  2.3 12.2 %copy-start.5 = (f32[192]{0:T(256)S(1)}, f32[192]{0:T(256)}, u32[]{:S(2)}) copy-start(f32[192]{0:T(256)} %param.11) | copy-start | bytes 2308
  2.3 12.3 %copy-start.6 = (f32[192]{0:T(256)S(1)}, f32[192]{0:T(256)}, u32[]{:S(2)}) copy-start(f32[192]{0:T(256)} %param.9) | copy-start | bytes 2308
  2.3 12.4 %copy-start.3 = (bf16[3,3,384,192]{2,3,1,0:T(8,128)(2,1)S(1)}, bf16[3,3,384,192]{2,3,1,0:T(8,128)(2,1)}, u32[]{:S(2)}) copy-start(bf16[3,3,384,192]{2,3,1,0:T(8,128)(2,1)} %param.10) | copy-start | bytes 3981316
  2.3 27.4 %all-to-all-start = ((bf16[16,6,24,128]{3,2,1,0:T(8,128)(2,1)}), bf16[16,6,24,128]{3,2,1,0:T(8,128)(2,1)}, u32[]{:S(2)}, u32[]{:S(2)}) async-start(bf16[16,6,24,128]{3,2,1,0:T(8,128)(2,1)} %maximum_bitcast_fusion.1), calls=%async_computation | async-start | bytes 1179648 | tf_op jit(solution)/shard_map/all_to_all | solution.py:16
  9.1 14.2 %collective-permute-start = (bf16[192,1,256]{2,0,1:T(8,128)(2,1)S(1)}, bf16[192,1,256]{2,0,1:T(8,128)(2,1)S(1)}, u32[]{:S(2)}, u32[]{:S(2)}) collective-permute-start(bf16[192,1,256]{2,0,1:T(8,128)(2,1)S(1)} %get-tuple-element.7), channel_id=1, source_target_pairs={{0,1},{1,2},{2,3},{3,4},{4,5},{5,6},{6,7},{7,8},{8,9},{9,10},{10,1... | collective-permute-start | bytes 294920 | tf_op jit(solution)/shard_map/ppermute | solution.py:23
  12.5 12.6 %collective-permute-start.1 = (bf16[192,1,256]{2,0,1:T(8,128)(2,1)S(1)}, bf16[192,1,256]{2,0,1:T(8,128)(2,1)}, u32[]{:S(2)}, u32[]{:S(2)}) collective-permute-start(bf16[192,1,256]{2,0,1:T(8,128)(2,1)S(1)} %get-tuple-element.8), channel_id=1, source_target_pairs={{1,0},{2,1},{3,2},{4,3},{5,4},{6,5},{7,6},{8,7},{9,8},{10,9},{11,1... | collective-permute-start | bytes 294920 | tf_op jit(solution)/shard_map/ppermute | solution.py:24
  26.2 4.6 %copy-start = (bf16[4,4,384,192]{2,3,1,0:T(8,128)(2,1)S(1)}, bf16[4,4,384,192]{2,3,1,0:T(8,128)(2,1)}, u32[]{:S(2)}) copy-start(bf16[4,4,384,192]{2,3,1,0:T(8,128)(2,1)} %param.8) | copy-start | bytes 7077892
  28.5 1.2 %copy-start.1 = (f32[192,2048]{1,0:T(8,128)}, f32[192,2048]{1,0:T(8,128)S(1)}, u32[]{:S(2)}) copy-start(f32[192,2048]{1,0:T(8,128)S(1)} %shard_map.64.part_ref) | copy-start | bytes 4718596
  30.8 1.4 %copy-start.2 = (f32[192,2048]{1,0:T(8,128)S(1)}, f32[192,2048]{1,0:T(8,128)}, u32[]{:S(2)}) copy-start(f32[192,2048]{1,0:T(8,128)} %copy-done.1) | copy-start | bytes 4718596

commit v4 on v2

--- a/solution.py
+++ b/solution.py
@@ -9,12 +9,13 @@
 def coarse_windows(coarse, peers):
     groups, rows, cols = coarse.shape
     tile = rows // peers
-    padded = jnp.pad(coarse, ((0, 0), (1, tile - 1), (0, 0)))
-    blocks = padded.reshape(groups, peers + 1, tile, cols)
-    windows = jnp.concatenate([blocks[:, :peers], blocks[:, 1:, :2]], axis=2)
-    windows = jnp.transpose(windows, (1, 2, 0, 3))
-    gathered = lax.all_to_all(windows, "row", 0, 2, tiled=True)
-    return gathered.reshape(tile + 2, peers * groups, cols)
+    padded = jnp.pad(coarse, ((0, 0), (1, 1), (0, 0)))
+    windows = jnp.stack([padded[:, r * tile : r * tile + tile + 2] for r in range(peers)])
+    windows = jnp.transpose(windows, (0, 2, 1, 3))
+    gathered = lax.all_to_all(windows, "row", 0, 0, tiled=True)
+    if groups % 8:
+        gathered = jnp.transpose(gathered, (1, 0, 2, 3)).reshape(1, tile + 2, peers * groups, cols)
+    return gathered
 
 
 def skip_rows(skip, peers):
@@ -32,8 +33,8 @@
     return jnp.where(lane == edge, 0.0, pltpu.roll(v, step % v.shape[1], 1))
 
 
-def decoder_kernel(flags, xw_ref, sk_ref, wu_ref, bu_ref, w3_ref, b3_ref, out_ref):
-    nwin, cin, cw = xw_ref.shape
+def decoder_kernel(flags, xw_ref, sk_ref, wu_ref, bu_ref, w3_ref, b3_ref, out_ref, act_ref):
+    peers, nwin, groups, cw = xw_ref.shape
     nfine, cout, fw = sk_ref.shape
     nout = nfine - 2
     span = (nwin - 1) * cw
@@ -42,7 +43,13 @@
     def dot(a, b):
         return jnp.dot(a, b, preferred_element_type=f32)
 
-    wide = jnp.concatenate([xw_ref[i] for i in range(nwin)], axis=1)
+    def window_row(i):
+        if peers == 1:
+            return xw_ref[0, i]
+        pieces = [xw_ref[s, i].astype(f32) for s in range(peers)]
+        return jnp.concatenate(pieces, axis=0).astype(jnp.bfloat16)
+
+    wide = jnp.concatenate([window_row(i) for i in range(nwin)], axis=1)
     later, earlier = wide[:, cw:], wide[:, :span]
     parity = []
     for first, second in ((0, 2), (1, 3)):
@@ -76,9 +83,10 @@
     pre = total[cout : 2 * cout]
     pre = pre + lane_shift(total[:cout], fw, 1) + lane_shift(total[2 * cout :], fw, -1)
     pre = pre + b3_ref[...]
-    act = (pre / (1.0 + jnp.exp(-pre))).astype(out_ref.dtype)
+    act = pre / (1.0 + jnp.exp(-pre))
     for y in range(nout):
-        out_ref[y] = act[:, y * fw : (y + 1) * fw]
+        act_ref[:, y, :] = act[:, y * fw : (y + 1) * fw]
+    out_ref[...] = act_ref[...].astype(out_ref.dtype)
 
 
 def decode(flags, xw, sk, wu, bu, w3, b3):
@@ -86,9 +94,10 @@
     vmem = pl.BlockSpec(memory_space=pltpu.VMEM)
     return pl.pallas_call(
         decoder_kernel,
-        out_shape=jax.ShapeDtypeStruct((nfine - 2, cout, fw), jnp.bfloat16),
+        out_shape=jax.ShapeDtypeStruct((cout, nfine - 2, fw), jnp.bfloat16),
         in_specs=[pl.BlockSpec(memory_space=pltpu.SMEM)] + [vmem] * 6,
         out_specs=vmem,
+        scratch_shapes=[pltpu.VMEM((cout, nfine - 2, fw), jnp.float32)],
         compiler_params=pltpu.CompilerParams(vmem_limit_bytes=48 * 1024 * 1024),
     )(flags, xw, sk, wu, bu, w3, b3)
 
@@ -102,8 +111,7 @@
     cout = up_weight.shape[3]
     wu = jnp.transpose(up_weight, (0, 1, 3, 2)).reshape(4, 4 * cout, -1)
     w3 = jnp.transpose(conv_weight, (0, 1, 3, 2)).reshape(3, 3 * cout, -1)
-    out = decode(flags, xw, sk, wu, up_bias[:, None], w3, conv_bias[:, None])
-    return jnp.transpose(out, (1, 0, 2))
+    return decode(flags, xw, sk, wu, up_bias[:, None], w3, conv_bias[:, None])
 
 
 def solution(mesh):

time: 37 us -> 46.2 us (1.25)
  local copies, waits for them, and re-layouts: 4.23 us -> 14.1 us
  waiting for transfers between devices: 10.1 us -> 9.37 us
    unnamed x10 -> x29, local copies, waits for them, and re-layouts: 1.43 us -> 13.2 us
    transpose x1 -> x0, local copies, waits for them, and re-layouts: 1.32 us -> none  [shards(): return jnp.transpose(out, (1, 0, 2))]
    transpose x1, other arithmetic: 0.12 us -> 1.26 us  [skip_rows(): return jnp.transpose(rimmed, (1, 0, 2))]
    all_to_all x1 -> x0, local copies, waits for them, and re-layouts: 1.12 us -> none  [coarse_windows(): gathered = lax.all_to_all(windows, 'row', 0, 2, tiled=True)]
    transpose x1 -> x0, other arithmetic: 0.87 us -> none  [coarse_windows(): windows = jnp.transpose(windows, (1, 2, 0, 3))]
    ppermute x1, waiting for transfers between devices: 8.44 us -> 7.7 us  [skip_rows(): before = lax.ppermute(skip[:, -1:], 'row', up)]
    another operation x0 -> x1, local copies, waits for them, and re-layouts: none -> 0.62 us  [coarse_windows(): jnp.stack([padded[:, r * tile:r * tile + tile + 2] for r in range(peers)])]
  transfers between devices with their start and end apart: 3 -> 3, of which waited for: 2 -> 2; matrix products, arithmetic and copies ran while one was open for 2% -> 4% of each run, Pallas kernels for 0% -> 0%
where the time goes in v4:
time: 46.2 us; the launch traced here: 45.9 us
  local copies, waits for them, and re-layouts  14.1 us (31%)
  starting transfers between devices  11.8 us (26%)
  waiting for transfers between devices  9.37 us (20%)
  Pallas kernels  9.15 us (20%)
  other arithmetic  1.33 us (3%)
    unnamed x29, local copies, waits for them, and re-layouts  13.2 us
    pallas_call x1, Pallas kernels, decode(): pl.pallas_call(decoder_kernel, out_shape=jax.ShapeDtypeStruct((cout, nfin...  9.15 us
    ppermute x1, waiting for transfers between devices, skip_rows(): before = lax.ppermute(skip[:, -1:], 'row', up)  7.7 us
    all_to_all x1, starting transfers between devices, coarse_windows(): gathered = lax.all_to_all(windows, 'row', 0, 0, tiled=True)  6.55 us
    ppermute x1, starting transfers between devices, skip_rows(): before = lax.ppermute(skip[:, -1:], 'row', up)  3.34 us
    ppermute x1, starting transfers between devices, skip_rows(): after = lax.ppermute(skip[:, :1], 'row', down)  1.92 us
    ppermute x1, waiting for transfers between devices, skip_rows(): after = lax.ppermute(skip[:, :1], 'row', down)  1.67 us
    transpose x1, other arithmetic, skip_rows(): return jnp.transpose(rimmed, (1, 0, 2))  1.26 us
  transfers between devices with their start and end apart: 3, of which 2 were waited for; matrix products, arithmetic and copies ran while one was open for 4% of the time, Pallas kernels for 0%

profile of v4, /device:TPU:13, one launch (start us, length us, event | category | flops | bytes accessed | tf_op | source)
XLA Modules:
  0.0 45.9 jit_solution(12544978563843386682)
XLA Ops:
  0.0 1.3 %copy.25 = bf16[24,64,128]{2,0,1:T(8,128)(2,1)S(1)} copy(bf16[24,64,128]{2,1,0:T(8,128)(2,1)} %param.6) | data formatting | bytes 786432 | tf_op args[0]
  1.3 0.6 %fusion.1 = bf16[16,24,6,128]{3,1,2,0:T(8,128)(2,1)} fusion(bf16[24,64,128]{2,0,1:T(8,128)(2,1)S(1)} %copy.25), kind=kLoop, calls=%fused_computation.4 | loop fusion | bytes 430080
  2.0 0.6 %fusion.17 = bf16[16,24,6,128]{3,1,2,0:T(8,128)(2,1)} fusion(bf16[16,24,6,128]{3,1,2,0:T(8,128)(2,1)} %fusion.1, bf16[24,64,128]{2,0,1:T(8,128)(2,1)S(1)} %copy.25), kind=kLoop, calls=%fused_computation.34 | loop fusion | bytes 73728
  2.6 0.6 %fusion.16 = bf16[16,24,6,128]{3,1,2,0:T(8,128)(2,1)} fusion(bf16[16,24,6,128]{3,1,2,0:T(8,128)(2,1)} %fusion.17, bf16[24,64,128]{2,0,1:T(8,128)(2,1)S(1)} %copy.25), kind=kLoop, calls=%fused_computation.32 | loop fusion | bytes 73728
  3.8 0.6 %fusion.14 = bf16[16,24,6,128]{3,1,2,0:T(8,128)(2,1)} fusion(bf16[16,24,6,128]{3,1,2,0:T(8,128)(2,1)} %fusion.15, bf16[24,64,128]{2,0,1:T(8,128)(2,1)S(1)} %copy.25), kind=kLoop, calls=%fused_computation.28 | loop fusion | bytes 73728
  5.0 0.6 %fusion.12 = bf16[16,24,6,128]{3,1,2,0:T(8,128)(2,1)} fusion(bf16[16,24,6,128]{3,1,2,0:T(8,128)(2,1)} %fusion.13, bf16[24,64,128]{2,0,1:T(8,128)(2,1)S(1)} %copy.25), kind=kLoop, calls=%fused_computation.24 | loop fusion | bytes 73728
  5.6 0.6 %fusion.11 = bf16[16,24,6,128]{3,1,2,0:T(8,128)(2,1)} fusion(bf16[16,24,6,128]{3,1,2,0:T(8,128)(2,1)} %fusion.12, bf16[24,64,128]{2,0,1:T(8,128)(2,1)S(1)} %copy.25), kind=kLoop, calls=%fused_computation.22 | loop fusion | bytes 73728
  6.3 0.6 %fusion.10 = bf16[16,24,6,128]{3,1,2,0:T(8,128)(2,1)} fusion(bf16[16,24,6,128]{3,1,2,0:T(8,128)(2,1)} %fusion.11, bf16[24,64,128]{2,0,1:T(8,128)(2,1)S(1)} %copy.25), kind=kLoop, calls=%fused_computation.20 | loop fusion | bytes 73728
  6.9 0.6 %fusion.9 = bf16[16,24,6,128]{3,1,2,0:T(8,128)(2,1)} fusion(bf16[16,24,6,128]{3,1,2,0:T(8,128)(2,1)} %fusion.10, bf16[24,64,128]{2,0,1:T(8,128)(2,1)S(1)} %copy.25), kind=kLoop, calls=%fused_computation.18 | loop fusion | bytes 73728
  7.5 0.6 %fusion.8 = bf16[16,24,6,128]{3,1,2,0:T(8,128)(2,1)} fusion(bf16[16,24,6,128]{3,1,2,0:T(8,128)(2,1)} %fusion.9, bf16[24,64,128]{2,0,1:T(8,128)(2,1)S(1)} %copy.25), kind=kLoop, calls=%fused_computation.16 | loop fusion | bytes 73728
  8.1 0.6 %fusion.7 = bf16[16,24,6,128]{3,1,2,0:T(8,128)(2,1)} fusion(bf16[16,24,6,128]{3,1,2,0:T(8,128)(2,1)} %fusion.8, bf16[24,64,128]{2,0,1:T(8,128)(2,1)S(1)} %copy.25), kind=kLoop, calls=%fused_computation.14 | loop fusion | bytes 73728
  8.7 0.6 %fusion.6 = bf16[16,24,6,128]{3,1,2,0:T(8,128)(2,1)} fusion(bf16[16,24,6,128]{3,1,2,0:T(8,128)(2,1)} %fusion.7, bf16[24,64,128]{2,0,1:T(8,128)(2,1)S(1)} %copy.25), kind=kLoop, calls=%fused_computation.12 | loop fusion | bytes 73728
  9.3 0.6 %fusion.5 = bf16[16,24,6,128]{3,1,2,0:T(8,128)(2,1)} fusion(bf16[16,24,6,128]{3,1,2,0:T(8,128)(2,1)} %fusion.6, bf16[24,64,128]{2,0,1:T(8,128)(2,1)S(1)} %copy.25), kind=kLoop, calls=%fused_computation.10 | loop fusion | bytes 73728
  9.9 0.6 %fusion.4 = bf16[16,24,6,128]{3,1,2,0:T(8,128)(2,1)} fusion(bf16[16,24,6,128]{3,1,2,0:T(8,128)(2,1)} %fusion.5, bf16[24,64,128]{2,0,1:T(8,128)(2,1)S(1)} %copy.25), kind=kLoop, calls=%fused_computation.8 | loop fusion | bytes 73728
  10.5 0.6 %fusion.3 = bf16[16,24,6,128]{3,1,2,0:T(8,128)(2,1)} fusion(bf16[16,24,6,128]{3,1,2,0:T(8,128)(2,1)} %fusion.4, bf16[24,64,128]{2,0,1:T(8,128)(2,1)S(1)} %copy.25), kind=kLoop, calls=%fused_computation.6 | loop fusion | bytes 430080 | tf_op jit(solution)/shard_map/stack | solution.py:13
  11.2 6.6 %all-to-all-start = ((bf16[16,6,24,128]{3,2,1,0:T(8,128)(2,1)}), bf16[16,6,24,128]{3,2,1,0:T(8,128)(2,1)S(1)}, u32[]{:S(2)}, u32[]{:S(2)}) async-start(bf16[16,6,24,128]{3,2,1,0:T(8,128)(2,1)} %bitcast.18), calls=%async_computation | async-start | bytes 1179648 | tf_op jit(solution)/shard_map/all_to_all | solution.py:15
  17.9 0.9 %copy-done.2 = bf16[192,8,256]{2,0,1:T(8,128)(2,1)} copy-done((bf16[192,8,256]{2,0,1:T(8,128)(2,1)}, bf16[192,8,256]{2,0,1:T(8,128)(2,1)S(1)}, u32[]{:S(2)}) %copy-start.2) | copy-done | bytes 786456
  18.8 3.3 %collective-permute-start = (bf16[192,1,256]{2,0,1:T(8,128)(2,1)S(1)}, bf16[192,1,256]{2,0,1:T(8,128)(2,1)S(1)}, u32[]{:S(2)}, u32[]{:S(2)}) collective-permute-start(bf16[192,1,256]{2,0,1:T(8,128)(2,1)S(1)} %get-tuple-element.5), channel_id=1, source_target_pairs={{0,1},{1,2},{2,3},{3,4},{4,5},{5,6},{6,7},{7,8},{8,9},{9,10},{10,1... | collective-permute-start | bytes 294920 | tf_op jit(solution)/shard_map/ppermute | solution.py:24
  22.1 1.9 %collective-permute-start.1 = (bf16[192,1,256]{2,0,1:T(8,128)(2,1)S(1)}, bf16[192,1,256]{2,0,1:T(8,128)(2,1)S(1)}, u32[]{:S(2)}, u32[]{:S(2)}) collective-permute-start(bf16[192,1,256]{2,0,1:T(8,128)(2,1)S(1)} %get-tuple-element.6), channel_id=1, source_target_pairs={{1,0},{2,1},{3,2},{4,3},{5,4},{6,5},{7,6},{8,7},{9,8},{10,9},{11,1... | collective-permute-start | bytes 294920 | tf_op jit(solution)/shard_map/ppermute | solution.py:25
  24.4 7.7 %collective-permute-done = bf16[192,1,256]{2,0,1:T(8,128)(2,1)S(1)} collective-permute-done((bf16[192,1,256]{2,0,1:T(8,128)(2,1)S(1)}, bf16[192,1,256]{2,0,1:T(8,128)(2,1)S(1)}, u32[]{:S(2)}, u32[]{:S(2)}) %collective-permute-start) | collective-permute-done | bytes 98336 | tf_op jit(solution)/shard_map/ppermute | solution.py:24
  32.1 1.7 %collective-permute-done.1 = bf16[192,1,256]{2,0,1:T(8,128)(2,1)S(1)} collective-permute-done((bf16[192,1,256]{2,0,1:T(8,128)(2,1)S(1)}, bf16[192,1,256]{2,0,1:T(8,128)(2,1)S(1)}, u32[]{:S(2)}, u32[]{:S(2)}) %collective-permute-start.1) | collective-permute-done | bytes 98336 | tf_op jit(solution)/shard_map/ppermute | solution.py:25
  33.8 1.3 %maximum_bitcast_fusion.sk_ref = bf16[10,192,256]{2,1,0:T(8,128)(2,1)S(1)} fusion(bf16[192,1,256]{2,0,1:T(8,128)(2,1)S(1)} %collective-permute-done.1, bf16[192,8,256]{2,0,1:T(8,128)(2,1)} %copy-done.2, bf16[192,1,256]{2,0,1:T(8,128)(2,1)S(1)} %collective-permute-done), kind=kLoop, calls=%fused_computation | loop fusion | flops 983040 | bytes 1966080 | tf_op jit(solution)/shard_map/transpose | solution.py:27
  35.1 1.7 %copy-done = bf16[4,4,384,192]{2,3,1,0:T(8,128)(2,1)S(1)} copy-done((bf16[4,4,384,192]{2,3,1,0:T(8,128)(2,1)S(1)}, bf16[4,4,384,192]{2,3,1,0:T(8,128)(2,1)}, u32[]{:S(2)}) %copy-start) | copy-done | bytes 2359320
  36.8 9.1 %shard_map.64 = bf16[192,8,256]{2,1,0:T(8,128)(2,1)} custom-call(s32[2]{0:T(128)S(1)} %add_convert_fusion.flags, bf16[16,6,24,128]{3,2,1,0:T(8,128)(2,1)S(1)} %all-to-all-done.xw_ref, bf16[10,192,256]{2,1,0:T(8,128)(2,1)S(1)} %maximum_bitcast_fusion.sk_ref, bf16[4,768,384]{2,1,0:T(8,128)(2,1)S(1)} %bitcast.77, f32[192,1]{1,0:T(8,128)S(1)} %copy.43.bu_ref, ...), custom_call_target="tpu_custom_call" | custom-call | tf_op jit(solution)/shard_map/pallas_call | solution.py:95
  (18 shorter events, 1.7 us)
Async XLA Ops:
  0.0 17.7 %copy-start.3 = (bf16[192,8,256]{2,1,0:T(8,128)(2,1)S(1)}, bf16[192,8,256]{2,1,0:T(8,128)(2,1)}, u32[]{:S(2)}) copy-start(bf16[192,8,256]{2,1,0:T(8,128)(2,1)} %param.7) | copy-start | bytes 2359300
  2.0 22.1 %copy-start.4 = (f32[192]{0:T(256)S(1)}, f32[192]{0:T(256)}, u32[]{:S(2)}) copy-start(f32[192]{0:T(256)} %param.9) | copy-start | bytes 2308
  2.0 22.3 %copy-start.5 = (f32[192]{0:T(256)S(1)}, f32[192]{0:T(256)}, u32[]{:S(2)}) copy-start(f32[192]{0:T(256)} %param.11) | copy-start | bytes 2308
  11.2 23.9 %all-to-all-start = ((bf16[16,6,24,128]{3,2,1,0:T(8,128)(2,1)}), bf16[16,6,24,128]{3,2,1,0:T(8,128)(2,1)S(1)}, u32[]{:S(2)}, u32[]{:S(2)}) async-start(bf16[16,6,24,128]{3,2,1,0:T(8,128)(2,1)} %bitcast.18), calls=%async_computation | async-start | bytes 1179648 | tf_op jit(solution)/shard_map/all_to_all | solution.py:15
  17.7 17.3 %copy-start.1 = (bf16[3,3,384,192]{2,3,1,0:T(8,128)(2,1)S(1)}, bf16[3,3,384,192]{2,3,1,0:T(8,128)(2,1)}, u32[]{:S(2)}) copy-start(bf16[3,3,384,192]{2,3,1,0:T(8,128)(2,1)} %param.10) | copy-start | bytes 3981316
  17.9 0.9 %copy-start.2 = (bf16[192,8,256]{2,0,1:T(8,128)(2,1)}, bf16[192,8,256]{2,0,1:T(8,128)(2,1)S(1)}, u32[]{:S(2)}) copy-start(bf16[192,8,256]{2,0,1:T(8,128)(2,1)S(1)} %copy.40) | copy-start | bytes 2359300
  18.8 13.3 %collective-permute-start = (bf16[192,1,256]{2,0,1:T(8,128)(2,1)S(1)}, bf16[192,1,256]{2,0,1:T(8,128)(2,1)S(1)}, u32[]{:S(2)}, u32[]{:S(2)}) collective-permute-start(bf16[192,1,256]{2,0,1:T(8,128)(2,1)S(1)} %get-tuple-element.5), channel_id=1, source_target_pairs={{0,1},{1,2},{2,3},{3,4},{4,5},{5,6},{6,7},{7,8},{8,9},{9,10},{10,1... | collective-permute-start | bytes 294920 | tf_op jit(solution)/shard_map/ppermute | solution.py:24
  22.1 11.7 %collective-permute-start.1 = (bf16[192,1,256]{2,0,1:T(8,128)(2,1)S(1)}, bf16[192,1,256]{2,0,1:T(8,128)(2,1)S(1)}, u32[]{:S(2)}, u32[]{:S(2)}) collective-permute-start(bf16[192,1,256]{2,0,1:T(8,128)(2,1)S(1)} %get-tuple-element.6), channel_id=1, source_target_pairs={{1,0},{2,1},{3,2},{4,3},{5,4},{6,5},{7,6},{8,7},{9,8},{10,9},{11,1... | collective-permute-start | bytes 294920 | tf_op jit(solution)/shard_map/ppermute | solution.py:25
  35.1 1.7 %copy-start = (bf16[4,4,384,192]{2,3,1,0:T(8,128)(2,1)S(1)}, bf16[4,4,384,192]{2,3,1,0:T(8,128)(2,1)}, u32[]{:S(2)}) copy-start(bf16[4,4,384,192]{2,3,1,0:T(8,128)(2,1)} %param.8) | copy-start | bytes 7077892

commit v5 on v4

--- a/solution.py
+++ b/solution.py
@@ -9,9 +9,10 @@
 def coarse_windows(coarse, peers):
     groups, rows, cols = coarse.shape
     tile = rows // peers
-    padded = jnp.pad(coarse, ((0, 0), (1, 1), (0, 0)))
-    windows = jnp.stack([padded[:, r * tile : r * tile + tile + 2] for r in range(peers)])
-    windows = jnp.transpose(windows, (0, 2, 1, 3))
+    padded = jnp.pad(coarse, ((0, 0), (1, tile - 1), (0, 0)))
+    blocks = padded.reshape(groups, peers + 1, tile, cols)
+    windows = jnp.concatenate([blocks[:, :peers], blocks[:, 1:, :2]], axis=2)
+    windows = jnp.transpose(windows, (1, 2, 0, 3))
     gathered = lax.all_to_all(windows, "row", 0, 0, tiled=True)
     if groups % 8:
         gathered = jnp.transpose(gathered, (1, 0, 2, 3)).reshape(1, tile + 2, peers * groups, cols)

time: 46.2 us -> 37.4 us (0.81)
  local copies, waits for them, and re-layouts: 14.1 us -> 4.32 us
  other arithmetic: 1.33 us -> 2.2 us
    unnamed x29 -> x14, local copies, waits for them, and re-layouts: 13.2 us -> 3.97 us
    transpose x0 -> x1, other arithmetic: none -> 0.86 us  [coarse_windows(): windows = jnp.transpose(windows, (1, 2, 0, 3))]
    another operation x1 -> x0, local copies, waits for them, and re-layouts: 0.62 us -> none  [coarse_windows(): jnp.stack([padded[:, r * tile:r * tile + tile + 2] for r in range(peers)])]
  transfers between devices with their start and end apart: 3 -> 3, of which waited for: 2 -> 2; matrix products, arithmetic and copies ran while one was open for 4% -> 5% of each run, Pallas kernels for 0% -> 0%
where the time goes in v5:
time: 37.4 us; the launch traced here: 37 us
  starting transfers between devices  11.8 us (32%)
  waiting for transfers between devices  9.37 us (25%)
  Pallas kernels  9.14 us (24%)
  local copies, waits for them, and re-layouts  4.32 us (12%)
  other arithmetic  2.2 us (6%)
    pallas_call x1, Pallas kernels, decode(): pl.pallas_call(decoder_kernel, out_shape=jax.ShapeDtypeStruct((cout, nfin...  9.14 us
    ppermute x1, waiting for transfers between devices, skip_rows(): before = lax.ppermute(skip[:, -1:], 'row', up)  7.7 us
    all_to_all x1, starting transfers between devices, coarse_windows(): gathered = lax.all_to_all(windows, 'row', 0, 0, tiled=True)  6.55 us
    unnamed x14, local copies, waits for them, and re-layouts  3.97 us
    ppermute x1, starting transfers between devices, skip_rows(): before = lax.ppermute(skip[:, -1:], 'row', up)  3.34 us
    ppermute x1, starting transfers between devices, skip_rows(): after = lax.ppermute(skip[:, :1], 'row', down)  1.92 us
    ppermute x1, waiting for transfers between devices, skip_rows(): after = lax.ppermute(skip[:, :1], 'row', down)  1.67 us
    transpose x1, other arithmetic, skip_rows(): return jnp.transpose(rimmed, (1, 0, 2))  1.26 us
  transfers between devices with their start and end apart: 3, of which 2 were waited for; matrix products, arithmetic and copies ran while one was open for 5% of the time, Pallas kernels for 0%

profile of v5, /device:TPU:13, one launch (start us, length us, event | category | flops | bytes accessed | tf_op | source)
XLA Modules:
  0.0 37.0 jit_solution(11754566150953778036)
XLA Ops:
  0.0 1.3 %copy.17 = bf16[24,64,128]{2,0,1:T(8,128)(2,1)S(1)} copy(bf16[24,64,128]{2,1,0:T(8,128)(2,1)} %param.6) | data formatting | bytes 786432
  1.3 0.0 copy-start.3
  1.4 0.0 copy-start.4
  1.4 0.0 copy-start.5
  1.4 0.9 %maximum_bitcast_fusion.1 = bf16[16,6,24,128]{3,2,1,0:T(8,128)(2,1)} fusion(bf16[24,16,2,128]{3,0,2,1:T(8,128)(2,1)S(1)} %slice.17, bf16[24,16,4,128]{3,0,2,1:T(8,128)(2,1)S(1)} %slice.16), kind=kLoop, calls=%fused_computation.1 | loop fusion | flops 294912 | bytes 1179648 | tf_op jit(solution)/shard_map/transpose | solution.py:15
  2.3 6.6 %all-to-all-start = ((bf16[16,6,24,128]{3,2,1,0:T(8,128)(2,1)}), bf16[16,6,24,128]{3,2,1,0:T(8,128)(2,1)S(1)}, u32[]{:S(2)}, u32[]{:S(2)}) async-start(bf16[16,6,24,128]{3,2,1,0:T(8,128)(2,1)} %maximum_bitcast_fusion.1), calls=%async_computation | async-start | bytes 1179648 | tf_op jit(solution)/shard_map/all_to_all | solution.py:16
  8.8 0.0 copy-done.3
  8.8 0.0 copy-start.1
  8.9 0.2 copy.12
  9.0 0.0 copy-start.2
  9.0 0.9 %copy-done.2 = bf16[192,8,256]{2,0,1:T(8,128)(2,1)} copy-done((bf16[192,8,256]{2,0,1:T(8,128)(2,1)}, bf16[192,8,256]{2,0,1:T(8,128)(2,1)S(1)}, u32[]{:S(2)}) %copy-start.2) | copy-done | bytes 786456
  9.9 3.3 %collective-permute-start = (bf16[192,1,256]{2,0,1:T(8,128)(2,1)S(1)}, bf16[192,1,256]{2,0,1:T(8,128)(2,1)S(1)}, u32[]{:S(2)}, u32[]{:S(2)}) collective-permute-start(bf16[192,1,256]{2,0,1:T(8,128)(2,1)S(1)} %get-tuple-element.5), channel_id=1, source_target_pairs={{0,1},{1,2},{2,3},{3,4},{4,5},{5,6},{6,7},{7,8},{8,9},{9,10},{10,1... | collective-permute-start | bytes 294920 | tf_op jit(solution)/shard_map/ppermute | solution.py:25
  13.3 1.9 %collective-permute-start.1 = (bf16[192,1,256]{2,0,1:T(8,128)(2,1)S(1)}, bf16[192,1,256]{2,0,1:T(8,128)(2,1)S(1)}, u32[]{:S(2)}, u32[]{:S(2)}) collective-permute-start(bf16[192,1,256]{2,0,1:T(8,128)(2,1)S(1)} %get-tuple-element.6), channel_id=1, source_target_pairs={{1,0},{2,1},{3,2},{4,3},{5,4},{6,5},{7,6},{8,7},{9,8},{10,9},{11,1... | collective-permute-start | bytes 294920 | tf_op jit(solution)/shard_map/ppermute | solution.py:26
  15.2 0.1 copy.15.bu_ref
  15.3 0.0 copy-done.5
  15.3 0.1 copy.16.b3_ref
  15.5 0.1 add_convert_fusion.flags
  15.5 7.7 %collective-permute-done = bf16[192,1,256]{2,0,1:T(8,128)(2,1)S(1)} collective-permute-done((bf16[192,1,256]{2,0,1:T(8,128)(2,1)S(1)}, bf16[192,1,256]{2,0,1:T(8,128)(2,1)S(1)}, u32[]{:S(2)}, u32[]{:S(2)}) %collective-permute-start) | collective-permute-done | bytes 98336 | tf_op jit(solution)/shard_map/ppermute | solution.py:25
  23.2 1.7 %collective-permute-done.1 = bf16[192,1,256]{2,0,1:T(8,128)(2,1)S(1)} collective-permute-done((bf16[192,1,256]{2,0,1:T(8,128)(2,1)S(1)}, bf16[192,1,256]{2,0,1:T(8,128)(2,1)S(1)}, u32[]{:S(2)}, u32[]{:S(2)}) %collective-permute-start.1) | collective-permute-done | bytes 98336 | tf_op jit(solution)/shard_map/ppermute | solution.py:26
  24.9 1.3 %maximum_bitcast_fusion.sk_ref = bf16[10,192,256]{2,1,0:T(8,128)(2,1)S(1)} fusion(bf16[192,1,256]{2,0,1:T(8,128)(2,1)S(1)} %collective-permute-done.1, bf16[192,8,256]{2,0,1:T(8,128)(2,1)} %copy-done.2, bf16[192,1,256]{2,0,1:T(8,128)(2,1)S(1)} %collective-permute-done), kind=kLoop, calls=%fused_computation | loop fusion | flops 983040 | bytes 1966080 | tf_op jit(solution)/shard_map/transpose | solution.py:28
  26.2 0.0 all-to-all-done.xw_ref
  26.2 0.0 copy-start
  26.2 1.7 %copy-done = bf16[4,4,384,192]{2,3,1,0:T(8,128)(2,1)S(1)} copy-done((bf16[4,4,384,192]{2,3,1,0:T(8,128)(2,1)S(1)}, bf16[4,4,384,192]{2,3,1,0:T(8,128)(2,1)}, u32[]{:S(2)}) %copy-start) | copy-done | bytes 2359320
  27.9 9.1 %shard_map.64 = bf16[192,8,256]{2,1,0:T(8,128)(2,1)} custom-call(s32[2]{0:T(128)S(1)} %add_convert_fusion.flags, bf16[16,6,24,128]{3,2,1,0:T(8,128)(2,1)S(1)} %all-to-all-done.xw_ref, bf16[10,192,256]{2,1,0:T(8,128)(2,1)S(1)} %maximum_bitcast_fusion.sk_ref, bf16[4,768,384]{2,1,0:T(8,128)(2,1)S(1)} %bitcast.15, f32[192,1]{1,0:T(8,128)S(1)} %copy.15.bu_ref, ...), custom_call_target="tpu_custom_call" | custom-call | tf_op jit(solution)/shard_map/pallas_call | solution.py:96
  (6 shorter events, 0.1 us)
Async XLA Ops:
  1.3 7.6 %copy-start.3 = (bf16[192,8,256]{2,1,0:T(8,128)(2,1)S(1)}, bf16[192,8,256]{2,1,0:T(8,128)(2,1)}, u32[]{:S(2)}) copy-start(bf16[192,8,256]{2,1,0:T(8,128)(2,1)} %param.7) | copy-start | bytes 2359300
  1.4 13.8 %copy-start.4 = (f32[192]{0:T(256)S(1)}, f32[192]{0:T(256)}, u32[]{:S(2)}) copy-start(f32[192]{0:T(256)} %param.9) | copy-start | bytes 2308
  1.4 14.0 %copy-start.5 = (f32[192]{0:T(256)S(1)}, f32[192]{0:T(256)}, u32[]{:S(2)}) copy-start(f32[192]{0:T(256)} %param.11) | copy-start | bytes 2308
  2.3 23.9 %all-to-all-start = ((bf16[16,6,24,128]{3,2,1,0:T(8,128)(2,1)}), bf16[16,6,24,128]{3,2,1,0:T(8,128)(2,1)S(1)}, u32[]{:S(2)}, u32[]{:S(2)}) async-start(bf16[16,6,24,128]{3,2,1,0:T(8,128)(2,1)} %maximum_bitcast_fusion.1), calls=%async_computation | async-start | bytes 1179648 | tf_op jit(solution)/shard_map/all_to_all | solution.py:16
  8.8 17.3 %copy-start.1 = (bf16[3,3,384,192]{2,3,1,0:T(8,128)(2,1)S(1)}, bf16[3,3,384,192]{2,3,1,0:T(8,128)(2,1)}, u32[]{:S(2)}) copy-start(bf16[3,3,384,192]{2,3,1,0:T(8,128)(2,1)} %param.10) | copy-start | bytes 3981316
  9.0 0.9 %copy-start.2 = (bf16[192,8,256]{2,0,1:T(8,128)(2,1)}, bf16[192,8,256]{2,0,1:T(8,128)(2,1)S(1)}, u32[]{:S(2)}) copy-start(bf16[192,8,256]{2,0,1:T(8,128)(2,1)S(1)} %copy.12) | copy-start | bytes 2359300
  9.9 13.3 %collective-permute-start = (bf16[192,1,256]{2,0,1:T(8,128)(2,1)S(1)}, bf16[192,1,256]{2,0,1:T(8,128)(2,1)S(1)}, u32[]{:S(2)}, u32[]{:S(2)}) collective-permute-start(bf16[192,1,256]{2,0,1:T(8,128)(2,1)S(1)} %get-tuple-element.5), channel_id=1, source_target_pairs={{0,1},{1,2},{2,3},{3,4},{4,5},{5,6},{6,7},{7,8},{8,9},{9,10},{10,1... | collective-permute-start | bytes 294920 | tf_op jit(solution)/shard_map/ppermute | solution.py:25
  13.3 11.7 %collective-permute-start.1 = (bf16[192,1,256]{2,0,1:T(8,128)(2,1)S(1)}, bf16[192,1,256]{2,0,1:T(8,128)(2,1)S(1)}, u32[]{:S(2)}, u32[]{:S(2)}) collective-permute-start(bf16[192,1,256]{2,0,1:T(8,128)(2,1)S(1)} %get-tuple-element.6), channel_id=1, source_target_pairs={{1,0},{2,1},{3,2},{4,3},{5,4},{6,5},{7,6},{8,7},{9,8},{10,9},{11,1... | collective-permute-start | bytes 294920 | tf_op jit(solution)/shard_map/ppermute | solution.py:26
  26.2 1.7 %copy-start = (bf16[4,4,384,192]{2,3,1,0:T(8,128)(2,1)S(1)}, bf16[4,4,384,192]{2,3,1,0:T(8,128)(2,1)}, u32[]{:S(2)}) copy-start(bf16[4,4,384,192]{2,3,1,0:T(8,128)(2,1)} %param.8) | copy-start | bytes 7077892

commit v6 on v5

--- a/solution.py
+++ b/solution.py
@@ -34,7 +34,11 @@
     return jnp.where(lane == edge, 0.0, pltpu.roll(v, step % v.shape[1], 1))
 
 
-def decoder_kernel(flags, xw_ref, sk_ref, wu_ref, bu_ref, w3_ref, b3_ref, out_ref, act_ref):
+def decoder_kernel(flags, xw_ref, sk_ref, wu_hbm, bu_ref, w3_hbm, b3_ref, out_ref, act_ref, wu_ref, w3_ref, sems):
+    loads = [pltpu.make_async_copy(wu_hbm.at[k], wu_ref.at[k], sems.at[k]) for k in range(4)]
+    loads.append(pltpu.make_async_copy(w3_hbm, w3_ref, sems.at[4]))
+    for load in loads:
+        load.start()
     peers, nwin, groups, cw = xw_ref.shape
     nfine, cout, fw = sk_ref.shape
     nout = nfine - 2
@@ -54,6 +58,8 @@
     later, earlier = wide[:, cw:], wide[:, :span]
     parity = []
     for first, second in ((0, 2), (1, 3)):
+        loads[first].wait()
+        loads[second].wait()
         z = dot(wu_ref[first], later) + dot(wu_ref[second], earlier)
         taps = [z[k * cout : (k + 1) * cout] for k in range(4)]
         even = taps[1] + lane_shift(taps[3], cw, 1) + bu_ref[...]
@@ -76,6 +82,7 @@
             row = jnp.where(flags[1] == 1, 0.0, row)
         joined.append(jnp.concatenate([sk_ref[t], row.astype(jnp.bfloat16)], axis=0))
     field = jnp.concatenate(joined, axis=1)
+    loads[4].wait()
 
     total = None
     for ky in range(3):
@@ -93,14 +100,20 @@
 def decode(flags, xw, sk, wu, bu, w3, b3):
     nfine, cout, fw = sk.shape
     vmem = pl.BlockSpec(memory_space=pltpu.VMEM)
+    hbm = pl.BlockSpec(memory_space=pltpu.HBM)
     return pl.pallas_call(
         decoder_kernel,
         out_shape=jax.ShapeDtypeStruct((cout, nfine - 2, fw), jnp.bfloat16),
-        in_specs=[pl.BlockSpec(memory_space=pltpu.SMEM)] + [vmem] * 6,
+        in_specs=[pl.BlockSpec(memory_space=pltpu.SMEM), vmem, vmem, hbm, vmem, hbm, vmem],
         out_specs=vmem,
-        scratch_shapes=[pltpu.VMEM((cout, nfine - 2, fw), jnp.float32)],
+        scratch_shapes=[
+            pltpu.VMEM((cout, nfine - 2, fw), jnp.float32),
+            pltpu.VMEM(wu.shape, wu.dtype),
+            pltpu.VMEM(w3.shape, w3.dtype),
+            pltpu.SemaphoreType.DMA((5,)),
+        ],
         compiler_params=pltpu.CompilerParams(vmem_limit_bytes=48 * 1024 * 1024),
-    )(flags, xw, sk, wu, bu, w3, b3)
+    )(flags, xw, sk, pltpu.with_memory_space_constraint(wu, pltpu.HBM), bu, pltpu.with_memory_space_constraint(w3, pltpu.HBM), b3)
 
 
 def shards(coarse, skip_field, up_weight, up_bias, conv_weight, conv_bias):

time: 37.4 us -> 36.4 us (0.973)
  local copies, waits for them, and re-layouts: 4.32 us -> 1.78 us
  Pallas kernels: 9.14 us -> 10.9 us
  other arithmetic: 2.2 us -> 1.07 us
  waiting for transfers between devices: 9.37 us -> 10.3 us
    unnamed x14 -> x8, local copies, waits for them, and re-layouts: 3.97 us -> 1.43 us
    pallas_call x1, Pallas kernels: 9.14 us -> 10.9 us  [decode(): pl.pallas_call(decoder_kernel, out_shape=jax.ShapeDtypeStruct((cout, nfin...]
    transpose x1, other arithmetic: 1.26 us -> 0.12 us  [skip_rows(): return jnp.transpose(rimmed, (1, 0, 2))]
    ppermute x1, waiting for transfers between devices: 7.7 us -> 8.59 us  [skip_rows(): before = lax.ppermute(skip[:, -1:], 'row', up)]
  transfers between devices with their start and end apart: 3 -> 3, of which waited for: 2 -> 2; matrix products, arithmetic and copies ran while one was open for 5% -> 2% of each run, Pallas kernels for 0% -> 0%
where the time goes in v6:
time: 36.4 us; the launch traced here: 36 us
  starting transfers between devices  11.8 us (32%)
  Pallas kernels  10.9 us (30%)
  waiting for transfers between devices  10.3 us (28%)
  local copies, waits for them, and re-layouts  1.78 us (5%)
  other arithmetic  1.07 us (3%)
    pallas_call x1, Pallas kernels, decode(): pl.pallas_call(decoder_kernel, out_shape=jax.ShapeDtypeStruct((cout, nfin...  10.9 us
    ppermute x1, waiting for transfers between devices, skip_rows(): before = lax.ppermute(skip[:, -1:], 'row', up)  8.59 us
    all_to_all x1, starting transfers between devices, coarse_windows(): gathered = lax.all_to_all(windows, 'row', 0, 0, tiled=True)  6.55 us
    ppermute x1, starting transfers between devices, skip_rows(): before = lax.ppermute(skip[:, -1:], 'row', up)  3.34 us
    ppermute x1, starting transfers between devices, skip_rows(): after = lax.ppermute(skip[:, :1], 'row', down)  1.92 us
    ppermute x1, waiting for transfers between devices, skip_rows(): after = lax.ppermute(skip[:, :1], 'row', down)  1.67 us
    unnamed x8, local copies, waits for them, and re-layouts  1.43 us
    transpose x1, other arithmetic, coarse_windows(): windows = jnp.transpose(windows, (1, 2, 0, 3))  0.87 us
  transfers between devices with their start and end apart: 3, of which 2 were waited for; matrix products, arithmetic and copies ran while one was open for 2% of the time, Pallas kernels for 0%

profile of v6, /device:TPU:13, one launch (start us, length us, event | category | flops | bytes accessed | tf_op | source)
XLA Modules:
  0.0 36.0 jit_solution(4850923217773974560)
XLA Ops:
  0.0 1.3 %copy.17 = bf16[24,64,128]{2,0,1:T(8,128)(2,1)S(1)} copy(bf16[24,64,128]{2,1,0:T(8,128)(2,1)} %param.6) | data formatting | bytes 786432
  1.3 0.0 copy-start
  1.4 0.0 copy-start.1
  1.4 0.0 copy-start.2
  1.4 0.9 %maximum_bitcast_fusion.1 = bf16[16,6,24,128]{3,2,1,0:T(8,128)(2,1)} fusion(bf16[24,16,2,128]{3,0,2,1:T(8,128)(2,1)S(1)} %slice.17, bf16[24,16,4,128]{3,0,2,1:T(8,128)(2,1)S(1)} %slice.16), kind=kLoop, calls=%fused_computation.1 | loop fusion | flops 294912 | bytes 1179648 | tf_op jit(solution)/shard_map/transpose | solution.py:15
  2.3 6.6 %all-to-all-start = ((bf16[16,6,24,128]{3,2,1,0:T(8,128)(2,1)}), bf16[16,6,24,128]{3,2,1,0:T(8,128)(2,1)S(1)}, u32[]{:S(2)}, u32[]{:S(2)}) async-start(bf16[16,6,24,128]{3,2,1,0:T(8,128)(2,1)} %maximum_bitcast_fusion.1), calls=%async_computation | async-start | bytes 1179648 | tf_op jit(solution)/shard_map/all_to_all | solution.py:16
  8.8 0.0 copy-done
  8.8 0.2 copy.12
  9.0 3.3 %collective-permute-start = (bf16[192,1,256]{2,0,1:T(8,128)(2,1)S(1)}, bf16[192,1,256]{2,0,1:T(8,128)(2,1)S(1)}, u32[]{:S(2)}, u32[]{:S(2)}) collective-permute-start(bf16[192,1,256]{2,0,1:T(8,128)(2,1)S(1)} %get-tuple-element.5), channel_id=1, source_target_pairs={{0,1},{1,2},{2,3},{3,4},{4,5},{5,6},{6,7},{7,8},{8,9},{9,10},{10,1... | collective-permute-start | bytes 294920 | tf_op jit(solution)/shard_map/ppermute | solution.py:25
  12.4 1.9 %collective-permute-start.1 = (bf16[192,1,256]{2,0,1:T(8,128)(2,1)S(1)}, bf16[192,1,256]{2,0,1:T(8,128)(2,1)S(1)}, u32[]{:S(2)}, u32[]{:S(2)}) collective-permute-start(bf16[192,1,256]{2,0,1:T(8,128)(2,1)S(1)} %get-tuple-element.6), channel_id=1, source_target_pairs={{1,0},{2,1},{3,2},{4,3},{5,4},{6,5},{7,6},{8,7},{9,8},{10,9},{11,1... | collective-permute-start | bytes 294920 | tf_op jit(solution)/shard_map/ppermute | solution.py:26
  14.3 0.0 copy-done.1
  14.3 0.1 copy.15.bu_ref
  14.5 0.0 copy-done.2
  14.5 0.1 copy.16.b3_ref
  14.6 0.1 add_convert_fusion.flags
  14.7 8.6 %collective-permute-done = bf16[192,1,256]{2,0,1:T(8,128)(2,1)S(1)} collective-permute-done((bf16[192,1,256]{2,0,1:T(8,128)(2,1)S(1)}, bf16[192,1,256]{2,0,1:T(8,128)(2,1)S(1)}, u32[]{:S(2)}, u32[]{:S(2)}) %collective-permute-start) | collective-permute-done | bytes 98336 | tf_op jit(solution)/shard_map/ppermute | solution.py:25
  23.2 1.7 %collective-permute-done.1 = bf16[192,1,256]{2,0,1:T(8,128)(2,1)S(1)} collective-permute-done((bf16[192,1,256]{2,0,1:T(8,128)(2,1)S(1)}, bf16[192,1,256]{2,0,1:T(8,128)(2,1)S(1)}, u32[]{:S(2)}, u32[]{:S(2)}) %collective-permute-start.1) | collective-permute-done | bytes 98336 | tf_op jit(solution)/shard_map/ppermute | solution.py:26
  24.9 0.1 maximum_bitcast_fusion.sk_ref
  25.0 0.0 all-to-all-done.xw_ref
  25.1 10.9 %shard_map.64 = bf16[192,8,256]{2,1,0:T(8,128)(2,1)} custom-call(s32[2]{0:T(128)S(1)} %add_convert_fusion.flags, bf16[16,6,24,128]{3,2,1,0:T(8,128)(2,1)S(1)} %all-to-all-done.xw_ref, bf16[10,192,256]{2,1,0:T(8,128)(2,1)S(1)} %maximum_bitcast_fusion.sk_ref, bf16[4,768,384]{2,1,0:T(8,128)(2,1)} %bitcast.17, f32[192,1]{1,0:T(8,128)S(1)} %copy.15.bu_ref, ...), custom_call_target="tpu_custom_call" | custom-call | tf_op jit(solution)/shard_map/pallas_call | solution.py:104
  (4 shorter events, 0.1 us)
Async XLA Ops:
  1.3 7.6 %copy-start = (bf16[192,8,256]{2,1,0:T(8,128)(2,1)S(1)}, bf16[192,8,256]{2,1,0:T(8,128)(2,1)}, u32[]{:S(2)}) copy-start(bf16[192,8,256]{2,1,0:T(8,128)(2,1)} %param.7) | copy-start | bytes 2359300
  1.4 13.0 %copy-start.1 = (f32[192]{0:T(256)S(1)}, f32[192]{0:T(256)}, u32[]{:S(2)}) copy-start(f32[192]{0:T(256)} %param.9) | copy-start | bytes 2308
  1.4 13.1 %copy-start.2 = (f32[192]{0:T(256)S(1)}, f32[192]{0:T(256)}, u32[]{:S(2)}) copy-start(f32[192]{0:T(256)} %param.11) | copy-start | bytes 2308
  2.3 22.8 %all-to-all-start = ((bf16[16,6,24,128]{3,2,1,0:T(8,128)(2,1)}), bf16[16,6,24,128]{3,2,1,0:T(8,128)(2,1)S(1)}, u32[]{:S(2)}, u32[]{:S(2)}) async-start(bf16[16,6,24,128]{3,2,1,0:T(8,128)(2,1)} %maximum_bitcast_fusion.1), calls=%async_computation | async-start | bytes 1179648 | tf_op jit(solution)/shard_map/all_to_all | solution.py:16
  9.0 14.2 %collective-permute-start = (bf16[192,1,256]{2,0,1:T(8,128)(2,1)S(1)}, bf16[192,1,256]{2,0,1:T(8,128)(2,1)S(1)}, u32[]{:S(2)}, u32[]{:S(2)}) collective-permute-start(bf16[192,1,256]{2,0,1:T(8,128)(2,1)S(1)} %get-tuple-element.5), channel_id=1, source_target_pairs={{0,1},{1,2},{2,3},{3,4},{4,5},{5,6},{6,7},{7,8},{8,9},{9,10},{10,1... | collective-permute-start | bytes 294920 | tf_op jit(solution)/shard_map/ppermute | solution.py:25
  12.4 12.5 %collective-permute-start.1 = (bf16[192,1,256]{2,0,1:T(8,128)(2,1)S(1)}, bf16[192,1,256]{2,0,1:T(8,128)(2,1)S(1)}, u32[]{:S(2)}, u32[]{:S(2)}) collective-permute-start(bf16[192,1,256]{2,0,1:T(8,128)(2,1)S(1)} %get-tuple-element.6), channel_id=1, source_target_pairs={{1,0},{2,1},{3,2},{4,3},{5,4},{6,5},{7,6},{8,7},{9,8},{10,9},{11,1... | collective-permute-start | bytes 294920 | tf_op jit(solution)/shard_map/ppermute | solution.py:26

commit v7 on v6

--- a/solution.py
+++ b/solution.py
@@ -34,10 +34,22 @@
     return jnp.where(lane == edge, 0.0, pltpu.roll(v, step % v.shape[1], 1))
 
 
+def conv_rows(field, w_ref, nout, fw):
+    total = None
+    for ky in range(3):
+        part = jnp.dot(w_ref[ky], field[:, ky * fw : (ky + nout) * fw], preferred_element_type=jnp.float32)
+        total = part if total is None else total + part
+    cout = total.shape[0] // 3
+    mid = total[cout : 2 * cout]
+    return mid + lane_shift(total[:cout], fw, 1) + lane_shift(total[2 * cout :], fw, -1)
+
+
 def decoder_kernel(flags, xw_ref, sk_ref, wu_hbm, bu_ref, w3_hbm, b3_ref, out_ref, act_ref, wu_ref, w3_ref, sems):
-    loads = [pltpu.make_async_copy(wu_hbm.at[k], wu_ref.at[k], sems.at[k]) for k in range(4)]
-    loads.append(pltpu.make_async_copy(w3_hbm, w3_ref, sems.at[4]))
-    for load in loads:
+    loads = {("w3", 0): pltpu.make_async_copy(w3_hbm.at[0], w3_ref.at[0], sems.at[4])}
+    for k in (0, 2, 1, 3):
+        loads[("wu", k)] = pltpu.make_async_copy(wu_hbm.at[k], wu_ref.at[k], sems.at[k])
+    loads[("w3", 1)] = pltpu.make_async_copy(w3_hbm.at[1], w3_ref.at[1], sems.at[5])
+    for load in loads.values():
         load.start()
     peers, nwin, groups, cw = xw_ref.shape
     nfine, cout, fw = sk_ref.shape
@@ -54,12 +66,16 @@
         pieces = [xw_ref[s, i].astype(f32) for s in range(peers)]
         return jnp.concatenate(pieces, axis=0).astype(jnp.bfloat16)
 
+    skips = jnp.concatenate([sk_ref[t] for t in range(nfine)], axis=1)
+    loads[("w3", 0)].wait()
+    pre = conv_rows(skips, w3_ref.at[0], nout, fw) + b3_ref[...]
+
     wide = jnp.concatenate([window_row(i) for i in range(nwin)], axis=1)
     later, earlier = wide[:, cw:], wide[:, :span]
     parity = []
     for first, second in ((0, 2), (1, 3)):
-        loads[first].wait()
-        loads[second].wait()
+        loads[("wu", first)].wait()
+        loads[("wu", second)].wait()
         z = dot(wu_ref[first], later) + dot(wu_ref[second], earlier)
         taps = [z[k * cout : (k + 1) * cout] for k in range(4)]
         even = taps[1] + lane_shift(taps[3], cw, 1) + bu_ref[...]
@@ -80,17 +96,10 @@
             row = jnp.where(flags[0] == 1, 0.0, row)
         if t == nfine - 1:
             row = jnp.where(flags[1] == 1, 0.0, row)
-        joined.append(jnp.concatenate([sk_ref[t], row.astype(jnp.bfloat16)], axis=0))
+        joined.append(row.astype(jnp.bfloat16))
     field = jnp.concatenate(joined, axis=1)
-    loads[4].wait()
-
-    total = None
-    for ky in range(3):
-        part = dot(w3_ref[ky], field[:, ky * fw : (ky + nout) * fw])
-        total = part if total is None else total + part
-    pre = total[cout : 2 * cout]
-    pre = pre + lane_shift(total[:cout], fw, 1) + lane_shift(total[2 * cout :], fw, -1)
-    pre = pre + b3_ref[...]
+    loads[("w3", 1)].wait()
+    pre = pre + conv_rows(field, w3_ref.at[1], nout, fw)
     act = pre / (1.0 + jnp.exp(-pre))
     for y in range(nout):
         act_ref[:, y, :] = act[:, y * fw : (y + 1) * fw]
@@ -110,7 +119,7 @@
             pltpu.VMEM((cout, nfine - 2, fw), jnp.float32),
             pltpu.VMEM(wu.shape, wu.dtype),
             pltpu.VMEM(w3.shape, w3.dtype),
-            pltpu.SemaphoreType.DMA((5,)),
+            pltpu.SemaphoreType.DMA((6,)),
         ],
         compiler_params=pltpu.CompilerParams(vmem_limit_bytes=48 * 1024 * 1024),
     )(flags, xw, sk, pltpu.with_memory_space_constraint(wu, pltpu.HBM), bu, pltpu.with_memory_space_constraint(w3, pltpu.HBM), b3)
@@ -124,7 +133,8 @@
     xw = coarse_windows(coarse, peers)
     cout = up_weight.shape[3]
     wu = jnp.transpose(up_weight, (0, 1, 3, 2)).reshape(4, 4 * cout, -1)
-    w3 = jnp.transpose(conv_weight, (0, 1, 3, 2)).reshape(3, 3 * cout, -1)
+    halves = conv_weight.reshape(3, 3, 2, -1, cout)
+    w3 = jnp.transpose(halves, (2, 0, 1, 4, 3)).reshape(2, 3, 3 * cout, -1)
     return decode(flags, xw, sk, wu, up_bias[:, None], w3, conv_bias[:, None])
 
 

time: 36.4 us -> 37 us (1.016)
  waiting for transfers between devices: 10.3 us -> 4.22 us
  local copies, waits for them, and re-layouts: 1.78 us -> 7.8 us
  Pallas kernels: 10.9 us -> 11.5 us
    ppermute x1, waiting for transfers between devices: 8.59 us -> 2.54 us  [skip_rows(): before = lax.ppermute(skip[:, -1:], 'row', up)]
    reshape x0 -> x2, local copies, waits for them, and re-layouts: none -> 6.02 us  [shards(): halves = conv_weight.reshape(3, 3, 2, -1, cout)]
    pallas_call x1, Pallas kernels: 10.9 us -> 11.5 us  [decode(): pl.pallas_call(decoder_kernel, out_shape=jax.ShapeDtypeStruct((cout, nfin...]
  transfers between devices with their start and end apart: 3 -> 3, of which waited for: 2 -> 2; matrix products, arithmetic and copies ran while one was open for 2% -> 18% of each run, Pallas kernels for 0% -> 0%
where the time goes in v7:
time: 37 us; the launch traced here: 36.5 us
  starting transfers between devices  11.8 us (32%)
  Pallas kernels  11.5 us (31%)
  local copies, waits for them, and re-layouts  7.8 us (21%)
  waiting for transfers between devices  4.22 us (11%)
  other arithmetic  1.07 us (3%)
    pallas_call x1, Pallas kernels, decode(): pl.pallas_call(decoder_kernel, out_shape=jax.ShapeDtypeStruct((cout, nfin...  11.5 us
    all_to_all x1, starting transfers between devices, coarse_windows(): gathered = lax.all_to_all(windows, 'row', 0, 0, tiled=True)  6.55 us
    reshape x2, local copies, waits for them, and re-layouts, shards(): halves = conv_weight.reshape(3, 3, 2, -1, cout)  6.02 us
    ppermute x1, starting transfers between devices, skip_rows(): before = lax.ppermute(skip[:, -1:], 'row', up)  3.34 us
    ppermute x1, waiting for transfers between devices, skip_rows(): before = lax.ppermute(skip[:, -1:], 'row', up)  2.54 us
    ppermute x1, starting transfers between devices, skip_rows(): after = lax.ppermute(skip[:, :1], 'row', down)  1.92 us
    ppermute x1, waiting for transfers between devices, skip_rows(): after = lax.ppermute(skip[:, :1], 'row', down)  1.67 us
    unnamed x8, local copies, waits for them, and re-layouts  1.43 us
  transfers between devices with their start and end apart: 3, of which 2 were waited for; matrix products, arithmetic and copies ran while one was open for 18% of the time, Pallas kernels for 0%

profile of v7, /device:TPU:13, one launch (start us, length us, event | category | flops | bytes accessed | tf_op | source)
XLA Modules:
  0.0 36.5 jit_solution(8708112494576339224)
XLA Ops:
  0.0 1.3 %copy.19 = bf16[24,64,128]{2,0,1:T(8,128)(2,1)S(1)} copy(bf16[24,64,128]{2,1,0:T(8,128)(2,1)} %param.6) | data formatting | bytes 786432
  1.3 0.0 copy-start
  1.4 0.9 %maximum_bitcast_fusion.1 = bf16[16,6,24,128]{3,2,1,0:T(8,128)(2,1)} fusion(bf16[24,16,2,128]{3,0,2,1:T(8,128)(2,1)S(1)} %slice.17, bf16[24,16,4,128]{3,0,2,1:T(8,128)(2,1)S(1)} %slice.16), kind=kLoop, calls=%fused_computation.1 | loop fusion | flops 294912 | bytes 1179648 | tf_op jit(solution)/shard_map/transpose | solution.py:15
  2.3 6.6 %all-to-all-start = ((bf16[16,6,24,128]{3,2,1,0:T(8,128)(2,1)}), bf16[16,6,24,128]{3,2,1,0:T(8,128)(2,1)S(1)}, u32[]{:S(2)}, u32[]{:S(2)}) async-start(bf16[16,6,24,128]{3,2,1,0:T(8,128)(2,1)} %maximum_bitcast_fusion.1), calls=%async_computation | async-start | bytes 1179648 | tf_op jit(solution)/shard_map/all_to_all | solution.py:16
  8.8 0.0 copy-done
  8.8 0.2 copy.13
  9.0 3.3 %collective-permute-start = (bf16[192,1,256]{2,0,1:T(8,128)(2,1)S(1)}, bf16[192,1,256]{2,0,1:T(8,128)(2,1)S(1)}, u32[]{:S(2)}, u32[]{:S(2)}) collective-permute-start(bf16[192,1,256]{2,0,1:T(8,128)(2,1)S(1)} %get-tuple-element.5), channel_id=1, source_target_pairs={{0,1},{1,2},{2,3},{3,4},{4,5},{5,6},{6,7},{7,8},{8,9},{9,10},{10,1... | collective-permute-start | bytes 294920 | tf_op jit(solution)/shard_map/ppermute | solution.py:25
  12.4 1.9 %collective-permute-start.1 = (bf16[192,1,256]{2,0,1:T(8,128)(2,1)S(1)}, bf16[192,1,256]{2,0,1:T(8,128)(2,1)S(1)}, u32[]{:S(2)}, u32[]{:S(2)}) collective-permute-start(bf16[192,1,256]{2,0,1:T(8,128)(2,1)S(1)} %get-tuple-element.6), channel_id=1, source_target_pairs={{1,0},{2,1},{3,2},{4,3},{5,4},{6,5},{7,6},{8,7},{9,8},{10,9},{11,1... | collective-permute-start | bytes 294920 | tf_op jit(solution)/shard_map/ppermute | solution.py:26
  14.3 4.5 %reshape.14 = bf16[3,3,2,192,192]{3,2,4,1,0:T(2,128)(2,1)S(1)} reshape(bf16[3,3,384,192]{2,3,1,0:T(8,128)(2,1)} %param.10) | data formatting | bytes 2654208 | tf_op jit(solution)/shard_map/reshape | solution.py:136
  18.8 0.0 copy-start.1
  18.8 0.0 copy-start.2
  18.8 1.5 %copy.16 = bf16[3,3,2,192,192]{3,4,1,0,2:T(8,128)(2,1)} copy(bf16[3,3,2,192,192]{3,2,4,1,0:T(2,128)(2,1)S(1)} %reshape.14) | data formatting | bytes 2654208 | tf_op jit(solution)/shard_map/reshape | solution.py:136
  20.3 0.0 copy-done.1
  20.3 0.1 copy.17.bu_ref
  20.5 0.0 copy-done.2
  20.5 0.1 copy.18.b3_ref
  20.6 0.1 add_convert_fusion.flags
  20.7 2.5 %collective-permute-done = bf16[192,1,256]{2,0,1:T(8,128)(2,1)S(1)} collective-permute-done((bf16[192,1,256]{2,0,1:T(8,128)(2,1)S(1)}, bf16[192,1,256]{2,0,1:T(8,128)(2,1)S(1)}, u32[]{:S(2)}, u32[]{:S(2)}) %collective-permute-start) | collective-permute-done | bytes 98336 | tf_op jit(solution)/shard_map/ppermute | solution.py:25
  23.2 1.7 %collective-permute-done.1 = bf16[192,1,256]{2,0,1:T(8,128)(2,1)S(1)} collective-permute-done((bf16[192,1,256]{2,0,1:T(8,128)(2,1)S(1)}, bf16[192,1,256]{2,0,1:T(8,128)(2,1)S(1)}, u32[]{:S(2)}, u32[]{:S(2)}) %collective-permute-start.1) | collective-permute-done | bytes 98336 | tf_op jit(solution)/shard_map/ppermute | solution.py:26
  24.9 0.1 maximum_bitcast_fusion.sk_ref
  25.0 0.0 all-to-all-done.xw_ref
  25.0 11.5 %shard_map.64 = bf16[192,8,256]{2,1,0:T(8,128)(2,1)} custom-call(s32[2]{0:T(128)S(1)} %add_convert_fusion.flags, bf16[16,6,24,128]{3,2,1,0:T(8,128)(2,1)S(1)} %all-to-all-done.xw_ref, bf16[10,192,256]{2,1,0:T(8,128)(2,1)S(1)} %maximum_bitcast_fusion.sk_ref, bf16[4,768,384]{2,1,0:T(8,128)(2,1)} %bitcast.22, f32[192,1]{1,0:T(8,128)S(1)} %copy.17.bu_ref, ...), custom_call_target="tpu_custom_call" | custom-call | tf_op jit(solution)/shard_map/pallas_call | solution.py:113
  (4 shorter events, 0.1 us)
Async XLA Ops:
  1.3 7.5 %copy-start = (bf16[192,8,256]{2,1,0:T(8,128)(2,1)S(1)}, bf16[192,8,256]{2,1,0:T(8,128)(2,1)}, u32[]{:S(2)}) copy-start(bf16[192,8,256]{2,1,0:T(8,128)(2,1)} %param.7) | copy-start | bytes 2359300
  2.3 22.8 %all-to-all-start = ((bf16[16,6,24,128]{3,2,1,0:T(8,128)(2,1)}), bf16[16,6,24,128]{3,2,1,0:T(8,128)(2,1)S(1)}, u32[]{:S(2)}, u32[]{:S(2)}) async-start(bf16[16,6,24,128]{3,2,1,0:T(8,128)(2,1)} %maximum_bitcast_fusion.1), calls=%async_computation | async-start | bytes 1179648 | tf_op jit(solution)/shard_map/all_to_all | solution.py:16
  9.0 14.2 %collective-permute-start = (bf16[192,1,256]{2,0,1:T(8,128)(2,1)S(1)}, bf16[192,1,256]{2,0,1:T(8,128)(2,1)S(1)}, u32[]{:S(2)}, u32[]{:S(2)}) collective-permute-start(bf16[192,1,256]{2,0,1:T(8,128)(2,1)S(1)} %get-tuple-element.5), channel_id=1, source_target_pairs={{0,1},{1,2},{2,3},{3,4},{4,5},{5,6},{6,7},{7,8},{8,9},{9,10},{10,1... | collective-permute-start | bytes 294920 | tf_op jit(solution)/shard_map/ppermute | solution.py:25
  12.4 12.5 %collective-permute-start.1 = (bf16[192,1,256]{2,0,1:T(8,128)(2,1)S(1)}, bf16[192,1,256]{2,0,1:T(8,128)(2,1)S(1)}, u32[]{:S(2)}, u32[]{:S(2)}) collective-permute-start(bf16[192,1,256]{2,0,1:T(8,128)(2,1)S(1)} %get-tuple-element.6), channel_id=1, source_target_pairs={{1,0},{2,1},{3,2},{4,3},{5,4},{6,5},{7,6},{8,7},{9,8},{10,9},{11,1... | collective-permute-start | bytes 294920 | tf_op jit(solution)/shard_map/ppermute | solution.py:26
  18.8 1.6 %copy-start.1 = (f32[192]{0:T(256)S(1)}, f32[192]{0:T(256)}, u32[]{:S(2)}) copy-start(f32[192]{0:T(256)} %param.9) | copy-start | bytes 2308
  18.8 1.7 %copy-start.2 = (f32[192]{0:T(256)S(1)}, f32[192]{0:T(256)}, u32[]{:S(2)}) copy-start(f32[192]{0:T(256)} %param.11) | copy-start | bytes 2308

commit v8 on v6

--- a/solution.py
+++ b/solution.py
@@ -35,8 +35,8 @@
 
 
 def decoder_kernel(flags, xw_ref, sk_ref, wu_hbm, bu_ref, w3_hbm, b3_ref, out_ref, act_ref, wu_ref, w3_ref, sems):
-    loads = [pltpu.make_async_copy(wu_hbm.at[k], wu_ref.at[k], sems.at[k]) for k in range(4)]
-    loads.append(pltpu.make_async_copy(w3_hbm, w3_ref, sems.at[4]))
+    loads = [pltpu.make_async_copy(wu_hbm.at[k], wu_ref.at[k], sems.at[k]) for k in range(2)]
+    loads.append(pltpu.make_async_copy(w3_hbm, w3_ref, sems.at[2]))
     for load in loads:
         load.start()
     peers, nwin, groups, cw = xw_ref.shape
@@ -55,12 +55,11 @@
         return jnp.concatenate(pieces, axis=0).astype(jnp.bfloat16)
 
     wide = jnp.concatenate([window_row(i) for i in range(nwin)], axis=1)
-    later, earlier = wide[:, cw:], wide[:, :span]
+    stacked = jnp.concatenate([wide[:, cw:], wide[:, :span]], axis=0)
     parity = []
-    for first, second in ((0, 2), (1, 3)):
-        loads[first].wait()
-        loads[second].wait()
-        z = dot(wu_ref[first], later) + dot(wu_ref[second], earlier)
+    for p in range(2):
+        loads[p].wait()
+        z = dot(wu_ref[p], stacked)
         taps = [z[k * cout : (k + 1) * cout] for k in range(4)]
         even = taps[1] + lane_shift(taps[3], cw, 1) + bu_ref[...]
         odd = taps[2] + lane_shift(taps[0], cw, -1) + bu_ref[...]
@@ -82,12 +81,10 @@
             row = jnp.where(flags[1] == 1, 0.0, row)
         joined.append(jnp.concatenate([sk_ref[t], row.astype(jnp.bfloat16)], axis=0))
     field = jnp.concatenate(joined, axis=1)
-    loads[4].wait()
+    loads[2].wait()
 
-    total = None
-    for ky in range(3):
-        part = dot(w3_ref[ky], field[:, ky * fw : (ky + nout) * fw])
-        total = part if total is None else total + part
+    rows = jnp.concatenate([field[:, ky * fw : (ky + nout) * fw] for ky in range(3)], axis=0)
+    total = dot(w3_ref[...], rows)
     pre = total[cout : 2 * cout]
     pre = pre + lane_shift(total[:cout], fw, 1) + lane_shift(total[2 * cout :], fw, -1)
     pre = pre + b3_ref[...]
@@ -110,7 +107,7 @@
             pltpu.VMEM((cout, nfine - 2, fw), jnp.float32),
             pltpu.VMEM(wu.shape, wu.dtype),
             pltpu.VMEM(w3.shape, w3.dtype),
-            pltpu.SemaphoreType.DMA((5,)),
+            pltpu.SemaphoreType.DMA((3,)),
         ],
         compiler_params=pltpu.CompilerParams(vmem_limit_bytes=48 * 1024 * 1024),
     )(flags, xw, sk, pltpu.with_memory_space_constraint(wu, pltpu.HBM), bu, pltpu.with_memory_space_constraint(w3, pltpu.HBM), b3)
@@ -123,8 +120,8 @@
     sk = skip_rows(skip_field, peers)
     xw = coarse_windows(coarse, peers)
     cout = up_weight.shape[3]
-    wu = jnp.transpose(up_weight, (0, 1, 3, 2)).reshape(4, 4 * cout, -1)
-    w3 = jnp.transpose(conv_weight, (0, 1, 3, 2)).reshape(3, 3 * cout, -1)
+    wu = jnp.transpose(up_weight.reshape(2, 2, 4, -1, cout), (1, 2, 4, 0, 3)).reshape(2, 4 * cout, -1)
+    w3 = jnp.transpose(conv_weight, (1, 3, 0, 2)).reshape(3 * cout, -1)
     return decode(flags, xw, sk, wu, up_bias[:, None], w3, conv_bias[:, None])
 
 

time: 36.4 us -> 37.8 us (1.038)
  the two profiles are of different devices: /device:TPU:13 before, /device:TPU:1 now
where the time goes in v8:
time: 37.8 us; the launch traced here: 37.5 us
  local copies, waits for them, and re-layouts  13.3 us (35%)
  starting transfers between devices  12.8 us (34%)
  Pallas kernels  10.1 us (27%)
  other arithmetic  1.07 us (3%)
    pallas_call x1, Pallas kernels, decode(): pl.pallas_call(decoder_kernel, out_shape=jax.ShapeDtypeStruct((cout, nfin...  10.1 us
    all_to_all x1, starting transfers between devices, coarse_windows(): gathered = lax.all_to_all(windows, 'row', 0, 0, tiled=True)  7.35 us
    reshape x1, local copies, waits for them, and re-layouts, shards(): up_weight.reshape(2, 2, 4, -1, cout)  4.09 us
    unnamed x13, local copies, waits for them, and re-layouts  3.62 us
    ppermute x1, starting transfers between devices, skip_rows(): before = lax.ppermute(skip[:, -1:], 'row', up)  3.54 us
    reshape x1, local copies, waits for them, and re-layouts, shards(): jnp.transpose(up_weight.reshape(2, 2, 4, -1, cout), (1, 2, 4, 0, 3))  2.79 us
    transpose x1, local copies, waits for them, and re-layouts, shards(): w3 = jnp.transpose(conv_weight, (1, 3, 0, 2)).reshape(3 * cout, -1)  2.47 us
    ppermute x1, starting transfers between devices, skip_rows(): after = lax.ppermute(skip[:, :1], 'row', down)  1.92 us
  transfers between devices with their start and end apart: 3, of which 0 were waited for; matrix products, arithmetic and copies ran while one was open for 30% of the time, Pallas kernels for 0%

profile of v8, /device:TPU:1, one launch (start us, length us, event | category | flops | bytes accessed | tf_op | source)
XLA Modules:
  0.0 37.5 jit_solution(15739691043075452502)
XLA Ops:
  0.0 1.3 %copy.21 = bf16[24,64,128]{2,0,1:T(8,128)(2,1)S(1)} copy(bf16[24,64,128]{2,1,0:T(8,128)(2,1)} %param.6) | data formatting | bytes 786432
  1.3 0.0 copy-start.2
  1.4 0.9 %maximum_bitcast_fusion.1 = bf16[16,6,24,128]{3,2,1,0:T(8,128)(2,1)} fusion(bf16[24,16,2,128]{3,0,2,1:T(8,128)(2,1)S(1)} %slice.17, bf16[24,16,4,128]{3,0,2,1:T(8,128)(2,1)S(1)} %slice.16), kind=kLoop, calls=%fused_computation.2 | loop fusion | flops 294912 | bytes 1179648 | tf_op jit(solution)/shard_map/transpose | solution.py:15
  2.3 7.3 %all-to-all-start = ((bf16[16,6,24,128]{3,2,1,0:T(8,128)(2,1)}), bf16[16,6,24,128]{3,2,1,0:T(8,128)(2,1)S(1)}, u32[]{:S(2)}, u32[]{:S(2)}) async-start(bf16[16,6,24,128]{3,2,1,0:T(8,128)(2,1)} %maximum_bitcast_fusion.1), calls=%async_computation | async-start | bytes 1179648 | tf_op jit(solution)/shard_map/all_to_all | solution.py:16
  9.6 0.2 copy.14
  9.8 0.0 copy-start
  9.8 0.9 %copy-done = bf16[192,8,256]{2,0,1:T(8,128)(2,1)} copy-done((bf16[192,8,256]{2,0,1:T(8,128)(2,1)}, bf16[192,8,256]{2,0,1:T(8,128)(2,1)S(1)}, u32[]{:S(2)}) %copy-start) | copy-done | bytes 786456
  10.7 3.5 %collective-permute-start = (bf16[192,1,256]{2,0,1:T(8,128)(2,1)S(1)}, bf16[192,1,256]{2,0,1:T(8,128)(2,1)S(1)}, u32[]{:S(2)}, u32[]{:S(2)}) collective-permute-start(bf16[192,1,256]{2,0,1:T(8,128)(2,1)S(1)} %get-tuple-element.5), channel_id=1, source_target_pairs={{0,1},{1,2},{2,3},{3,4},{4,5},{5,6},{6,7},{7,8},{8,9},{9,10},{10,1... | collective-permute-start | bytes 294920 | tf_op jit(solution)/shard_map/ppermute | solution.py:25
  14.2 1.9 %collective-permute-start.1 = (bf16[192,1,256]{2,0,1:T(8,128)(2,1)S(1)}, bf16[192,1,256]{2,0,1:T(8,128)(2,1)S(1)}, u32[]{:S(2)}, u32[]{:S(2)}) collective-permute-start(bf16[192,1,256]{2,0,1:T(8,128)(2,1)S(1)} %get-tuple-element.6), channel_id=1, source_target_pairs={{1,0},{2,1},{3,2},{4,3},{5,4},{6,5},{7,6},{8,7},{9,8},{10,9},{11,1... | collective-permute-start | bytes 294920 | tf_op jit(solution)/shard_map/ppermute | solution.py:26
  16.2 4.1 %copy.24 = bf16[2,2,4,384,192]{3,0,4,2,1:T(2,128)(2,1)S(1)} copy(bf16[2,2,4,384,192]{3,4,2,1,0:T(8,128)(2,1)} %bitcast.22) | data formatting | bytes 4718592 | tf_op jit(solution)/shard_map/reshape | solution.py:123
  20.3 2.8 %reshape.14.wu_hbm = bf16[2,768,768]{2,1,0:T(8,128)(2,1)} reshape(bf16[2,4,192,2,384]{4,3,2,1,0:T(2,128)(2,1)S(1)} %bitcast.17) | data formatting | bytes 4718592 | tf_op jit(solution)/shard_map/reshape | solution.py:123
  23.1 2.5 %copy.18 = bf16[3,192,3,384]{3,2,1,0:T(4,128)(2,1)S(1)} copy(bf16[3,192,3,384]{3,1,0,2:T(8,128)(2,1)} %bitcast.23) | data formatting | bytes 2654208 | tf_op jit(solution)/shard_map/transpose | solution.py:124
  25.5 0.0 copy-start.4
  25.6 0.0 copy-start.1
  25.6 1.3 %copy.22 = bf16[72,8,3,384]{3,1,2,0:T(8,128)(2,1)} copy(bf16[72,8,3,384]{3,2,1,0:T(4,128)(2,1)S(1)} %bitcast.18) | data formatting | bytes 2654208
  26.9 0.1 copy.19.bu_ref
  27.0 0.1 copy.20.b3_ref
  27.1 0.1 add_convert_fusion.flags
  27.2 0.0 collective-permute-done
  27.2 0.0 collective-permute-done.1
  27.2 0.0 copy-done.1
  27.2 0.1 maximum_bitcast_fusion.sk_ref
  27.4 0.0 all-to-all-done.xw_ref
  27.4 10.1 %shard_map.64 = bf16[192,8,256]{2,1,0:T(8,128)(2,1)} custom-call(s32[2]{0:T(128)S(1)} %add_convert_fusion.flags, bf16[16,6,24,128]{3,2,1,0:T(8,128)(2,1)S(1)} %all-to-all-done.xw_ref, bf16[10,192,256]{2,1,0:T(8,128)(2,1)S(1)} %maximum_bitcast_fusion.sk_ref, bf16[2,768,768]{2,1,0:T(8,128)(2,1)} %reshape.14.wu_hbm, f32[192,1]{1,0:T(8,128)S(1)} %copy.19.bu_ref, ...), custom_call_target="tpu_custom_call" | custom-call | tf_op jit(solution)/shard_map/pallas_call | solution.py:101
  (8 shorter events, 0.1 us)
Async XLA Ops:
  1.3 8.4 %copy-start.2 = (bf16[192,8,256]{2,1,0:T(8,128)(2,1)S(1)}, bf16[192,8,256]{2,1,0:T(8,128)(2,1)}, u32[]{:S(2)}) copy-start(bf16[192,8,256]{2,1,0:T(8,128)(2,1)} %param.7) | copy-start | bytes 2359300
  2.3 25.1 %all-to-all-start = ((bf16[16,6,24,128]{3,2,1,0:T(8,128)(2,1)}), bf16[16,6,24,128]{3,2,1,0:T(8,128)(2,1)S(1)}, u32[]{:S(2)}, u32[]{:S(2)}) async-start(bf16[16,6,24,128]{3,2,1,0:T(8,128)(2,1)} %maximum_bitcast_fusion.1), calls=%async_computation | async-start | bytes 1179648 | tf_op jit(solution)/shard_map/all_to_all | solution.py:16
  9.8 0.9 %copy-start = (bf16[192,8,256]{2,0,1:T(8,128)(2,1)}, bf16[192,8,256]{2,0,1:T(8,128)(2,1)S(1)}, u32[]{:S(2)}) copy-start(bf16[192,8,256]{2,0,1:T(8,128)(2,1)S(1)} %copy.14) | copy-start | bytes 2359300
  10.7 16.5 %collective-permute-start = (bf16[192,1,256]{2,0,1:T(8,128)(2,1)S(1)}, bf16[192,1,256]{2,0,1:T(8,128)(2,1)S(1)}, u32[]{:S(2)}, u32[]{:S(2)}) collective-permute-start(bf16[192,1,256]{2,0,1:T(8,128)(2,1)S(1)} %get-tuple-element.5), channel_id=1, source_target_pairs={{0,1},{1,2},{2,3},{3,4},{4,5},{5,6},{6,7},{7,8},{8,9},{9,10},{10,1... | collective-permute-start | bytes 294920 | tf_op jit(solution)/shard_map/ppermute | solution.py:25
  14.2 13.0 %collective-permute-start.1 = (bf16[192,1,256]{2,0,1:T(8,128)(2,1)S(1)}, bf16[192,1,256]{2,0,1:T(8,128)(2,1)S(1)}, u32[]{:S(2)}, u32[]{:S(2)}) collective-permute-start(bf16[192,1,256]{2,0,1:T(8,128)(2,1)S(1)} %get-tuple-element.6), channel_id=1, source_target_pairs={{1,0},{2,1},{3,2},{4,3},{5,4},{6,5},{7,6},{8,7},{9,8},{10,9},{11,1... | collective-permute-start | bytes 294920 | tf_op jit(solution)/shard_map/ppermute | solution.py:26
  23.1 3.8 %copy-start.3 = (f32[192]{0:T(256)S(1)}, f32[192]{0:T(256)}, u32[]{:S(2)}) copy-start(f32[192]{0:T(256)} %param.9) | copy-start | bytes 2308
  25.5 1.5 %copy-start.4 = (f32[192]{0:T(256)S(1)}, f32[192]{0:T(256)}, u32[]{:S(2)}) copy-start(f32[192]{0:T(256)} %param.11) | copy-start | bytes 2308
  25.6 1.7 %copy-start.1 = (bf16[192,8,256]{2,0,1:T(8,128)(2,1)S(1)}, bf16[192,8,256]{2,0,1:T(8,128)(2,1)}, u32[]{:S(2)}) copy-start(bf16[192,8,256]{2,0,1:T(8,128)(2,1)} %copy-done) | copy-start | bytes 2359300

commit v9 on v8

--- a/solution.py
+++ b/solution.py
@@ -35,10 +35,15 @@
 
 
 def decoder_kernel(flags, xw_ref, sk_ref, wu_hbm, bu_ref, w3_hbm, b3_ref, out_ref, act_ref, wu_ref, w3_ref, sems):
-    loads = [pltpu.make_async_copy(wu_hbm.at[k], wu_ref.at[k], sems.at[k]) for k in range(2)]
-    loads.append(pltpu.make_async_copy(w3_hbm, w3_ref, sems.at[2]))
-    for load in loads:
-        load.start()
+    cin = wu_hbm.shape[2]
+
+    def load(src, dst, k):
+        copy = pltpu.make_async_copy(src, dst, sems.at[k])
+        copy.start()
+        return copy
+
+    up_loads = [[load(wu_hbm.at[p + 2 * h], wu_ref.at[p, :, pl.ds(h * cin, cin)], 2 * p + h) for h in range(2)] for p in range(2)]
+    conv_loads = [load(w3_hbm.at[ky], w3_ref.at[:, pl.ds(ky * cin, cin)], 4 + ky) for ky in range(3)]
     peers, nwin, groups, cw = xw_ref.shape
     nfine, cout, fw = sk_ref.shape
     nout = nfine - 2
@@ -58,7 +63,8 @@
     stacked = jnp.concatenate([wide[:, cw:], wide[:, :span]], axis=0)
     parity = []
     for p in range(2):
-        loads[p].wait()
+        for copy in up_loads[p]:
+            copy.wait()
         z = dot(wu_ref[p], stacked)
         taps = [z[k * cout : (k + 1) * cout] for k in range(4)]
         even = taps[1] + lane_shift(taps[3], cw, 1) + bu_ref[...]
@@ -81,7 +87,8 @@
             row = jnp.where(flags[1] == 1, 0.0, row)
         joined.append(jnp.concatenate([sk_ref[t], row.astype(jnp.bfloat16)], axis=0))
     field = jnp.concatenate(joined, axis=1)
-    loads[2].wait()
+    for copy in conv_loads:
+        copy.wait()
 
     rows = jnp.concatenate([field[:, ky * fw : (ky + nout) * fw] for ky in range(3)], axis=0)
     total = dot(w3_ref[...], rows)
@@ -105,9 +112,9 @@
         out_specs=vmem,
         scratch_shapes=[
             pltpu.VMEM((cout, nfine - 2, fw), jnp.float32),
-            pltpu.VMEM(wu.shape, wu.dtype),
-            pltpu.VMEM(w3.shape, w3.dtype),
-            pltpu.SemaphoreType.DMA((3,)),
+            pltpu.VMEM((2, wu.shape[1], 2 * wu.shape[2]), wu.dtype),
+            pltpu.VMEM((w3.shape[1], 3 * w3.shape[2]), w3.dtype),
+            pltpu.SemaphoreType.DMA((7,)),
         ],
         compiler_params=pltpu.CompilerParams(vmem_limit_bytes=48 * 1024 * 1024),
     )(flags, xw, sk, pltpu.with_memory_space_constraint(wu, pltpu.HBM), bu, pltpu.with_memory_space_constraint(w3, pltpu.HBM), b3)
@@ -120,8 +127,8 @@
     sk = skip_rows(skip_field, peers)
     xw = coarse_windows(coarse, peers)
     cout = up_weight.shape[3]
-    wu = jnp.transpose(up_weight.reshape(2, 2, 4, -1, cout), (1, 2, 4, 0, 3)).reshape(2, 4 * cout, -1)
-    w3 = jnp.transpose(conv_weight, (1, 3, 0, 2)).reshape(3 * cout, -1)
+    wu = jnp.transpose(up_weight, (0, 1, 3, 2)).reshape(4, 4 * cout, -1)
+    w3 = jnp.transpose(conv_weight, (0, 1, 3, 2)).reshape(3, 3 * cout, -1)
     return decode(flags, xw, sk, wu, up_bias[:, None], w3, conv_bias[:, None])
 
 

time: 37.8 us -> 35.6 us (0.942)
  the two profiles are of different devices: /device:TPU:1 before, /device:TPU:13 now
where the time goes in v9:
time: 35.6 us; the launch traced here: 35.1 us
  starting transfers between devices  11.8 us (33%)
  waiting for transfers between devices  10.3 us (29%)
  Pallas kernels  10.1 us (28%)
  local copies, waits for them, and re-layouts  1.78 us (5%)
  other arithmetic  1.07 us (3%)
    pallas_call x1, Pallas kernels, decode(): pl.pallas_call(decoder_kernel, out_shape=jax.ShapeDtypeStruct((cout, nfin...  10.1 us
    ppermute x1, waiting for transfers between devices, skip_rows(): before = lax.ppermute(skip[:, -1:], 'row', up)  8.59 us
    all_to_all x1, starting transfers between devices, coarse_windows(): gathered = lax.all_to_all(windows, 'row', 0, 0, tiled=True)  6.55 us
    ppermute x1, starting transfers between devices, skip_rows(): before = lax.ppermute(skip[:, -1:], 'row', up)  3.34 us
    ppermute x1, starting transfers between devices, skip_rows(): after = lax.ppermute(skip[:, :1], 'row', down)  1.92 us
    ppermute x1, waiting for transfers between devices, skip_rows(): after = lax.ppermute(skip[:, :1], 'row', down)  1.67 us
    unnamed x8, local copies, waits for them, and re-layouts  1.43 us
    transpose x1, other arithmetic, coarse_windows(): windows = jnp.transpose(windows, (1, 2, 0, 3))  0.87 us
  transfers between devices with their start and end apart: 3, of which 2 were waited for; matrix products, arithmetic and copies ran while one was open for 2% of the time, Pallas kernels for 0%

profile of v9, /device:TPU:13, one launch (start us, length us, event | category | flops | bytes accessed | tf_op | source)
XLA Modules:
  0.0 35.1 jit_solution(13473518917774555602)
XLA Ops:
  0.0 1.3 %copy.17 = bf16[24,64,128]{2,0,1:T(8,128)(2,1)S(1)} copy(bf16[24,64,128]{2,1,0:T(8,128)(2,1)} %param.6) | data formatting | bytes 786432
  1.3 0.0 copy-start
  1.4 0.0 copy-start.1
  1.4 0.0 copy-start.2
  1.4 0.9 %maximum_bitcast_fusion.1 = bf16[16,6,24,128]{3,2,1,0:T(8,128)(2,1)} fusion(bf16[24,16,2,128]{3,0,2,1:T(8,128)(2,1)S(1)} %slice.17, bf16[24,16,4,128]{3,0,2,1:T(8,128)(2,1)S(1)} %slice.16), kind=kLoop, calls=%fused_computation.1 | loop fusion | flops 294912 | bytes 1179648 | tf_op jit(solution)/shard_map/transpose | solution.py:15
  2.3 6.6 %all-to-all-start = ((bf16[16,6,24,128]{3,2,1,0:T(8,128)(2,1)}), bf16[16,6,24,128]{3,2,1,0:T(8,128)(2,1)S(1)}, u32[]{:S(2)}, u32[]{:S(2)}) async-start(bf16[16,6,24,128]{3,2,1,0:T(8,128)(2,1)} %maximum_bitcast_fusion.1), calls=%async_computation | async-start | bytes 1179648 | tf_op jit(solution)/shard_map/all_to_all | solution.py:16
  8.8 0.0 copy-done
  8.8 0.2 copy.12
  9.0 3.3 %collective-permute-start = (bf16[192,1,256]{2,0,1:T(8,128)(2,1)S(1)}, bf16[192,1,256]{2,0,1:T(8,128)(2,1)S(1)}, u32[]{:S(2)}, u32[]{:S(2)}) collective-permute-start(bf16[192,1,256]{2,0,1:T(8,128)(2,1)S(1)} %get-tuple-element.5), channel_id=1, source_target_pairs={{0,1},{1,2},{2,3},{3,4},{4,5},{5,6},{6,7},{7,8},{8,9},{9,10},{10,1... | collective-permute-start | bytes 294920 | tf_op jit(solution)/shard_map/ppermute | solution.py:25
  12.4 1.9 %collective-permute-start.1 = (bf16[192,1,256]{2,0,1:T(8,128)(2,1)S(1)}, bf16[192,1,256]{2,0,1:T(8,128)(2,1)S(1)}, u32[]{:S(2)}, u32[]{:S(2)}) collective-permute-start(bf16[192,1,256]{2,0,1:T(8,128)(2,1)S(1)} %get-tuple-element.6), channel_id=1, source_target_pairs={{1,0},{2,1},{3,2},{4,3},{5,4},{6,5},{7,6},{8,7},{9,8},{10,9},{11,1... | collective-permute-start | bytes 294920 | tf_op jit(solution)/shard_map/ppermute | solution.py:26
  14.3 0.0 copy-done.1
  14.3 0.1 copy.15.bu_ref
  14.5 0.0 copy-done.2
  14.5 0.1 copy.16.b3_ref
  14.6 0.1 add_convert_fusion.flags
  14.7 8.6 %collective-permute-done = bf16[192,1,256]{2,0,1:T(8,128)(2,1)S(1)} collective-permute-done((bf16[192,1,256]{2,0,1:T(8,128)(2,1)S(1)}, bf16[192,1,256]{2,0,1:T(8,128)(2,1)S(1)}, u32[]{:S(2)}, u32[]{:S(2)}) %collective-permute-start) | collective-permute-done | bytes 98336 | tf_op jit(solution)/shard_map/ppermute | solution.py:25
  23.2 1.7 %collective-permute-done.1 = bf16[192,1,256]{2,0,1:T(8,128)(2,1)S(1)} collective-permute-done((bf16[192,1,256]{2,0,1:T(8,128)(2,1)S(1)}, bf16[192,1,256]{2,0,1:T(8,128)(2,1)S(1)}, u32[]{:S(2)}, u32[]{:S(2)}) %collective-permute-start.1) | collective-permute-done | bytes 98336 | tf_op jit(solution)/shard_map/ppermute | solution.py:26
  24.9 0.1 maximum_bitcast_fusion.sk_ref
  25.0 0.0 all-to-all-done.xw_ref
  25.1 10.1 %shard_map.64 = bf16[192,8,256]{2,1,0:T(8,128)(2,1)} custom-call(s32[2]{0:T(128)S(1)} %add_convert_fusion.flags, bf16[16,6,24,128]{3,2,1,0:T(8,128)(2,1)S(1)} %all-to-all-done.xw_ref, bf16[10,192,256]{2,1,0:T(8,128)(2,1)S(1)} %maximum_bitcast_fusion.sk_ref, bf16[4,768,384]{2,1,0:T(8,128)(2,1)} %bitcast.17, f32[192,1]{1,0:T(8,128)S(1)} %copy.15.bu_ref, ...), custom_call_target="tpu_custom_call" | custom-call | tf_op jit(solution)/shard_map/pallas_call | solution.py:108
  (4 shorter events, 0.1 us)
Async XLA Ops:
  1.3 7.6 %copy-start = (bf16[192,8,256]{2,1,0:T(8,128)(2,1)S(1)}, bf16[192,8,256]{2,1,0:T(8,128)(2,1)}, u32[]{:S(2)}) copy-start(bf16[192,8,256]{2,1,0:T(8,128)(2,1)} %param.7) | copy-start | bytes 2359300
  1.4 13.0 %copy-start.1 = (f32[192]{0:T(256)S(1)}, f32[192]{0:T(256)}, u32[]{:S(2)}) copy-start(f32[192]{0:T(256)} %param.9) | copy-start | bytes 2308
  1.4 13.1 %copy-start.2 = (f32[192]{0:T(256)S(1)}, f32[192]{0:T(256)}, u32[]{:S(2)}) copy-start(f32[192]{0:T(256)} %param.11) | copy-start | bytes 2308
  2.3 22.8 %all-to-all-start = ((bf16[16,6,24,128]{3,2,1,0:T(8,128)(2,1)}), bf16[16,6,24,128]{3,2,1,0:T(8,128)(2,1)S(1)}, u32[]{:S(2)}, u32[]{:S(2)}) async-start(bf16[16,6,24,128]{3,2,1,0:T(8,128)(2,1)} %maximum_bitcast_fusion.1), calls=%async_computation | async-start | bytes 1179648 | tf_op jit(solution)/shard_map/all_to_all | solution.py:16
  9.0 14.2 %collective-permute-start = (bf16[192,1,256]{2,0,1:T(8,128)(2,1)S(1)}, bf16[192,1,256]{2,0,1:T(8,128)(2,1)S(1)}, u32[]{:S(2)}, u32[]{:S(2)}) collective-permute-start(bf16[192,1,256]{2,0,1:T(8,128)(2,1)S(1)} %get-tuple-element.5), channel_id=1, source_target_pairs={{0,1},{1,2},{2,3},{3,4},{4,5},{5,6},{6,7},{7,8},{8,9},{9,10},{10,1... | collective-permute-start | bytes 294920 | tf_op jit(solution)/shard_map/ppermute | solution.py:25
  12.4 12.5 %collective-permute-start.1 = (bf16[192,1,256]{2,0,1:T(8,128)(2,1)S(1)}, bf16[192,1,256]{2,0,1:T(8,128)(2,1)S(1)}, u32[]{:S(2)}, u32[]{:S(2)}) collective-permute-start(bf16[192,1,256]{2,0,1:T(8,128)(2,1)S(1)} %get-tuple-element.6), channel_id=1, source_target_pairs={{1,0},{2,1},{3,2},{4,3},{5,4},{6,5},{7,6},{8,7},{9,8},{10,9},{11,1... | collective-permute-start | bytes 294920 | tf_op jit(solution)/shard_map/ppermute | solution.py:26

commit v10 on v9

--- a/solution.py
+++ b/solution.py
@@ -34,7 +34,21 @@
     return jnp.where(lane == edge, 0.0, pltpu.roll(v, step % v.shape[1], 1))
 
 
-def decoder_kernel(flags, xw_ref, sk_ref, wu_hbm, bu_ref, w3_hbm, b3_ref, out_ref, act_ref, wu_ref, w3_ref, sems):
+def conv_rows(field, w, nout, fw):
+    rows = jnp.concatenate([field[:, ky * fw : (ky + nout) * fw] for ky in range(3)], axis=0)
+    total = jnp.dot(w, rows, preferred_element_type=jnp.float32)
+    cout = total.shape[0] // 3
+    mid = total[cout : 2 * cout]
+    return mid + lane_shift(total[:cout], fw, 1) + lane_shift(total[2 * cout :], fw, -1)
+
+
+def skip_kernel(sk_ref, w_ref, b_ref, out_ref):
+    nfine, _, fw = sk_ref.shape
+    field = jnp.concatenate([sk_ref[t] for t in range(nfine)], axis=1)
+    out_ref[...] = conv_rows(field, w_ref[...], nfine - 2, fw) + b_ref[...]
+
+
+def decoder_kernel(flags, xw_ref, part_hbm, wu_hbm, bu_ref, w3_hbm, out_ref, act_ref, part_ref, wu_ref, w3_ref, sems):
     cin = wu_hbm.shape[2]
 
     def load(src, dst, k):
@@ -43,10 +57,11 @@
         return copy
 
     up_loads = [[load(wu_hbm.at[p + 2 * h], wu_ref.at[p, :, pl.ds(h * cin, cin)], 2 * p + h) for h in range(2)] for p in range(2)]
-    conv_loads = [load(w3_hbm.at[ky], w3_ref.at[:, pl.ds(ky * cin, cin)], 4 + ky) for ky in range(3)]
+    conv_load = load(w3_hbm, w3_ref, 4)
+    part_load = load(part_hbm, part_ref, 5)
     peers, nwin, groups, cw = xw_ref.shape
-    nfine, cout, fw = sk_ref.shape
-    nout = nfine - 2
+    cout, nout, fw = out_ref.shape
+    nfine = nout + 2
     span = (nwin - 1) * cw
     f32 = jnp.float32
 
@@ -85,39 +100,53 @@
             row = jnp.where(flags[0] == 1, 0.0, row)
         if t == nfine - 1:
             row = jnp.where(flags[1] == 1, 0.0, row)
-        joined.append(jnp.concatenate([sk_ref[t], row.astype(jnp.bfloat16)], axis=0))
+        joined.append(row.astype(jnp.bfloat16))
     field = jnp.concatenate(joined, axis=1)
-    for copy in conv_loads:
-        copy.wait()
-
-    rows = jnp.concatenate([field[:, ky * fw : (ky + nout) * fw] for ky in range(3)], axis=0)
-    total = dot(w3_ref[...], rows)
-    pre = total[cout : 2 * cout]
-    pre = pre + lane_shift(total[:cout], fw, 1) + lane_shift(total[2 * cout :], fw, -1)
-    pre = pre + b3_ref[...]
+    conv_load.wait()
+    pre = conv_rows(field, w3_ref[...], nout, fw)
+    part_load.wait()
+    pre = pre + part_ref[...]
     act = pre / (1.0 + jnp.exp(-pre))
     for y in range(nout):
         act_ref[:, y, :] = act[:, y * fw : (y + 1) * fw]
     out_ref[...] = act_ref[...].astype(out_ref.dtype)
 
 
-def decode(flags, xw, sk, wu, bu, w3, b3):
+def skip_conv(sk, w3s, b3):
     nfine, cout, fw = sk.shape
+    nout = nfine - 2
+    vmem = pl.BlockSpec(memory_space=pltpu.VMEM)
+    flops = 2 * w3s.shape[0] * w3s.shape[1] * nout * fw
+    moved = sk.size * 2 + w3s.size * 2 + cout * nout * fw * 4
+    return pl.pallas_call(
+        skip_kernel,
+        out_shape=jax.ShapeDtypeStruct((cout, nout * fw), jnp.float32),
+        in_specs=[vmem] * 3,
+        out_specs=vmem,
+        compiler_params=pltpu.CompilerParams(vmem_limit_bytes=48 * 1024 * 1024),
+        cost_estimate=pl.CostEstimate(flops=flops, transcendentals=0, bytes_accessed=moved),
+    )(sk, w3s, b3)
+
+
+def decode(flags, xw, part, wu, bu, w3u, nout, fw):
+    cout = bu.shape[0]
     vmem = pl.BlockSpec(memory_space=pltpu.VMEM)
     hbm = pl.BlockSpec(memory_space=pltpu.HBM)
+    in_hbm = lambda x: pltpu.with_memory_space_constraint(x, pltpu.HBM)
     return pl.pallas_call(
         decoder_kernel,
-        out_shape=jax.ShapeDtypeStruct((cout, nfine - 2, fw), jnp.bfloat16),
-        in_specs=[pl.BlockSpec(memory_space=pltpu.SMEM), vmem, vmem, hbm, vmem, hbm, vmem],
+        out_shape=jax.ShapeDtypeStruct((cout, nout, fw), jnp.bfloat16),
+        in_specs=[pl.BlockSpec(memory_space=pltpu.SMEM), vmem, hbm, hbm, vmem, hbm],
         out_specs=vmem,
         scratch_shapes=[
-            pltpu.VMEM((cout, nfine - 2, fw), jnp.float32),
+            pltpu.VMEM((cout, nout, fw), jnp.float32),
+            pltpu.VMEM(part.shape, part.dtype),
             pltpu.VMEM((2, wu.shape[1], 2 * wu.shape[2]), wu.dtype),
-            pltpu.VMEM((w3.shape[1], 3 * w3.shape[2]), w3.dtype),
-            pltpu.SemaphoreType.DMA((7,)),
+            pltpu.VMEM(w3u.shape, w3u.dtype),
+            pltpu.SemaphoreType.DMA((6,)),
         ],
         compiler_params=pltpu.CompilerParams(vmem_limit_bytes=48 * 1024 * 1024),
-    )(flags, xw, sk, pltpu.with_memory_space_constraint(wu, pltpu.HBM), bu, pltpu.with_memory_space_constraint(w3, pltpu.HBM), b3)
+    )(flags, xw, in_hbm(part), in_hbm(wu), bu, in_hbm(w3u))
 
 
 def shards(coarse, skip_field, up_weight, up_bias, conv_weight, conv_bias):
@@ -128,8 +157,12 @@
     xw = coarse_windows(coarse, peers)
     cout = up_weight.shape[3]
     wu = jnp.transpose(up_weight, (0, 1, 3, 2)).reshape(4, 4 * cout, -1)
-    w3 = jnp.transpose(conv_weight, (0, 1, 3, 2)).reshape(3, 3 * cout, -1)
-    return decode(flags, xw, sk, wu, up_bias[:, None], w3, conv_bias[:, None])
+    skips = skip_field.shape[0]
+    halves = conv_weight.reshape(3, 3, 2, skips, cout)
+    w3 = jnp.transpose(halves, (2, 1, 4, 0, 3)).reshape(2, 3 * cout, 3 * skips)
+    part = skip_conv(sk, w3[0], conv_bias[:, None])
+    nout, fw = skip_field.shape[1], skip_field.shape[2]
+    return decode(flags, xw, part, wu, up_bias[:, None], w3[1], nout, fw)
 
 
 def solution(mesh):

time: 35.6 us -> 42.9 us (1.21)
  the two profiles are of different devices: /device:TPU:13 before, /device:TPU:1 now
where the time goes in v10:
time: 42.9 us; the launch traced here: 42.5 us
  local copies, waits for them, and re-layouts  15.8 us (37%)
  starting transfers between devices  12.8 us (30%)
  Pallas kernels  11.6 us (27%)
  other arithmetic  2.01 us (5%)
    pallas_call x1, Pallas kernels, decode(): pl.pallas_call(decoder_kernel, out_shape=jax.ShapeDtypeStruct((cout, nout...  9.44 us
    all_to_all x1, starting transfers between devices, coarse_windows(): gathered = lax.all_to_all(windows, 'row', 0, 0, tiled=True)  7.35 us
    reshape x2, local copies, waits for them, and re-layouts, shards(): halves = conv_weight.reshape(3, 3, 2, skips, cout)  6 us
    ppermute x1, starting transfers between devices, skip_rows(): before = lax.ppermute(skip[:, -1:], 'row', up)  3.53 us
    squeeze x1, local copies, waits for them, and re-layouts, shards(): part = skip_conv(sk, w3[0], conv_bias[:, None])  2.75 us
    unnamed x10, local copies, waits for them, and re-layouts  2.56 us
    pallas_call x1, Pallas kernels, skip_conv(): pl.pallas_call(skip_kernel, out_shape=jax.ShapeDtypeStruct((cout, nout *...  2.13 us
    ppermute x1, starting transfers between devices, skip_rows(): after = lax.ppermute(skip[:, :1], 'row', down)  1.92 us
  transfers between devices with their start and end apart: 3, of which 0 were waited for; matrix products, arithmetic and copies ran while one was open for 34% of the time, Pallas kernels for 5%

profile of v10, /device:TPU:1, one launch (start us, length us, event | category | flops | bytes accessed | tf_op | source)
XLA Modules:
  0.0 42.5 jit_solution(3784045749807093261)
XLA Ops:
  0.0 1.3 %copy.19 = bf16[24,64,128]{2,0,1:T(8,128)(2,1)S(1)} copy(bf16[24,64,128]{2,1,0:T(8,128)(2,1)} %param.6) | data formatting | bytes 786432
  1.3 0.0 copy-start.1
  1.4 0.9 %maximum_bitcast_fusion.1 = bf16[16,6,24,128]{3,2,1,0:T(8,128)(2,1)} fusion(bf16[24,16,2,128]{3,0,2,1:T(8,128)(2,1)S(1)} %slice.27, bf16[24,16,4,128]{3,0,2,1:T(8,128)(2,1)S(1)} %slice.26), kind=kLoop, calls=%fused_computation.2 | loop fusion | flops 294912 | bytes 1179648 | tf_op jit(solution)/shard_map/transpose | solution.py:15
  2.3 7.3 %all-to-all-start = ((bf16[16,6,24,128]{3,2,1,0:T(8,128)(2,1)}), bf16[16,6,24,128]{3,2,1,0:T(8,128)(2,1)S(1)}, u32[]{:S(2)}, u32[]{:S(2)}) async-start(bf16[16,6,24,128]{3,2,1,0:T(8,128)(2,1)} %maximum_bitcast_fusion.1), calls=%async_computation | async-start | bytes 1179648 | tf_op jit(solution)/shard_map/all_to_all | solution.py:16
  9.6 0.0 copy-done.1
  9.6 0.2 copy.13
  9.8 0.7 %fusion.1 = (bf16[192,1,256]{2,0,1:T(8,128)(2,1)}, bf16[192,1,256]{2,0,1:T(8,128)(2,1)S(1)}) fusion(bf16[192,8,256]{2,0,1:T(8,128)(2,1)S(1)} %copy.13), kind=kLoop, calls=%fused_computation.5 | loop fusion | bytes 393216 | tf_op jit(solution)/shard_map/slice | solution.py:25
  10.4 3.5 %collective-permute-start = (bf16[192,1,256]{2,0,1:T(8,128)(2,1)}, bf16[192,1,256]{2,0,1:T(8,128)(2,1)}, u32[]{:S(2)}, u32[]{:S(2)}) collective-permute-start(bf16[192,1,256]{2,0,1:T(8,128)(2,1)} %get-tuple-element.7), channel_id=1, source_target_pairs={{0,1},{1,2},{2,3},{3,4},{4,5},{5,6},{6,7},{7,8},{8,9},{9,10},{10,1... | collective-permute-start | bytes 294920 | tf_op jit(solution)/shard_map/ppermute | solution.py:25
  14.0 1.9 %collective-permute-start.1 = (bf16[192,1,256]{2,0,1:T(8,128)(2,1)S(1)}, bf16[192,1,256]{2,0,1:T(8,128)(2,1)}, u32[]{:S(2)}, u32[]{:S(2)}) collective-permute-start(bf16[192,1,256]{2,0,1:T(8,128)(2,1)S(1)} %get-tuple-element.8), channel_id=1, source_target_pairs={{1,0},{2,1},{3,2},{4,3},{5,4},{6,5},{7,6},{8,7},{9,8},{10,9},{11,1... | collective-permute-start | bytes 294920 | tf_op jit(solution)/shard_map/ppermute | solution.py:26
  15.9 4.5 %reshape.15 = bf16[3,3,2,192,192]{3,2,4,1,0:T(2,128)(2,1)S(1)} reshape(bf16[3,3,384,192]{2,3,1,0:T(8,128)(2,1)} %param.10) | data formatting | bytes 2654208 | tf_op jit(solution)/shard_map/reshape | solution.py:161
  20.4 1.5 %copy.21 = bf16[3,3,2,192,192]{3,0,4,1,2:T(4,128)(2,1)S(1)} copy(bf16[3,3,2,192,192]{3,2,4,1,0:T(2,128)(2,1)S(1)} %reshape.15) | data formatting | bytes 2654208 | tf_op jit(solution)/shard_map/reshape | solution.py:161
  21.9 1.8 %fusion = (bf16[1,3,192,3,192]{4,3,2,1,0:T(4,128)(2,1)S(1)}, bf16[1,3,192,3,192]{4,3,2,1,0:T(4,128)(2,1)}) fusion(bf16[2,3,192,3,192]{4,3,2,1,0:T(4,128)(2,1)S(1)} %bitcast.19), kind=kLoop, calls=%fused_computation.4 | loop fusion | bytes 2654208 | tf_op jit(solution)/shard_map/slice | solution.py:165
  23.8 2.7 %squeeze.6.w_ref = bf16[576,576]{1,0:T(8,128)(2,1)S(1)} reshape(bf16[1,3,192,3,192]{4,3,2,1,0:T(4,128)(2,1)} %get-tuple-element.6) | data formatting | bytes 1327104 | tf_op jit(solution)/shard_map/squeeze | solution.py:163
  26.5 0.1 copy.17.b_ref
  26.7 1.7 %squeeze.7.w3_hbm = bf16[576,576]{1,0:T(8,128)(2,1)} reshape(bf16[1,3,192,3,192]{4,3,2,1,0:T(4,128)(2,1)S(1)} %get-tuple-element.5) | data formatting | bytes 1327104 | tf_op jit(solution)/shard_map/squeeze | solution.py:165
  28.3 0.1 copy.18.bu_ref
  28.5 0.1 add_convert_fusion.flags
  28.5 0.0 collective-permute-done
  28.5 0.0 collective-permute-done.1
  28.5 1.1 %maximum_bitcast_fusion.sk_ref = bf16[10,192,256]{2,1,0:T(8,128)(2,1)S(1)} fusion(bf16[192,1,256]{2,0,1:T(8,128)(2,1)} %collective-permute-done.1, bf16[192,8,256]{2,0,1:T(8,128)(2,1)S(1)} %copy.13, bf16[192,1,256]{2,0,1:T(8,128)(2,1)} %collective-permute-done), kind=kLoop, calls=%fused_computation.1 | loop fusion | flops 983040 | bytes 1966080 | tf_op jit(solution)/shard_map/transpose | solution.py:28
  29.6 2.1 %shard_map.64.part_hbm = f32[192,2048]{1,0:T(8,128)S(1)} custom-call(bf16[10,192,256]{2,1,0:T(8,128)(2,1)S(1)} %maximum_bitcast_fusion.sk_ref, bf16[576,576]{1,0:T(8,128)(2,1)S(1)} %squeeze.6.w_ref, f32[192,1]{1,0:T(8,128)S(1)} %copy.17.b_ref), custom_call_target="tpu_custom_call" | custom-call | flops 1358954496 | bytes 3219456 | tf_op jit(solution)/shard_map/pallas_call | solution.py:121
  31.8 1.1 %copy-done = f32[192,2048]{1,0:T(8,128)} copy-done((f32[192,2048]{1,0:T(8,128)}, f32[192,2048]{1,0:T(8,128)S(1)}, u32[]{:S(2)}) %copy-start) | copy-done | bytes 1572888
  32.9 0.0 all-to-all-done.xw_ref
  32.9 9.4 %shard_map.65 = bf16[192,8,256]{2,1,0:T(8,128)(2,1)} custom-call(s32[2]{0:T(128)S(1)} %add_convert_fusion.flags, bf16[16,6,24,128]{3,2,1,0:T(8,128)(2,1)S(1)} %all-to-all-done.xw_ref, f32[192,2048]{1,0:T(8,128)} %copy-done, bf16[4,768,384]{2,1,0:T(8,128)(2,1)} %bitcast.22, f32[192,1]{1,0:T(8,128)S(1)} %copy.18.bu_ref, bf16[576,576]{1,0:T(8,128)(2,1)} %squeeze.7.w3_hbm), custom_call_target="tpu_custom_call" | custom-call | tf_op jit(solution)/shard_map/pallas_call | solution.py:136
  (8 shorter events, 0.1 us)
Async XLA Ops:
  1.3 8.3 %copy-start.1 = (bf16[192,8,256]{2,1,0:T(8,128)(2,1)S(1)}, bf16[192,8,256]{2,1,0:T(8,128)(2,1)}, u32[]{:S(2)}) copy-start(bf16[192,8,256]{2,1,0:T(8,128)(2,1)} %param.7) | copy-start | bytes 2359300
  2.3 30.6 %all-to-all-start = ((bf16[16,6,24,128]{3,2,1,0:T(8,128)(2,1)}), bf16[16,6,24,128]{3,2,1,0:T(8,128)(2,1)S(1)}, u32[]{:S(2)}, u32[]{:S(2)}) async-start(bf16[16,6,24,128]{3,2,1,0:T(8,128)(2,1)} %maximum_bitcast_fusion.1), calls=%async_computation | async-start | bytes 1179648 | tf_op jit(solution)/shard_map/all_to_all | solution.py:16
  10.4 18.1 %collective-permute-start = (bf16[192,1,256]{2,0,1:T(8,128)(2,1)}, bf16[192,1,256]{2,0,1:T(8,128)(2,1)}, u32[]{:S(2)}, u32[]{:S(2)}) collective-permute-start(bf16[192,1,256]{2,0,1:T(8,128)(2,1)} %get-tuple-element.7), channel_id=1, source_target_pairs={{0,1},{1,2},{2,3},{3,4},{4,5},{5,6},{6,7},{7,8},{8,9},{9,10},{10,1... | collective-permute-start | bytes 294920 | tf_op jit(solution)/shard_map/ppermute | solution.py:25
  14.0 14.6 %collective-permute-start.1 = (bf16[192,1,256]{2,0,1:T(8,128)(2,1)S(1)}, bf16[192,1,256]{2,0,1:T(8,128)(2,1)}, u32[]{:S(2)}, u32[]{:S(2)}) collective-permute-start(bf16[192,1,256]{2,0,1:T(8,128)(2,1)S(1)} %get-tuple-element.8), channel_id=1, source_target_pairs={{1,0},{2,1},{3,2},{4,3},{5,4},{6,5},{7,6},{8,7},{9,8},{10,9},{11,1... | collective-permute-start | bytes 294920 | tf_op jit(solution)/shard_map/ppermute | solution.py:26
  23.8 2.8 %copy-start.2 = (f32[192]{0:T(256)S(1)}, f32[192]{0:T(256)}, u32[]{:S(2)}) copy-start(f32[192]{0:T(256)} %param.11) | copy-start | bytes 2308
  23.8 4.6 %copy-start.3 = (f32[192]{0:T(256)S(1)}, f32[192]{0:T(256)}, u32[]{:S(2)}) copy-start(f32[192]{0:T(256)} %param.9) | copy-start | bytes 2308
  31.7 1.1 %copy-start = (f32[192,2048]{1,0:T(8,128)}, f32[192,2048]{1,0:T(8,128)S(1)}, u32[]{:S(2)}) copy-start(f32[192,2048]{1,0:T(8,128)S(1)} %shard_map.64.part_hbm) | copy-start | bytes 4718596

commit v11 on v9

--- a/solution.py
+++ b/solution.py
@@ -75,12 +75,14 @@
     pos = lax.broadcasted_iota(jnp.int32, (cw, fw), 1)
     put_even = (pos == 2 * col).astype(jnp.bfloat16)
     put_odd = (pos == 2 * col + 1).astype(jnp.bfloat16)
+    put = jnp.concatenate([put_even, put_odd], axis=0)
 
     joined = []
     for t in range(nfine):
         even, odd = parity[t % 2]
         q = t // 2
-        row = dot(even[:, q * cw : (q + 1) * cw], put_even) + dot(odd[:, q * cw : (q + 1) * cw], put_odd)
+        pair = jnp.concatenate([even[:, q * cw : (q + 1) * cw], odd[:, q * cw : (q + 1) * cw]], axis=1)
+        row = dot(pair, put)
         if t == 0:
             row = jnp.where(flags[0] == 1, 0.0, row)
         if t == nfine - 1:

time: 35.6 us -> 35.4 us (level)
  no operation moved by 1% of the time
where the time goes in v11:
time: 35.4 us; the launch traced here: 34.9 us
  starting transfers between devices  11.8 us (33%)
  waiting for transfers between devices  10.3 us (29%)
  Pallas kernels  9.88 us (28%)
  local copies, waits for them, and re-layouts  1.78 us (5%)
  other arithmetic  1.07 us (3%)
    pallas_call x1, Pallas kernels, decode(): pl.pallas_call(decoder_kernel, out_shape=jax.ShapeDtypeStruct((cout, nfin...  9.88 us
    ppermute x1, waiting for transfers between devices, skip_rows(): before = lax.ppermute(skip[:, -1:], 'row', up)  8.59 us
    all_to_all x1, starting transfers between devices, coarse_windows(): gathered = lax.all_to_all(windows, 'row', 0, 0, tiled=True)  6.55 us
    ppermute x1, starting transfers between devices, skip_rows(): before = lax.ppermute(skip[:, -1:], 'row', up)  3.34 us
    ppermute x1, starting transfers between devices, skip_rows(): after = lax.ppermute(skip[:, :1], 'row', down)  1.92 us
    ppermute x1, waiting for transfers between devices, skip_rows(): after = lax.ppermute(skip[:, :1], 'row', down)  1.67 us
    unnamed x8, local copies, waits for them, and re-layouts  1.43 us
    transpose x1, other arithmetic, coarse_windows(): windows = jnp.transpose(windows, (1, 2, 0, 3))  0.87 us
  transfers between devices with their start and end apart: 3, of which 2 were waited for; matrix products, arithmetic and copies ran while one was open for 2% of the time, Pallas kernels for 0%

profile of v11, /device:TPU:13, one launch (start us, length us, event | category | flops | bytes accessed | tf_op | source)
XLA Modules:
  0.0 34.9 jit_solution(10452331405595877893)
XLA Ops:
  0.0 1.3 %copy.17 = bf16[24,64,128]{2,0,1:T(8,128)(2,1)S(1)} copy(bf16[24,64,128]{2,1,0:T(8,128)(2,1)} %param.6) | data formatting | bytes 786432
  1.3 0.0 copy-start
  1.4 0.0 copy-start.1
  1.4 0.0 copy-start.2
  1.4 0.9 %maximum_bitcast_fusion.1 = bf16[16,6,24,128]{3,2,1,0:T(8,128)(2,1)} fusion(bf16[24,16,2,128]{3,0,2,1:T(8,128)(2,1)S(1)} %slice.17, bf16[24,16,4,128]{3,0,2,1:T(8,128)(2,1)S(1)} %slice.16), kind=kLoop, calls=%fused_computation.1 | loop fusion | flops 294912 | bytes 1179648 | tf_op jit(solution)/shard_map/transpose | solution.py:15
  2.3 6.6 %all-to-all-start = ((bf16[16,6,24,128]{3,2,1,0:T(8,128)(2,1)}), bf16[16,6,24,128]{3,2,1,0:T(8,128)(2,1)S(1)}, u32[]{:S(2)}, u32[]{:S(2)}) async-start(bf16[16,6,24,128]{3,2,1,0:T(8,128)(2,1)} %maximum_bitcast_fusion.1), calls=%async_computation | async-start | bytes 1179648 | tf_op jit(solution)/shard_map/all_to_all | solution.py:16
  8.8 0.0 copy-done
  8.8 0.2 copy.12
  9.0 3.3 %collective-permute-start = (bf16[192,1,256]{2,0,1:T(8,128)(2,1)S(1)}, bf16[192,1,256]{2,0,1:T(8,128)(2,1)S(1)}, u32[]{:S(2)}, u32[]{:S(2)}) collective-permute-start(bf16[192,1,256]{2,0,1:T(8,128)(2,1)S(1)} %get-tuple-element.5), channel_id=1, source_target_pairs={{0,1},{1,2},{2,3},{3,4},{4,5},{5,6},{6,7},{7,8},{8,9},{9,10},{10,1... | collective-permute-start | bytes 294920 | tf_op jit(solution)/shard_map/ppermute | solution.py:25
  12.4 1.9 %collective-permute-start.1 = (bf16[192,1,256]{2,0,1:T(8,128)(2,1)S(1)}, bf16[192,1,256]{2,0,1:T(8,128)(2,1)S(1)}, u32[]{:S(2)}, u32[]{:S(2)}) collective-permute-start(bf16[192,1,256]{2,0,1:T(8,128)(2,1)S(1)} %get-tuple-element.6), channel_id=1, source_target_pairs={{1,0},{2,1},{3,2},{4,3},{5,4},{6,5},{7,6},{8,7},{9,8},{10,9},{11,1... | collective-permute-start | bytes 294920 | tf_op jit(solution)/shard_map/ppermute | solution.py:26
  14.3 0.0 copy-done.1
  14.3 0.1 copy.15.bu_ref
  14.5 0.0 copy-done.2
  14.5 0.1 copy.16.b3_ref
  14.6 0.1 add_convert_fusion.flags
  14.7 8.6 %collective-permute-done = bf16[192,1,256]{2,0,1:T(8,128)(2,1)S(1)} collective-permute-done((bf16[192,1,256]{2,0,1:T(8,128)(2,1)S(1)}, bf16[192,1,256]{2,0,1:T(8,128)(2,1)S(1)}, u32[]{:S(2)}, u32[]{:S(2)}) %collective-permute-start) | collective-permute-done | bytes 98336 | tf_op jit(solution)/shard_map/ppermute | solution.py:25
  23.2 1.7 %collective-permute-done.1 = bf16[192,1,256]{2,0,1:T(8,128)(2,1)S(1)} collective-permute-done((bf16[192,1,256]{2,0,1:T(8,128)(2,1)S(1)}, bf16[192,1,256]{2,0,1:T(8,128)(2,1)S(1)}, u32[]{:S(2)}, u32[]{:S(2)}) %collective-permute-start.1) | collective-permute-done | bytes 98336 | tf_op jit(solution)/shard_map/ppermute | solution.py:26
  24.9 0.1 maximum_bitcast_fusion.sk_ref
  25.0 0.0 all-to-all-done.xw_ref
  25.1 9.9 %shard_map.64 = bf16[192,8,256]{2,1,0:T(8,128)(2,1)} custom-call(s32[2]{0:T(128)S(1)} %add_convert_fusion.flags, bf16[16,6,24,128]{3,2,1,0:T(8,128)(2,1)S(1)} %all-to-all-done.xw_ref, bf16[10,192,256]{2,1,0:T(8,128)(2,1)S(1)} %maximum_bitcast_fusion.sk_ref, bf16[4,768,384]{2,1,0:T(8,128)(2,1)} %bitcast.17, f32[192,1]{1,0:T(8,128)S(1)} %copy.15.bu_ref, ...), custom_call_target="tpu_custom_call" | custom-call | tf_op jit(solution)/shard_map/pallas_call | solution.py:110
  (4 shorter events, 0.1 us)
Async XLA Ops:
  1.3 7.6 %copy-start = (bf16[192,8,256]{2,1,0:T(8,128)(2,1)S(1)}, bf16[192,8,256]{2,1,0:T(8,128)(2,1)}, u32[]{:S(2)}) copy-start(bf16[192,8,256]{2,1,0:T(8,128)(2,1)} %param.7) | copy-start | bytes 2359300
  1.4 13.0 %copy-start.1 = (f32[192]{0:T(256)S(1)}, f32[192]{0:T(256)}, u32[]{:S(2)}) copy-start(f32[192]{0:T(256)} %param.9) | copy-start | bytes 2308
  1.4 13.1 %copy-start.2 = (f32[192]{0:T(256)S(1)}, f32[192]{0:T(256)}, u32[]{:S(2)}) copy-start(f32[192]{0:T(256)} %param.11) | copy-start | bytes 2308
  2.3 22.8 %all-to-all-start = ((bf16[16,6,24,128]{3,2,1,0:T(8,128)(2,1)}), bf16[16,6,24,128]{3,2,1,0:T(8,128)(2,1)S(1)}, u32[]{:S(2)}, u32[]{:S(2)}) async-start(bf16[16,6,24,128]{3,2,1,0:T(8,128)(2,1)} %maximum_bitcast_fusion.1), calls=%async_computation | async-start | bytes 1179648 | tf_op jit(solution)/shard_map/all_to_all | solution.py:16
  9.0 14.2 %collective-permute-start = (bf16[192,1,256]{2,0,1:T(8,128)(2,1)S(1)}, bf16[192,1,256]{2,0,1:T(8,128)(2,1)S(1)}, u32[]{:S(2)}, u32[]{:S(2)}) collective-permute-start(bf16[192,1,256]{2,0,1:T(8,128)(2,1)S(1)} %get-tuple-element.5), channel_id=1, source_target_pairs={{0,1},{1,2},{2,3},{3,4},{4,5},{5,6},{6,7},{7,8},{8,9},{9,10},{10,1... | collective-permute-start | bytes 294920 | tf_op jit(solution)/shard_map/ppermute | solution.py:25
  12.4 12.5 %collective-permute-start.1 = (bf16[192,1,256]{2,0,1:T(8,128)(2,1)S(1)}, bf16[192,1,256]{2,0,1:T(8,128)(2,1)S(1)}, u32[]{:S(2)}, u32[]{:S(2)}) collective-permute-start(bf16[192,1,256]{2,0,1:T(8,128)(2,1)S(1)} %get-tuple-element.6), channel_id=1, source_target_pairs={{1,0},{2,1},{3,2},{4,3},{5,4},{6,5},{7,6},{8,7},{9,8},{10,9},{11,1... | collective-permute-start | bytes 294920 | tf_op jit(solution)/shard_map/ppermute | solution.py:26

commit v12 on v11

--- a/solution.py
+++ b/solution.py
@@ -29,7 +29,8 @@
 
 
 def lane_shift(v, period, step):
-    lane = lax.broadcasted_iota(jnp.int32, v.shape, 1) % period
+    lane = lax.broadcasted_iota(jnp.int32, v.shape, 1)
+    lane = lane & (period - 1) if period & (period - 1) == 0 else lane % period
     edge = 0 if step > 0 else period - 1
     return jnp.where(lane == edge, 0.0, pltpu.roll(v, step % v.shape[1], 1))
 

time: 35.4 us -> 35.4 us (level)
  no operation moved by 1% of the time
where the time goes in v12:
time: 35.4 us; the launch traced here: 34.9 us
  starting transfers between devices  11.8 us (33%)
  waiting for transfers between devices  10.3 us (29%)
  Pallas kernels  9.88 us (28%)
  local copies, waits for them, and re-layouts  1.78 us (5%)
  other arithmetic  1.07 us (3%)
    pallas_call x1, Pallas kernels, decode(): pl.pallas_call(decoder_kernel, out_shape=jax.ShapeDtypeStruct((cout, nfin...  9.88 us
    ppermute x1, waiting for transfers between devices, skip_rows(): before = lax.ppermute(skip[:, -1:], 'row', up)  8.59 us
    all_to_all x1, starting transfers between devices, coarse_windows(): gathered = lax.all_to_all(windows, 'row', 0, 0, tiled=True)  6.55 us
    ppermute x1, starting transfers between devices, skip_rows(): before = lax.ppermute(skip[:, -1:], 'row', up)  3.34 us
    ppermute x1, starting transfers between devices, skip_rows(): after = lax.ppermute(skip[:, :1], 'row', down)  1.92 us
    ppermute x1, waiting for transfers between devices, skip_rows(): after = lax.ppermute(skip[:, :1], 'row', down)  1.67 us
    unnamed x8, local copies, waits for them, and re-layouts  1.43 us
    transpose x1, other arithmetic, coarse_windows(): windows = jnp.transpose(windows, (1, 2, 0, 3))  0.87 us
  transfers between devices with their start and end apart: 3, of which 2 were waited for; matrix products, arithmetic and copies ran while one was open for 2% of the time, Pallas kernels for 0%

profile of v12, /device:TPU:13, one launch (start us, length us, event | category | flops | bytes accessed | tf_op | source)
XLA Modules:
  0.0 34.9 jit_solution(10452331405595877893)
XLA Ops:
  0.0 1.3 %copy.17 = bf16[24,64,128]{2,0,1:T(8,128)(2,1)S(1)} copy(bf16[24,64,128]{2,1,0:T(8,128)(2,1)} %param.6) | data formatting | bytes 786432
  1.3 0.0 copy-start
  1.4 0.0 copy-start.1
  1.4 0.0 copy-start.2
  1.4 0.9 %maximum_bitcast_fusion.1 = bf16[16,6,24,128]{3,2,1,0:T(8,128)(2,1)} fusion(bf16[24,16,2,128]{3,0,2,1:T(8,128)(2,1)S(1)} %slice.17, bf16[24,16,4,128]{3,0,2,1:T(8,128)(2,1)S(1)} %slice.16), kind=kLoop, calls=%fused_computation.1 | loop fusion | flops 294912 | bytes 1179648 | tf_op jit(solution)/shard_map/transpose | solution.py:15
  2.3 6.6 %all-to-all-start = ((bf16[16,6,24,128]{3,2,1,0:T(8,128)(2,1)}), bf16[16,6,24,128]{3,2,1,0:T(8,128)(2,1)S(1)}, u32[]{:S(2)}, u32[]{:S(2)}) async-start(bf16[16,6,24,128]{3,2,1,0:T(8,128)(2,1)} %maximum_bitcast_fusion.1), calls=%async_computation | async-start | bytes 1179648 | tf_op jit(solution)/shard_map/all_to_all | solution.py:16
  8.8 0.0 copy-done
  8.8 0.2 copy.12
  9.0 3.3 %collective-permute-start = (bf16[192,1,256]{2,0,1:T(8,128)(2,1)S(1)}, bf16[192,1,256]{2,0,1:T(8,128)(2,1)S(1)}, u32[]{:S(2)}, u32[]{:S(2)}) collective-permute-start(bf16[192,1,256]{2,0,1:T(8,128)(2,1)S(1)} %get-tuple-element.5), channel_id=1, source_target_pairs={{0,1},{1,2},{2,3},{3,4},{4,5},{5,6},{6,7},{7,8},{8,9},{9,10},{10,1... | collective-permute-start | bytes 294920 | tf_op jit(solution)/shard_map/ppermute | solution.py:25
  12.4 1.9 %collective-permute-start.1 = (bf16[192,1,256]{2,0,1:T(8,128)(2,1)S(1)}, bf16[192,1,256]{2,0,1:T(8,128)(2,1)S(1)}, u32[]{:S(2)}, u32[]{:S(2)}) collective-permute-start(bf16[192,1,256]{2,0,1:T(8,128)(2,1)S(1)} %get-tuple-element.6), channel_id=1, source_target_pairs={{1,0},{2,1},{3,2},{4,3},{5,4},{6,5},{7,6},{8,7},{9,8},{10,9},{11,1... | collective-permute-start | bytes 294920 | tf_op jit(solution)/shard_map/ppermute | solution.py:26
  14.3 0.0 copy-done.1
  14.3 0.1 copy.15.bu_ref
  14.5 0.0 copy-done.2
  14.5 0.1 copy.16.b3_ref
  14.6 0.1 add_convert_fusion.flags
  14.7 8.6 %collective-permute-done = bf16[192,1,256]{2,0,1:T(8,128)(2,1)S(1)} collective-permute-done((bf16[192,1,256]{2,0,1:T(8,128)(2,1)S(1)}, bf16[192,1,256]{2,0,1:T(8,128)(2,1)S(1)}, u32[]{:S(2)}, u32[]{:S(2)}) %collective-permute-start) | collective-permute-done | bytes 98336 | tf_op jit(solution)/shard_map/ppermute | solution.py:25
  23.2 1.7 %collective-permute-done.1 = bf16[192,1,256]{2,0,1:T(8,128)(2,1)S(1)} collective-permute-done((bf16[192,1,256]{2,0,1:T(8,128)(2,1)S(1)}, bf16[192,1,256]{2,0,1:T(8,128)(2,1)S(1)}, u32[]{:S(2)}, u32[]{:S(2)}) %collective-permute-start.1) | collective-permute-done | bytes 98336 | tf_op jit(solution)/shard_map/ppermute | solution.py:26
  24.9 0.1 maximum_bitcast_fusion.sk_ref
  25.0 0.0 all-to-all-done.xw_ref
  25.1 9.9 %shard_map.64 = bf16[192,8,256]{2,1,0:T(8,128)(2,1)} custom-call(s32[2]{0:T(128)S(1)} %add_convert_fusion.flags, bf16[16,6,24,128]{3,2,1,0:T(8,128)(2,1)S(1)} %all-to-all-done.xw_ref, bf16[10,192,256]{2,1,0:T(8,128)(2,1)S(1)} %maximum_bitcast_fusion.sk_ref, bf16[4,768,384]{2,1,0:T(8,128)(2,1)} %bitcast.17, f32[192,1]{1,0:T(8,128)S(1)} %copy.15.bu_ref, ...), custom_call_target="tpu_custom_call" | custom-call | tf_op jit(solution)/shard_map/pallas_call | solution.py:111
  (4 shorter events, 0.1 us)
Async XLA Ops:
  1.3 7.6 %copy-start = (bf16[192,8,256]{2,1,0:T(8,128)(2,1)S(1)}, bf16[192,8,256]{2,1,0:T(8,128)(2,1)}, u32[]{:S(2)}) copy-start(bf16[192,8,256]{2,1,0:T(8,128)(2,1)} %param.7) | copy-start | bytes 2359300
  1.4 13.0 %copy-start.1 = (f32[192]{0:T(256)S(1)}, f32[192]{0:T(256)}, u32[]{:S(2)}) copy-start(f32[192]{0:T(256)} %param.9) | copy-start | bytes 2308
  1.4 13.1 %copy-start.2 = (f32[192]{0:T(256)S(1)}, f32[192]{0:T(256)}, u32[]{:S(2)}) copy-start(f32[192]{0:T(256)} %param.11) | copy-start | bytes 2308
  2.3 22.8 %all-to-all-start = ((bf16[16,6,24,128]{3,2,1,0:T(8,128)(2,1)}), bf16[16,6,24,128]{3,2,1,0:T(8,128)(2,1)S(1)}, u32[]{:S(2)}, u32[]{:S(2)}) async-start(bf16[16,6,24,128]{3,2,1,0:T(8,128)(2,1)} %maximum_bitcast_fusion.1), calls=%async_computation | async-start | bytes 1179648 | tf_op jit(solution)/shard_map/all_to_all | solution.py:16
  9.0 14.2 %collective-permute-start = (bf16[192,1,256]{2,0,1:T(8,128)(2,1)S(1)}, bf16[192,1,256]{2,0,1:T(8,128)(2,1)S(1)}, u32[]{:S(2)}, u32[]{:S(2)}) collective-permute-start(bf16[192,1,256]{2,0,1:T(8,128)(2,1)S(1)} %get-tuple-element.5), channel_id=1, source_target_pairs={{0,1},{1,2},{2,3},{3,4},{4,5},{5,6},{6,7},{7,8},{8,9},{9,10},{10,1... | collective-permute-start | bytes 294920 | tf_op jit(solution)/shard_map/ppermute | solution.py:25
  12.4 12.5 %collective-permute-start.1 = (bf16[192,1,256]{2,0,1:T(8,128)(2,1)S(1)}, bf16[192,1,256]{2,0,1:T(8,128)(2,1)S(1)}, u32[]{:S(2)}, u32[]{:S(2)}) collective-permute-start(bf16[192,1,256]{2,0,1:T(8,128)(2,1)S(1)} %get-tuple-element.6), channel_id=1, source_target_pairs={{1,0},{2,1},{3,2},{4,3},{5,4},{6,5},{7,6},{8,7},{9,8},{10,9},{11,1... | collective-permute-start | bytes 294920 | tf_op jit(solution)/shard_map/ppermute | solution.py:26

commit v13 on v11

--- a/solution.py
+++ b/solution.py
@@ -42,8 +42,15 @@
         copy.start()
         return copy
 
-    up_loads = [[load(wu_hbm.at[p + 2 * h], wu_ref.at[p, :, pl.ds(h * cin, cin)], 2 * p + h) for h in range(2)] for p in range(2)]
-    conv_loads = [load(w3_hbm.at[ky], w3_ref.at[:, pl.ds(ky * cin, cin)], 4 + ky) for ky in range(3)]
+    half = wu_hbm.shape[1] // 2
+    up_loads = [
+        [
+            [load(wu_hbm.at[p + 2 * h, pl.ds(m * half, half)], wu_ref.at[p, pl.ds(m * half, half), pl.ds(h * cin, cin)], 4 * p + 2 * m + h) for h in range(2)]
+            for m in range(2)
+        ]
+        for p in range(2)
+    ]
+    conv_loads = [load(w3_hbm.at[ky], w3_ref.at[:, pl.ds(ky * cin, cin)], 8 + ky) for ky in range(3)]
     peers, nwin, groups, cw = xw_ref.shape
     nfine, cout, fw = sk_ref.shape
     nout = nfine - 2
@@ -63,10 +70,12 @@
     stacked = jnp.concatenate([wide[:, cw:], wide[:, :span]], axis=0)
     parity = []
     for p in range(2):
-        for copy in up_loads[p]:
-            copy.wait()
-        z = dot(wu_ref[p], stacked)
-        taps = [z[k * cout : (k + 1) * cout] for k in range(4)]
+        taps = []
+        for m in range(2):
+            for copy in up_loads[p][m]:
+                copy.wait()
+            z = dot(wu_ref[p, m * half : (m + 1) * half], stacked)
+            taps += [z[k * cout : (k + 1) * cout] for k in range(2)]
         even = taps[1] + lane_shift(taps[3], cw, 1) + bu_ref[...]
         odd = taps[2] + lane_shift(taps[0], cw, -1) + bu_ref[...]
         parity.append((even.astype(jnp.bfloat16), odd.astype(jnp.bfloat16)))
@@ -116,7 +125,7 @@
             pltpu.VMEM((cout, nfine - 2, fw), jnp.float32),
             pltpu.VMEM((2, wu.shape[1], 2 * wu.shape[2]), wu.dtype),
             pltpu.VMEM((w3.shape[1], 3 * w3.shape[2]), w3.dtype),
-            pltpu.SemaphoreType.DMA((7,)),
+            pltpu.SemaphoreType.DMA((11,)),
         ],
         compiler_params=pltpu.CompilerParams(vmem_limit_bytes=48 * 1024 * 1024),
     )(flags, xw, sk, pltpu.with_memory_space_constraint(wu, pltpu.HBM), bu, pltpu.with_memory_space_constraint(w3, pltpu.HBM), b3)

time: 35.4 us -> 35.6 us (level)
  no operation moved by 1% of the time
where the time goes in v13:
time: 35.6 us; the launch traced here: 35.1 us
  starting transfers between devices  11.8 us (33%)
  waiting for transfers between devices  10.3 us (29%)
  Pallas kernels  10.1 us (28%)
  local copies, waits for them, and re-layouts  1.78 us (5%)
  other arithmetic  1.07 us (3%)
    pallas_call x1, Pallas kernels, decode(): pl.pallas_call(decoder_kernel, out_shape=jax.ShapeDtypeStruct((cout, nfin...  10.1 us
    ppermute x1, waiting for transfers between devices, skip_rows(): before = lax.ppermute(skip[:, -1:], 'row', up)  8.59 us
    all_to_all x1, starting transfers between devices, coarse_windows(): gathered = lax.all_to_all(windows, 'row', 0, 0, tiled=True)  6.55 us
    ppermute x1, starting transfers between devices, skip_rows(): before = lax.ppermute(skip[:, -1:], 'row', up)  3.34 us
    ppermute x1, starting transfers between devices, skip_rows(): after = lax.ppermute(skip[:, :1], 'row', down)  1.92 us
    ppermute x1, waiting for transfers between devices, skip_rows(): after = lax.ppermute(skip[:, :1], 'row', down)  1.67 us
    unnamed x8, local copies, waits for them, and re-layouts  1.43 us
    transpose x1, other arithmetic, coarse_windows(): windows = jnp.transpose(windows, (1, 2, 0, 3))  0.87 us
  transfers between devices with their start and end apart: 3, of which 2 were waited for; matrix products, arithmetic and copies ran while one was open for 2% of the time, Pallas kernels for 0%

profile of v13, /device:TPU:13, one launch (start us, length us, event | category | flops | bytes accessed | tf_op | source)
XLA Modules:
  0.0 35.1 jit_solution(13944041864706884675)
XLA Ops:
  0.0 1.3 %copy.17 = bf16[24,64,128]{2,0,1:T(8,128)(2,1)S(1)} copy(bf16[24,64,128]{2,1,0:T(8,128)(2,1)} %param.6) | data formatting | bytes 786432
  1.3 0.0 copy-start
  1.4 0.0 copy-start.1
  1.4 0.0 copy-start.2
  1.4 0.9 %maximum_bitcast_fusion.1 = bf16[16,6,24,128]{3,2,1,0:T(8,128)(2,1)} fusion(bf16[24,16,2,128]{3,0,2,1:T(8,128)(2,1)S(1)} %slice.17, bf16[24,16,4,128]{3,0,2,1:T(8,128)(2,1)S(1)} %slice.16), kind=kLoop, calls=%fused_computation.1 | loop fusion | flops 294912 | bytes 1179648 | tf_op jit(solution)/shard_map/transpose | solution.py:15
  2.3 6.6 %all-to-all-start = ((bf16[16,6,24,128]{3,2,1,0:T(8,128)(2,1)}), bf16[16,6,24,128]{3,2,1,0:T(8,128)(2,1)S(1)}, u32[]{:S(2)}, u32[]{:S(2)}) async-start(bf16[16,6,24,128]{3,2,1,0:T(8,128)(2,1)} %maximum_bitcast_fusion.1), calls=%async_computation | async-start | bytes 1179648 | tf_op jit(solution)/shard_map/all_to_all | solution.py:16
  8.8 0.0 copy-done
  8.8 0.2 copy.12
  9.0 3.3 %collective-permute-start = (bf16[192,1,256]{2,0,1:T(8,128)(2,1)S(1)}, bf16[192,1,256]{2,0,1:T(8,128)(2,1)S(1)}, u32[]{:S(2)}, u32[]{:S(2)}) collective-permute-start(bf16[192,1,256]{2,0,1:T(8,128)(2,1)S(1)} %get-tuple-element.5), channel_id=1, source_target_pairs={{0,1},{1,2},{2,3},{3,4},{4,5},{5,6},{6,7},{7,8},{8,9},{9,10},{10,1... | collective-permute-start | bytes 294920 | tf_op jit(solution)/shard_map/ppermute | solution.py:25
  12.4 1.9 %collective-permute-start.1 = (bf16[192,1,256]{2,0,1:T(8,128)(2,1)S(1)}, bf16[192,1,256]{2,0,1:T(8,128)(2,1)S(1)}, u32[]{:S(2)}, u32[]{:S(2)}) collective-permute-start(bf16[192,1,256]{2,0,1:T(8,128)(2,1)S(1)} %get-tuple-element.6), channel_id=1, source_target_pairs={{1,0},{2,1},{3,2},{4,3},{5,4},{6,5},{7,6},{8,7},{9,8},{10,9},{11,1... | collective-permute-start | bytes 294920 | tf_op jit(solution)/shard_map/ppermute | solution.py:26
  14.3 0.0 copy-done.1
  14.3 0.1 copy.15.bu_ref
  14.5 0.0 copy-done.2
  14.5 0.1 copy.16.b3_ref
  14.6 0.1 add_convert_fusion.flags
  14.7 8.6 %collective-permute-done = bf16[192,1,256]{2,0,1:T(8,128)(2,1)S(1)} collective-permute-done((bf16[192,1,256]{2,0,1:T(8,128)(2,1)S(1)}, bf16[192,1,256]{2,0,1:T(8,128)(2,1)S(1)}, u32[]{:S(2)}, u32[]{:S(2)}) %collective-permute-start) | collective-permute-done | bytes 98336 | tf_op jit(solution)/shard_map/ppermute | solution.py:25
  23.2 1.7 %collective-permute-done.1 = bf16[192,1,256]{2,0,1:T(8,128)(2,1)S(1)} collective-permute-done((bf16[192,1,256]{2,0,1:T(8,128)(2,1)S(1)}, bf16[192,1,256]{2,0,1:T(8,128)(2,1)S(1)}, u32[]{:S(2)}, u32[]{:S(2)}) %collective-permute-start.1) | collective-permute-done | bytes 98336 | tf_op jit(solution)/shard_map/ppermute | solution.py:26
  24.9 0.1 maximum_bitcast_fusion.sk_ref
  25.0 0.0 all-to-all-done.xw_ref
  25.1 10.1 %shard_map.64 = bf16[192,8,256]{2,1,0:T(8,128)(2,1)} custom-call(s32[2]{0:T(128)S(1)} %add_convert_fusion.flags, bf16[16,6,24,128]{3,2,1,0:T(8,128)(2,1)S(1)} %all-to-all-done.xw_ref, bf16[10,192,256]{2,1,0:T(8,128)(2,1)S(1)} %maximum_bitcast_fusion.sk_ref, bf16[4,768,384]{2,1,0:T(8,128)(2,1)} %bitcast.17, f32[192,1]{1,0:T(8,128)S(1)} %copy.15.bu_ref, ...), custom_call_target="tpu_custom_call" | custom-call | tf_op jit(solution)/shard_map/pallas_call | solution.py:119
  (4 shorter events, 0.1 us)
Async XLA Ops:
  1.3 7.6 %copy-start = (bf16[192,8,256]{2,1,0:T(8,128)(2,1)S(1)}, bf16[192,8,256]{2,1,0:T(8,128)(2,1)}, u32[]{:S(2)}) copy-start(bf16[192,8,256]{2,1,0:T(8,128)(2,1)} %param.7) | copy-start | bytes 2359300
  1.4 13.0 %copy-start.1 = (f32[192]{0:T(256)S(1)}, f32[192]{0:T(256)}, u32[]{:S(2)}) copy-start(f32[192]{0:T(256)} %param.9) | copy-start | bytes 2308
  1.4 13.1 %copy-start.2 = (f32[192]{0:T(256)S(1)}, f32[192]{0:T(256)}, u32[]{:S(2)}) copy-start(f32[192]{0:T(256)} %param.11) | copy-start | bytes 2308
  2.3 22.8 %all-to-all-start = ((bf16[16,6,24,128]{3,2,1,0:T(8,128)(2,1)}), bf16[16,6,24,128]{3,2,1,0:T(8,128)(2,1)S(1)}, u32[]{:S(2)}, u32[]{:S(2)}) async-start(bf16[16,6,24,128]{3,2,1,0:T(8,128)(2,1)} %maximum_bitcast_fusion.1), calls=%async_computation | async-start | bytes 1179648 | tf_op jit(solution)/shard_map/all_to_all | solution.py:16
  9.0 14.2 %collective-permute-start = (bf16[192,1,256]{2,0,1:T(8,128)(2,1)S(1)}, bf16[192,1,256]{2,0,1:T(8,128)(2,1)S(1)}, u32[]{:S(2)}, u32[]{:S(2)}) collective-permute-start(bf16[192,1,256]{2,0,1:T(8,128)(2,1)S(1)} %get-tuple-element.5), channel_id=1, source_target_pairs={{0,1},{1,2},{2,3},{3,4},{4,5},{5,6},{6,7},{7,8},{8,9},{9,10},{10,1... | collective-permute-start | bytes 294920 | tf_op jit(solution)/shard_map/ppermute | solution.py:25
  12.4 12.5 %collective-permute-start.1 = (bf16[192,1,256]{2,0,1:T(8,128)(2,1)S(1)}, bf16[192,1,256]{2,0,1:T(8,128)(2,1)S(1)}, u32[]{:S(2)}, u32[]{:S(2)}) collective-permute-start(bf16[192,1,256]{2,0,1:T(8,128)(2,1)S(1)} %get-tuple-element.6), channel_id=1, source_target_pairs={{1,0},{2,1},{3,2},{4,3},{5,4},{6,5},{7,6},{8,7},{9,8},{10,9},{11,1... | collective-permute-start | bytes 294920 | tf_op jit(solution)/shard_map/ppermute | solution.py:26

commit v14 on v11

--- a/solution.py
+++ b/solution.py
@@ -88,11 +88,10 @@
         if t == nfine - 1:
             row = jnp.where(flags[1] == 1, 0.0, row)
         joined.append(jnp.concatenate([sk_ref[t], row.astype(jnp.bfloat16)], axis=0))
-    field = jnp.concatenate(joined, axis=1)
     for copy in conv_loads:
         copy.wait()
 
-    rows = jnp.concatenate([field[:, ky * fw : (ky + nout) * fw] for ky in range(3)], axis=0)
+    rows = jnp.concatenate([jnp.concatenate(joined[ky : ky + nout], axis=1) for ky in range(3)], axis=0)
     total = dot(w3_ref[...], rows)
     pre = total[cout : 2 * cout]
     pre = pre + lane_shift(total[:cout], fw, 1) + lane_shift(total[2 * cout :], fw, -1)

time: 35.4 us -> 35.4 us (level)
  no operation moved by 1% of the time
where the time goes in v14:
time: 35.4 us; the launch traced here: 34.9 us
  starting transfers between devices  11.8 us (33%)
  waiting for transfers between devices  10.3 us (29%)
  Pallas kernels  9.88 us (28%)
  local copies, waits for them, and re-layouts  1.78 us (5%)
  other arithmetic  1.07 us (3%)
    pallas_call x1, Pallas kernels, decode(): pl.pallas_call(decoder_kernel, out_shape=jax.ShapeDtypeStruct((cout, nfin...  9.88 us
    ppermute x1, waiting for transfers between devices, skip_rows(): before = lax.ppermute(skip[:, -1:], 'row', up)  8.59 us
    all_to_all x1, starting transfers between devices, coarse_windows(): gathered = lax.all_to_all(windows, 'row', 0, 0, tiled=True)  6.55 us
    ppermute x1, starting transfers between devices, skip_rows(): before = lax.ppermute(skip[:, -1:], 'row', up)  3.34 us
    ppermute x1, starting transfers between devices, skip_rows(): after = lax.ppermute(skip[:, :1], 'row', down)  1.92 us
    ppermute x1, waiting for transfers between devices, skip_rows(): after = lax.ppermute(skip[:, :1], 'row', down)  1.67 us
    unnamed x8, local copies, waits for them, and re-layouts  1.43 us
    transpose x1, other arithmetic, coarse_windows(): windows = jnp.transpose(windows, (1, 2, 0, 3))  0.87 us
  transfers between devices with their start and end apart: 3, of which 2 were waited for; matrix products, arithmetic and copies ran while one was open for 2% of the time, Pallas kernels for 0%

profile of v14, /device:TPU:13, one launch (start us, length us, event | category | flops | bytes accessed | tf_op | source)
XLA Modules:
  0.0 34.9 jit_solution(10452331405595877893)
XLA Ops:
  0.0 1.3 %copy.17 = bf16[24,64,128]{2,0,1:T(8,128)(2,1)S(1)} copy(bf16[24,64,128]{2,1,0:T(8,128)(2,1)} %param.6) | data formatting | bytes 786432
  1.3 0.0 copy-start
  1.4 0.0 copy-start.1
  1.4 0.0 copy-start.2
  1.4 0.9 %maximum_bitcast_fusion.1 = bf16[16,6,24,128]{3,2,1,0:T(8,128)(2,1)} fusion(bf16[24,16,2,128]{3,0,2,1:T(8,128)(2,1)S(1)} %slice.17, bf16[24,16,4,128]{3,0,2,1:T(8,128)(2,1)S(1)} %slice.16), kind=kLoop, calls=%fused_computation.1 | loop fusion | flops 294912 | bytes 1179648 | tf_op jit(solution)/shard_map/transpose | solution.py:15
  2.3 6.6 %all-to-all-start = ((bf16[16,6,24,128]{3,2,1,0:T(8,128)(2,1)}), bf16[16,6,24,128]{3,2,1,0:T(8,128)(2,1)S(1)}, u32[]{:S(2)}, u32[]{:S(2)}) async-start(bf16[16,6,24,128]{3,2,1,0:T(8,128)(2,1)} %maximum_bitcast_fusion.1), calls=%async_computation | async-start | bytes 1179648 | tf_op jit(solution)/shard_map/all_to_all | solution.py:16
  8.8 0.0 copy-done
  8.8 0.2 copy.12
  9.0 3.3 %collective-permute-start = (bf16[192,1,256]{2,0,1:T(8,128)(2,1)S(1)}, bf16[192,1,256]{2,0,1:T(8,128)(2,1)S(1)}, u32[]{:S(2)}, u32[]{:S(2)}) collective-permute-start(bf16[192,1,256]{2,0,1:T(8,128)(2,1)S(1)} %get-tuple-element.5), channel_id=1, source_target_pairs={{0,1},{1,2},{2,3},{3,4},{4,5},{5,6},{6,7},{7,8},{8,9},{9,10},{10,1... | collective-permute-start | bytes 294920 | tf_op jit(solution)/shard_map/ppermute | solution.py:25
  12.4 1.9 %collective-permute-start.1 = (bf16[192,1,256]{2,0,1:T(8,128)(2,1)S(1)}, bf16[192,1,256]{2,0,1:T(8,128)(2,1)S(1)}, u32[]{:S(2)}, u32[]{:S(2)}) collective-permute-start(bf16[192,1,256]{2,0,1:T(8,128)(2,1)S(1)} %get-tuple-element.6), channel_id=1, source_target_pairs={{1,0},{2,1},{3,2},{4,3},{5,4},{6,5},{7,6},{8,7},{9,8},{10,9},{11,1... | collective-permute-start | bytes 294920 | tf_op jit(solution)/shard_map/ppermute | solution.py:26
  14.3 0.0 copy-done.1
  14.3 0.1 copy.15.bu_ref
  14.5 0.0 copy-done.2
  14.5 0.1 copy.16.b3_ref
  14.6 0.1 add_convert_fusion.flags
  14.7 8.6 %collective-permute-done = bf16[192,1,256]{2,0,1:T(8,128)(2,1)S(1)} collective-permute-done((bf16[192,1,256]{2,0,1:T(8,128)(2,1)S(1)}, bf16[192,1,256]{2,0,1:T(8,128)(2,1)S(1)}, u32[]{:S(2)}, u32[]{:S(2)}) %collective-permute-start) | collective-permute-done | bytes 98336 | tf_op jit(solution)/shard_map/ppermute | solution.py:25
  23.2 1.7 %collective-permute-done.1 = bf16[192,1,256]{2,0,1:T(8,128)(2,1)S(1)} collective-permute-done((bf16[192,1,256]{2,0,1:T(8,128)(2,1)S(1)}, bf16[192,1,256]{2,0,1:T(8,128)(2,1)S(1)}, u32[]{:S(2)}, u32[]{:S(2)}) %collective-permute-start.1) | collective-permute-done | bytes 98336 | tf_op jit(solution)/shard_map/ppermute | solution.py:26
  24.9 0.1 maximum_bitcast_fusion.sk_ref
  25.0 0.0 all-to-all-done.xw_ref
  25.1 9.9 %shard_map.64 = bf16[192,8,256]{2,1,0:T(8,128)(2,1)} custom-call(s32[2]{0:T(128)S(1)} %add_convert_fusion.flags, bf16[16,6,24,128]{3,2,1,0:T(8,128)(2,1)S(1)} %all-to-all-done.xw_ref, bf16[10,192,256]{2,1,0:T(8,128)(2,1)S(1)} %maximum_bitcast_fusion.sk_ref, bf16[4,768,384]{2,1,0:T(8,128)(2,1)} %bitcast.17, f32[192,1]{1,0:T(8,128)S(1)} %copy.15.bu_ref, ...), custom_call_target="tpu_custom_call" | custom-call | tf_op jit(solution)/shard_map/pallas_call | solution.py:109
  (4 shorter events, 0.1 us)
Async XLA Ops:
  1.3 7.6 %copy-start = (bf16[192,8,256]{2,1,0:T(8,128)(2,1)S(1)}, bf16[192,8,256]{2,1,0:T(8,128)(2,1)}, u32[]{:S(2)}) copy-start(bf16[192,8,256]{2,1,0:T(8,128)(2,1)} %param.7) | copy-start | bytes 2359300
  1.4 13.0 %copy-start.1 = (f32[192]{0:T(256)S(1)}, f32[192]{0:T(256)}, u32[]{:S(2)}) copy-start(f32[192]{0:T(256)} %param.9) | copy-start | bytes 2308
  1.4 13.1 %copy-start.2 = (f32[192]{0:T(256)S(1)}, f32[192]{0:T(256)}, u32[]{:S(2)}) copy-start(f32[192]{0:T(256)} %param.11) | copy-start | bytes 2308
  2.3 22.8 %all-to-all-start = ((bf16[16,6,24,128]{3,2,1,0:T(8,128)(2,1)}), bf16[16,6,24,128]{3,2,1,0:T(8,128)(2,1)S(1)}, u32[]{:S(2)}, u32[]{:S(2)}) async-start(bf16[16,6,24,128]{3,2,1,0:T(8,128)(2,1)} %maximum_bitcast_fusion.1), calls=%async_computation | async-start | bytes 1179648 | tf_op jit(solution)/shard_map/all_to_all | solution.py:16
  9.0 14.2 %collective-permute-start = (bf16[192,1,256]{2,0,1:T(8,128)(2,1)S(1)}, bf16[192,1,256]{2,0,1:T(8,128)(2,1)S(1)}, u32[]{:S(2)}, u32[]{:S(2)}) collective-permute-start(bf16[192,1,256]{2,0,1:T(8,128)(2,1)S(1)} %get-tuple-element.5), channel_id=1, source_target_pairs={{0,1},{1,2},{2,3},{3,4},{4,5},{5,6},{6,7},{7,8},{8,9},{9,10},{10,1... | collective-permute-start | bytes 294920 | tf_op jit(solution)/shard_map/ppermute | solution.py:25
  12.4 12.5 %collective-permute-start.1 = (bf16[192,1,256]{2,0,1:T(8,128)(2,1)S(1)}, bf16[192,1,256]{2,0,1:T(8,128)(2,1)S(1)}, u32[]{:S(2)}, u32[]{:S(2)}) collective-permute-start(bf16[192,1,256]{2,0,1:T(8,128)(2,1)S(1)} %get-tuple-element.6), channel_id=1, source_target_pairs={{1,0},{2,1},{3,2},{4,3},{5,4},{6,5},{7,6},{8,7},{9,8},{10,9},{11,1... | collective-permute-start | bytes 294920 | tf_op jit(solution)/shard_map/ppermute | solution.py:26

commit v15 on v11

--- a/solution.py
+++ b/solution.py
@@ -77,12 +77,16 @@
     put_odd = (pos == 2 * col + 1).astype(jnp.bfloat16)
     put = jnp.concatenate([put_even, put_odd], axis=0)
 
-    joined = []
+    pairs = []
     for t in range(nfine):
         even, odd = parity[t % 2]
         q = t // 2
-        pair = jnp.concatenate([even[:, q * cw : (q + 1) * cw], odd[:, q * cw : (q + 1) * cw]], axis=1)
-        row = dot(pair, put)
+        pairs.append(jnp.concatenate([even[:, q * cw : (q + 1) * cw], odd[:, q * cw : (q + 1) * cw]], axis=1))
+    placed = dot(jnp.concatenate(pairs, axis=0), put)
+
+    joined = []
+    for t in range(nfine):
+        row = placed[t * cout : (t + 1) * cout]
         if t == 0:
             row = jnp.where(flags[0] == 1, 0.0, row)
         if t == nfine - 1:

time: 35.4 us -> 35.3 us (level)
  no operation moved by 1% of the time
where the time goes in v15:
time: 35.3 us; the launch traced here: 34.9 us
  starting transfers between devices  11.8 us (33%)
  waiting for transfers between devices  10.3 us (29%)
  Pallas kernels  9.82 us (28%)
  local copies, waits for them, and re-layouts  1.78 us (5%)
  other arithmetic  1.07 us (3%)
    pallas_call x1, Pallas kernels, decode(): pl.pallas_call(decoder_kernel, out_shape=jax.ShapeDtypeStruct((cout, nfin...  9.82 us
    ppermute x1, waiting for transfers between devices, skip_rows(): before = lax.ppermute(skip[:, -1:], 'row', up)  8.59 us
    all_to_all x1, starting transfers between devices, coarse_windows(): gathered = lax.all_to_all(windows, 'row', 0, 0, tiled=True)  6.55 us
    ppermute x1, starting transfers between devices, skip_rows(): before = lax.ppermute(skip[:, -1:], 'row', up)  3.34 us
    ppermute x1, starting transfers between devices, skip_rows(): after = lax.ppermute(skip[:, :1], 'row', down)  1.92 us
    ppermute x1, waiting for transfers between devices, skip_rows(): after = lax.ppermute(skip[:, :1], 'row', down)  1.67 us
    unnamed x8, local copies, waits for them, and re-layouts  1.43 us
    transpose x1, other arithmetic, coarse_windows(): windows = jnp.transpose(windows, (1, 2, 0, 3))  0.87 us
  transfers between devices with their start and end apart: 3, of which 2 were waited for; matrix products, arithmetic and copies ran while one was open for 2% of the time, Pallas kernels for 0%

profile of v15, /device:TPU:13, one launch (start us, length us, event | category | flops | bytes accessed | tf_op | source)
XLA Modules:
  0.0 34.9 jit_solution(12498333405911713463)
XLA Ops:
  0.0 1.3 %copy.17 = bf16[24,64,128]{2,0,1:T(8,128)(2,1)S(1)} copy(bf16[24,64,128]{2,1,0:T(8,128)(2,1)} %param.6) | data formatting | bytes 786432
  1.3 0.0 copy-start
  1.4 0.0 copy-start.1
  1.4 0.0 copy-start.2
  1.4 0.9 %maximum_bitcast_fusion.1 = bf16[16,6,24,128]{3,2,1,0:T(8,128)(2,1)} fusion(bf16[24,16,2,128]{3,0,2,1:T(8,128)(2,1)S(1)} %slice.17, bf16[24,16,4,128]{3,0,2,1:T(8,128)(2,1)S(1)} %slice.16), kind=kLoop, calls=%fused_computation.1 | loop fusion | flops 294912 | bytes 1179648 | tf_op jit(solution)/shard_map/transpose | solution.py:15
  2.3 6.6 %all-to-all-start = ((bf16[16,6,24,128]{3,2,1,0:T(8,128)(2,1)}), bf16[16,6,24,128]{3,2,1,0:T(8,128)(2,1)S(1)}, u32[]{:S(2)}, u32[]{:S(2)}) async-start(bf16[16,6,24,128]{3,2,1,0:T(8,128)(2,1)} %maximum_bitcast_fusion.1), calls=%async_computation | async-start | bytes 1179648 | tf_op jit(solution)/shard_map/all_to_all | solution.py:16
  8.8 0.0 copy-done
  8.8 0.2 copy.12
  9.0 3.3 %collective-permute-start = (bf16[192,1,256]{2,0,1:T(8,128)(2,1)S(1)}, bf16[192,1,256]{2,0,1:T(8,128)(2,1)S(1)}, u32[]{:S(2)}, u32[]{:S(2)}) collective-permute-start(bf16[192,1,256]{2,0,1:T(8,128)(2,1)S(1)} %get-tuple-element.5), channel_id=1, source_target_pairs={{0,1},{1,2},{2,3},{3,4},{4,5},{5,6},{6,7},{7,8},{8,9},{9,10},{10,1... | collective-permute-start | bytes 294920 | tf_op jit(solution)/shard_map/ppermute | solution.py:25
  12.4 1.9 %collective-permute-start.1 = (bf16[192,1,256]{2,0,1:T(8,128)(2,1)S(1)}, bf16[192,1,256]{2,0,1:T(8,128)(2,1)S(1)}, u32[]{:S(2)}, u32[]{:S(2)}) collective-permute-start(bf16[192,1,256]{2,0,1:T(8,128)(2,1)S(1)} %get-tuple-element.6), channel_id=1, source_target_pairs={{1,0},{2,1},{3,2},{4,3},{5,4},{6,5},{7,6},{8,7},{9,8},{10,9},{11,1... | collective-permute-start | bytes 294920 | tf_op jit(solution)/shard_map/ppermute | solution.py:26
  14.3 0.0 copy-done.1
  14.3 0.1 copy.15.bu_ref
  14.5 0.0 copy-done.2
  14.5 0.1 copy.16.b3_ref
  14.6 0.1 add_convert_fusion.flags
  14.7 8.6 %collective-permute-done = bf16[192,1,256]{2,0,1:T(8,128)(2,1)S(1)} collective-permute-done((bf16[192,1,256]{2,0,1:T(8,128)(2,1)S(1)}, bf16[192,1,256]{2,0,1:T(8,128)(2,1)S(1)}, u32[]{:S(2)}, u32[]{:S(2)}) %collective-permute-start) | collective-permute-done | bytes 98336 | tf_op jit(solution)/shard_map/ppermute | solution.py:25
  23.2 1.7 %collective-permute-done.1 = bf16[192,1,256]{2,0,1:T(8,128)(2,1)S(1)} collective-permute-done((bf16[192,1,256]{2,0,1:T(8,128)(2,1)S(1)}, bf16[192,1,256]{2,0,1:T(8,128)(2,1)S(1)}, u32[]{:S(2)}, u32[]{:S(2)}) %collective-permute-start.1) | collective-permute-done | bytes 98336 | tf_op jit(solution)/shard_map/ppermute | solution.py:26
  24.9 0.1 maximum_bitcast_fusion.sk_ref
  25.0 0.0 all-to-all-done.xw_ref
  25.1 9.8 %shard_map.64 = bf16[192,8,256]{2,1,0:T(8,128)(2,1)} custom-call(s32[2]{0:T(128)S(1)} %add_convert_fusion.flags, bf16[16,6,24,128]{3,2,1,0:T(8,128)(2,1)S(1)} %all-to-all-done.xw_ref, bf16[10,192,256]{2,1,0:T(8,128)(2,1)S(1)} %maximum_bitcast_fusion.sk_ref, bf16[4,768,384]{2,1,0:T(8,128)(2,1)} %bitcast.17, f32[192,1]{1,0:T(8,128)S(1)} %copy.15.bu_ref, ...), custom_call_target="tpu_custom_call" | custom-call | tf_op jit(solution)/shard_map/pallas_call | solution.py:114
  (4 shorter events, 0.1 us)
Async XLA Ops:
  1.3 7.6 %copy-start = (bf16[192,8,256]{2,1,0:T(8,128)(2,1)S(1)}, bf16[192,8,256]{2,1,0:T(8,128)(2,1)}, u32[]{:S(2)}) copy-start(bf16[192,8,256]{2,1,0:T(8,128)(2,1)} %param.7) | copy-start | bytes 2359300
  1.4 13.0 %copy-start.1 = (f32[192]{0:T(256)S(1)}, f32[192]{0:T(256)}, u32[]{:S(2)}) copy-start(f32[192]{0:T(256)} %param.9) | copy-start | bytes 2308
  1.4 13.1 %copy-start.2 = (f32[192]{0:T(256)S(1)}, f32[192]{0:T(256)}, u32[]{:S(2)}) copy-start(f32[192]{0:T(256)} %param.11) | copy-start | bytes 2308
  2.3 22.8 %all-to-all-start = ((bf16[16,6,24,128]{3,2,1,0:T(8,128)(2,1)}), bf16[16,6,24,128]{3,2,1,0:T(8,128)(2,1)S(1)}, u32[]{:S(2)}, u32[]{:S(2)}) async-start(bf16[16,6,24,128]{3,2,1,0:T(8,128)(2,1)} %maximum_bitcast_fusion.1), calls=%async_computation | async-start | bytes 1179648 | tf_op jit(solution)/shard_map/all_to_all | solution.py:16
  9.0 14.2 %collective-permute-start = (bf16[192,1,256]{2,0,1:T(8,128)(2,1)S(1)}, bf16[192,1,256]{2,0,1:T(8,128)(2,1)S(1)}, u32[]{:S(2)}, u32[]{:S(2)}) collective-permute-start(bf16[192,1,256]{2,0,1:T(8,128)(2,1)S(1)} %get-tuple-element.5), channel_id=1, source_target_pairs={{0,1},{1,2},{2,3},{3,4},{4,5},{5,6},{6,7},{7,8},{8,9},{9,10},{10,1... | collective-permute-start | bytes 294920 | tf_op jit(solution)/shard_map/ppermute | solution.py:25
  12.4 12.5 %collective-permute-start.1 = (bf16[192,1,256]{2,0,1:T(8,128)(2,1)S(1)}, bf16[192,1,256]{2,0,1:T(8,128)(2,1)S(1)}, u32[]{:S(2)}, u32[]{:S(2)}) collective-permute-start(bf16[192,1,256]{2,0,1:T(8,128)(2,1)S(1)} %get-tuple-element.6), channel_id=1, source_target_pairs={{1,0},{2,1},{3,2},{4,3},{5,4},{6,5},{7,6},{8,7},{9,8},{10,9},{11,1... | collective-permute-start | bytes 294920 | tf_op jit(solution)/shard_map/ppermute | solution.py:26

commit v16 on v11

--- a/solution.py
+++ b/solution.py
@@ -34,7 +34,7 @@
     return jnp.where(lane == edge, 0.0, pltpu.roll(v, step % v.shape[1], 1))
 
 
-def decoder_kernel(flags, xw_ref, sk_ref, wu_hbm, bu_ref, w3_hbm, b3_ref, out_ref, act_ref, wu_ref, w3_ref, sems):
+def decoder_kernel(flags, xw_ref, sk_ref, wu_hbm, bu_ref, w3_hbm, b3_ref, out_ref, act_ref, out_buf, wu_ref, w3_ref, sems):
     cin = wu_hbm.shape[2]
 
     def load(src, dst, k):
@@ -94,13 +94,19 @@
 
     rows = jnp.concatenate([field[:, ky * fw : (ky + nout) * fw] for ky in range(3)], axis=0)
     total = dot(w3_ref[...], rows)
-    pre = total[cout : 2 * cout]
-    pre = pre + lane_shift(total[:cout], fw, 1) + lane_shift(total[2 * cout :], fw, -1)
-    pre = pre + b3_ref[...]
-    act = pre / (1.0 + jnp.exp(-pre))
-    for y in range(nout):
-        act_ref[:, y, :] = act[:, y * fw : (y + 1) * fw]
-    out_ref[...] = act_ref[...].astype(out_ref.dtype)
+    block = cout // 3 if cout % 48 == 0 else cout
+    stores = []
+    for c0 in range(0, cout, block):
+        part = lambda kx: total[kx * cout + c0 : kx * cout + c0 + block]
+        pre = part(1) + lane_shift(part(0), fw, 1) + lane_shift(part(2), fw, -1)
+        pre = pre + b3_ref[pl.ds(c0, block)]
+        act = pre / (1.0 + jnp.exp(-pre))
+        for y in range(nout):
+            act_ref[pl.ds(c0, block), y, :] = act[:, y * fw : (y + 1) * fw]
+        out_buf[pl.ds(c0, block)] = act_ref[pl.ds(c0, block)].astype(out_buf.dtype)
+        stores.append(load(out_buf.at[pl.ds(c0, block)], out_ref.at[pl.ds(c0, block)], 7 + len(stores)))
+    for copy in stores:
+        copy.wait()
 
 
 def decode(flags, xw, sk, wu, bu, w3, b3):
@@ -111,12 +117,13 @@
         decoder_kernel,
         out_shape=jax.ShapeDtypeStruct((cout, nfine - 2, fw), jnp.bfloat16),
         in_specs=[pl.BlockSpec(memory_space=pltpu.SMEM), vmem, vmem, hbm, vmem, hbm, vmem],
-        out_specs=vmem,
+        out_specs=pl.BlockSpec(memory_space=pl.ANY),
         scratch_shapes=[
             pltpu.VMEM((cout, nfine - 2, fw), jnp.float32),
+            pltpu.VMEM((cout, nfine - 2, fw), jnp.bfloat16),
             pltpu.VMEM((2, wu.shape[1], 2 * wu.shape[2]), wu.dtype),
             pltpu.VMEM((w3.shape[1], 3 * w3.shape[2]), w3.dtype),
-            pltpu.SemaphoreType.DMA((7,)),
+            pltpu.SemaphoreType.DMA((10,)),
         ],
         compiler_params=pltpu.CompilerParams(vmem_limit_bytes=48 * 1024 * 1024),
     )(flags, xw, sk, pltpu.with_memory_space_constraint(wu, pltpu.HBM), bu, pltpu.with_memory_space_constraint(w3, pltpu.HBM), b3)

time: 35.4 us -> 35.2 us (level)
  no operation moved by 1% of the time
where the time goes in v16:
time: 35.2 us; the launch traced here: 34.8 us
  starting transfers between devices  11.8 us (34%)
  waiting for transfers between devices  10.3 us (29%)
  Pallas kernels  9.73 us (28%)
  local copies, waits for them, and re-layouts  1.78 us (5%)
  other arithmetic  1.07 us (3%)
    pallas_call x1, Pallas kernels, decode(): pl.pallas_call(decoder_kernel, out_shape=jax.ShapeDtypeStruct((cout, nfin...  9.73 us
    ppermute x1, waiting for transfers between devices, skip_rows(): before = lax.ppermute(skip[:, -1:], 'row', up)  8.59 us
    all_to_all x1, starting transfers between devices, coarse_windows(): gathered = lax.all_to_all(windows, 'row', 0, 0, tiled=True)  6.55 us
    ppermute x1, starting transfers between devices, skip_rows(): before = lax.ppermute(skip[:, -1:], 'row', up)  3.34 us
    ppermute x1, starting transfers between devices, skip_rows(): after = lax.ppermute(skip[:, :1], 'row', down)  1.92 us
    ppermute x1, waiting for transfers between devices, skip_rows(): after = lax.ppermute(skip[:, :1], 'row', down)  1.67 us
    unnamed x8, local copies, waits for them, and re-layouts  1.43 us
    transpose x1, other arithmetic, coarse_windows(): windows = jnp.transpose(windows, (1, 2, 0, 3))  0.87 us
  transfers between devices with their start and end apart: 3, of which 2 were waited for; matrix products, arithmetic and copies ran while one was open for 2% of the time, Pallas kernels for 0%

profile of v16, /device:TPU:13, one launch (start us, length us, event | category | flops | bytes accessed | tf_op | source)
XLA Modules:
  0.0 34.8 jit_solution(15612899379621470960)
XLA Ops:
  0.0 1.3 %copy.17 = bf16[24,64,128]{2,0,1:T(8,128)(2,1)S(1)} copy(bf16[24,64,128]{2,1,0:T(8,128)(2,1)} %param.6) | data formatting | bytes 786432
  1.3 0.0 copy-start
  1.4 0.0 copy-start.1
  1.4 0.0 copy-start.2
  1.4 0.9 %maximum_bitcast_fusion.1 = bf16[16,6,24,128]{3,2,1,0:T(8,128)(2,1)} fusion(bf16[24,16,2,128]{3,0,2,1:T(8,128)(2,1)S(1)} %slice.17, bf16[24,16,4,128]{3,0,2,1:T(8,128)(2,1)S(1)} %slice.16), kind=kLoop, calls=%fused_computation.1 | loop fusion | flops 294912 | bytes 1179648 | tf_op jit(solution)/shard_map/transpose | solution.py:15
  2.3 6.6 %all-to-all-start = ((bf16[16,6,24,128]{3,2,1,0:T(8,128)(2,1)}), bf16[16,6,24,128]{3,2,1,0:T(8,128)(2,1)S(1)}, u32[]{:S(2)}, u32[]{:S(2)}) async-start(bf16[16,6,24,128]{3,2,1,0:T(8,128)(2,1)} %maximum_bitcast_fusion.1), calls=%async_computation | async-start | bytes 1179648 | tf_op jit(solution)/shard_map/all_to_all | solution.py:16
  8.8 0.0 copy-done
  8.8 0.2 copy.12
  9.0 3.3 %collective-permute-start = (bf16[192,1,256]{2,0,1:T(8,128)(2,1)S(1)}, bf16[192,1,256]{2,0,1:T(8,128)(2,1)S(1)}, u32[]{:S(2)}, u32[]{:S(2)}) collective-permute-start(bf16[192,1,256]{2,0,1:T(8,128)(2,1)S(1)} %get-tuple-element.5), channel_id=1, source_target_pairs={{0,1},{1,2},{2,3},{3,4},{4,5},{5,6},{6,7},{7,8},{8,9},{9,10},{10,1... | collective-permute-start | bytes 294920 | tf_op jit(solution)/shard_map/ppermute | solution.py:25
  12.4 1.9 %collective-permute-start.1 = (bf16[192,1,256]{2,0,1:T(8,128)(2,1)S(1)}, bf16[192,1,256]{2,0,1:T(8,128)(2,1)S(1)}, u32[]{:S(2)}, u32[]{:S(2)}) collective-permute-start(bf16[192,1,256]{2,0,1:T(8,128)(2,1)S(1)} %get-tuple-element.6), channel_id=1, source_target_pairs={{1,0},{2,1},{3,2},{4,3},{5,4},{6,5},{7,6},{8,7},{9,8},{10,9},{11,1... | collective-permute-start | bytes 294920 | tf_op jit(solution)/shard_map/ppermute | solution.py:26
  14.3 0.0 copy-done.1
  14.3 0.1 copy.15.bu_ref
  14.5 0.0 copy-done.2
  14.5 0.1 copy.16.b3_ref
  14.6 0.1 add_convert_fusion.flags
  14.7 8.6 %collective-permute-done = bf16[192,1,256]{2,0,1:T(8,128)(2,1)S(1)} collective-permute-done((bf16[192,1,256]{2,0,1:T(8,128)(2,1)S(1)}, bf16[192,1,256]{2,0,1:T(8,128)(2,1)S(1)}, u32[]{:S(2)}, u32[]{:S(2)}) %collective-permute-start) | collective-permute-done | bytes 98336 | tf_op jit(solution)/shard_map/ppermute | solution.py:25
  23.2 1.7 %collective-permute-done.1 = bf16[192,1,256]{2,0,1:T(8,128)(2,1)S(1)} collective-permute-done((bf16[192,1,256]{2,0,1:T(8,128)(2,1)S(1)}, bf16[192,1,256]{2,0,1:T(8,128)(2,1)S(1)}, u32[]{:S(2)}, u32[]{:S(2)}) %collective-permute-start.1) | collective-permute-done | bytes 98336 | tf_op jit(solution)/shard_map/ppermute | solution.py:26
  24.9 0.1 maximum_bitcast_fusion.sk_ref
  25.0 0.0 all-to-all-done.xw_ref
  25.1 9.7 %shard_map.64 = bf16[192,8,256]{2,1,0:T(8,128)(2,1)} custom-call(s32[2]{0:T(128)S(1)} %add_convert_fusion.flags, bf16[16,6,24,128]{3,2,1,0:T(8,128)(2,1)S(1)} %all-to-all-done.xw_ref, bf16[10,192,256]{2,1,0:T(8,128)(2,1)S(1)} %maximum_bitcast_fusion.sk_ref, bf16[4,768,384]{2,1,0:T(8,128)(2,1)} %bitcast.17, f32[192,1]{1,0:T(8,128)S(1)} %copy.15.bu_ref, ...), custom_call_target="tpu_custom_call" | custom-call | tf_op jit(solution)/shard_map/pallas_call | solution.py:116
  (4 shorter events, 0.1 us)
Async XLA Ops:
  1.3 7.6 %copy-start = (bf16[192,8,256]{2,1,0:T(8,128)(2,1)S(1)}, bf16[192,8,256]{2,1,0:T(8,128)(2,1)}, u32[]{:S(2)}) copy-start(bf16[192,8,256]{2,1,0:T(8,128)(2,1)} %param.7) | copy-start | bytes 2359300
  1.4 13.0 %copy-start.1 = (f32[192]{0:T(256)S(1)}, f32[192]{0:T(256)}, u32[]{:S(2)}) copy-start(f32[192]{0:T(256)} %param.9) | copy-start | bytes 2308
  1.4 13.1 %copy-start.2 = (f32[192]{0:T(256)S(1)}, f32[192]{0:T(256)}, u32[]{:S(2)}) copy-start(f32[192]{0:T(256)} %param.11) | copy-start | bytes 2308
  2.3 22.8 %all-to-all-start = ((bf16[16,6,24,128]{3,2,1,0:T(8,128)(2,1)}), bf16[16,6,24,128]{3,2,1,0:T(8,128)(2,1)S(1)}, u32[]{:S(2)}, u32[]{:S(2)}) async-start(bf16[16,6,24,128]{3,2,1,0:T(8,128)(2,1)} %maximum_bitcast_fusion.1), calls=%async_computation | async-start | bytes 1179648 | tf_op jit(solution)/shard_map/all_to_all | solution.py:16
  9.0 14.2 %collective-permute-start = (bf16[192,1,256]{2,0,1:T(8,128)(2,1)S(1)}, bf16[192,1,256]{2,0,1:T(8,128)(2,1)S(1)}, u32[]{:S(2)}, u32[]{:S(2)}) collective-permute-start(bf16[192,1,256]{2,0,1:T(8,128)(2,1)S(1)} %get-tuple-element.5), channel_id=1, source_target_pairs={{0,1},{1,2},{2,3},{3,4},{4,5},{5,6},{6,7},{7,8},{8,9},{9,10},{10,1... | collective-permute-start | bytes 294920 | tf_op jit(solution)/shard_map/ppermute | solution.py:25
  12.4 12.5 %collective-permute-start.1 = (bf16[192,1,256]{2,0,1:T(8,128)(2,1)S(1)}, bf16[192,1,256]{2,0,1:T(8,128)(2,1)S(1)}, u32[]{:S(2)}, u32[]{:S(2)}) collective-permute-start(bf16[192,1,256]{2,0,1:T(8,128)(2,1)S(1)} %get-tuple-element.6), channel_id=1, source_target_pairs={{1,0},{2,1},{3,2},{4,3},{5,4},{6,5},{7,6},{8,7},{9,8},{10,9},{11,1... | collective-permute-start | bytes 294920 | tf_op jit(solution)/shard_map/ppermute | solution.py:26

commit v17 on v11

--- a/solution.py
+++ b/solution.py
@@ -61,11 +61,13 @@
 
     wide = jnp.concatenate([window_row(i) for i in range(nwin)], axis=1)
     stacked = jnp.concatenate([wide[:, cw:], wide[:, :span]], axis=0)
+    for copies in up_loads:
+        for copy in copies:
+            copy.wait()
+    zz = dot(wu_ref[...].reshape(2 * wu_ref.shape[1], wu_ref.shape[2]), stacked)
     parity = []
     for p in range(2):
-        for copy in up_loads[p]:
-            copy.wait()
-        z = dot(wu_ref[p], stacked)
+        z = zz[p * 4 * cout : (p + 1) * 4 * cout]
         taps = [z[k * cout : (k + 1) * cout] for k in range(4)]
         even = taps[1] + lane_shift(taps[3], cw, 1) + bu_ref[...]
         odd = taps[2] + lane_shift(taps[0], cw, -1) + bu_ref[...]

time: 35.4 us -> 35.4 us (level)
  no operation moved by 1% of the time
where the time goes in v17:
time: 35.4 us; the launch traced here: 34.9 us
  starting transfers between devices  11.8 us (33%)
  waiting for transfers between devices  10.3 us (29%)
  Pallas kernels  9.87 us (28%)
  local copies, waits for them, and re-layouts  1.78 us (5%)
  other arithmetic  1.07 us (3%)
    pallas_call x1, Pallas kernels, decode(): pl.pallas_call(decoder_kernel, out_shape=jax.ShapeDtypeStruct((cout, nfin...  9.87 us
    ppermute x1, waiting for transfers between devices, skip_rows(): before = lax.ppermute(skip[:, -1:], 'row', up)  8.59 us
    all_to_all x1, starting transfers between devices, coarse_windows(): gathered = lax.all_to_all(windows, 'row', 0, 0, tiled=True)  6.55 us
    ppermute x1, starting transfers between devices, skip_rows(): before = lax.ppermute(skip[:, -1:], 'row', up)  3.34 us
    ppermute x1, starting transfers between devices, skip_rows(): after = lax.ppermute(skip[:, :1], 'row', down)  1.92 us
    ppermute x1, waiting for transfers between devices, skip_rows(): after = lax.ppermute(skip[:, :1], 'row', down)  1.67 us
    unnamed x8, local copies, waits for them, and re-layouts  1.43 us
    transpose x1, other arithmetic, coarse_windows(): windows = jnp.transpose(windows, (1, 2, 0, 3))  0.87 us
  transfers between devices with their start and end apart: 3, of which 2 were waited for; matrix products, arithmetic and copies ran while one was open for 2% of the time, Pallas kernels for 0%

profile of v17, /device:TPU:13, one launch (start us, length us, event | category | flops | bytes accessed | tf_op | source)
XLA Modules:
  0.0 34.9 jit_solution(17817101261083960181)
XLA Ops:
  0.0 1.3 %copy.17 = bf16[24,64,128]{2,0,1:T(8,128)(2,1)S(1)} copy(bf16[24,64,128]{2,1,0:T(8,128)(2,1)} %param.6) | data formatting | bytes 786432
  1.3 0.0 copy-start
  1.4 0.0 copy-start.1
  1.4 0.0 copy-start.2
  1.4 0.9 %maximum_bitcast_fusion.1 = bf16[16,6,24,128]{3,2,1,0:T(8,128)(2,1)} fusion(bf16[24,16,2,128]{3,0,2,1:T(8,128)(2,1)S(1)} %slice.17, bf16[24,16,4,128]{3,0,2,1:T(8,128)(2,1)S(1)} %slice.16), kind=kLoop, calls=%fused_computation.1 | loop fusion | flops 294912 | bytes 1179648 | tf_op jit(solution)/shard_map/transpose | solution.py:15
  2.3 6.6 %all-to-all-start = ((bf16[16,6,24,128]{3,2,1,0:T(8,128)(2,1)}), bf16[16,6,24,128]{3,2,1,0:T(8,128)(2,1)S(1)}, u32[]{:S(2)}, u32[]{:S(2)}) async-start(bf16[16,6,24,128]{3,2,1,0:T(8,128)(2,1)} %maximum_bitcast_fusion.1), calls=%async_computation | async-start | bytes 1179648 | tf_op jit(solution)/shard_map/all_to_all | solution.py:16
  8.8 0.0 copy-done
  8.8 0.2 copy.12
  9.0 3.3 %collective-permute-start = (bf16[192,1,256]{2,0,1:T(8,128)(2,1)S(1)}, bf16[192,1,256]{2,0,1:T(8,128)(2,1)S(1)}, u32[]{:S(2)}, u32[]{:S(2)}) collective-permute-start(bf16[192,1,256]{2,0,1:T(8,128)(2,1)S(1)} %get-tuple-element.5), channel_id=1, source_target_pairs={{0,1},{1,2},{2,3},{3,4},{4,5},{5,6},{6,7},{7,8},{8,9},{9,10},{10,1... | collective-permute-start | bytes 294920 | tf_op jit(solution)/shard_map/ppermute | solution.py:25
  12.4 1.9 %collective-permute-start.1 = (bf16[192,1,256]{2,0,1:T(8,128)(2,1)S(1)}, bf16[192,1,256]{2,0,1:T(8,128)(2,1)S(1)}, u32[]{:S(2)}, u32[]{:S(2)}) collective-permute-start(bf16[192,1,256]{2,0,1:T(8,128)(2,1)S(1)} %get-tuple-element.6), channel_id=1, source_target_pairs={{1,0},{2,1},{3,2},{4,3},{5,4},{6,5},{7,6},{8,7},{9,8},{10,9},{11,1... | collective-permute-start | bytes 294920 | tf_op jit(solution)/shard_map/ppermute | solution.py:26
  14.3 0.0 copy-done.1
  14.3 0.1 copy.15.bu_ref
  14.5 0.0 copy-done.2
  14.5 0.1 copy.16.b3_ref
  14.6 0.1 add_convert_fusion.flags
  14.7 8.6 %collective-permute-done = bf16[192,1,256]{2,0,1:T(8,128)(2,1)S(1)} collective-permute-done((bf16[192,1,256]{2,0,1:T(8,128)(2,1)S(1)}, bf16[192,1,256]{2,0,1:T(8,128)(2,1)S(1)}, u32[]{:S(2)}, u32[]{:S(2)}) %collective-permute-start) | collective-permute-done | bytes 98336 | tf_op jit(solution)/shard_map/ppermute | solution.py:25
  23.2 1.7 %collective-permute-done.1 = bf16[192,1,256]{2,0,1:T(8,128)(2,1)S(1)} collective-permute-done((bf16[192,1,256]{2,0,1:T(8,128)(2,1)S(1)}, bf16[192,1,256]{2,0,1:T(8,128)(2,1)S(1)}, u32[]{:S(2)}, u32[]{:S(2)}) %collective-permute-start.1) | collective-permute-done | bytes 98336 | tf_op jit(solution)/shard_map/ppermute | solution.py:26
  24.9 0.1 maximum_bitcast_fusion.sk_ref
  25.0 0.0 all-to-all-done.xw_ref
  25.1 9.9 %shard_map.64 = bf16[192,8,256]{2,1,0:T(8,128)(2,1)} custom-call(s32[2]{0:T(128)S(1)} %add_convert_fusion.flags, bf16[16,6,24,128]{3,2,1,0:T(8,128)(2,1)S(1)} %all-to-all-done.xw_ref, bf16[10,192,256]{2,1,0:T(8,128)(2,1)S(1)} %maximum_bitcast_fusion.sk_ref, bf16[4,768,384]{2,1,0:T(8,128)(2,1)} %bitcast.17, f32[192,1]{1,0:T(8,128)S(1)} %copy.15.bu_ref, ...), custom_call_target="tpu_custom_call" | custom-call | tf_op jit(solution)/shard_map/pallas_call | solution.py:112
  (4 shorter events, 0.1 us)
Async XLA Ops:
  1.3 7.6 %copy-start = (bf16[192,8,256]{2,1,0:T(8,128)(2,1)S(1)}, bf16[192,8,256]{2,1,0:T(8,128)(2,1)}, u32[]{:S(2)}) copy-start(bf16[192,8,256]{2,1,0:T(8,128)(2,1)} %param.7) | copy-start | bytes 2359300
  1.4 13.0 %copy-start.1 = (f32[192]{0:T(256)S(1)}, f32[192]{0:T(256)}, u32[]{:S(2)}) copy-start(f32[192]{0:T(256)} %param.9) | copy-start | bytes 2308
  1.4 13.1 %copy-start.2 = (f32[192]{0:T(256)S(1)}, f32[192]{0:T(256)}, u32[]{:S(2)}) copy-start(f32[192]{0:T(256)} %param.11) | copy-start | bytes 2308
  2.3 22.8 %all-to-all-start = ((bf16[16,6,24,128]{3,2,1,0:T(8,128)(2,1)}), bf16[16,6,24,128]{3,2,1,0:T(8,128)(2,1)S(1)}, u32[]{:S(2)}, u32[]{:S(2)}) async-start(bf16[16,6,24,128]{3,2,1,0:T(8,128)(2,1)} %maximum_bitcast_fusion.1), calls=%async_computation | async-start | bytes 1179648 | tf_op jit(solution)/shard_map/all_to_all | solution.py:16
  9.0 14.2 %collective-permute-start = (bf16[192,1,256]{2,0,1:T(8,128)(2,1)S(1)}, bf16[192,1,256]{2,0,1:T(8,128)(2,1)S(1)}, u32[]{:S(2)}, u32[]{:S(2)}) collective-permute-start(bf16[192,1,256]{2,0,1:T(8,128)(2,1)S(1)} %get-tuple-element.5), channel_id=1, source_target_pairs={{0,1},{1,2},{2,3},{3,4},{4,5},{5,6},{6,7},{7,8},{8,9},{9,10},{10,1... | collective-permute-start | bytes 294920 | tf_op jit(solution)/shard_map/ppermute | solution.py:25
  12.4 12.5 %collective-permute-start.1 = (bf16[192,1,256]{2,0,1:T(8,128)(2,1)S(1)}, bf16[192,1,256]{2,0,1:T(8,128)(2,1)S(1)}, u32[]{:S(2)}, u32[]{:S(2)}) collective-permute-start(bf16[192,1,256]{2,0,1:T(8,128)(2,1)S(1)} %get-tuple-element.6), channel_id=1, source_target_pairs={{1,0},{2,1},{3,2},{4,3},{5,4},{6,5},{7,6},{8,7},{9,8},{10,9},{11,1... | collective-permute-start | bytes 294920 | tf_op jit(solution)/shard_map/ppermute | solution.py:26

commit v18 on v11

--- a/solution.py
+++ b/solution.py
@@ -92,14 +92,16 @@
     for copy in conv_loads:
         copy.wait()
 
-    rows = jnp.concatenate([field[:, ky * fw : (ky + nout) * fw] for ky in range(3)], axis=0)
-    total = dot(w3_ref[...], rows)
-    pre = total[cout : 2 * cout]
-    pre = pre + lane_shift(total[:cout], fw, 1) + lane_shift(total[2 * cout :], fw, -1)
-    pre = pre + b3_ref[...]
-    act = pre / (1.0 + jnp.exp(-pre))
-    for y in range(nout):
-        act_ref[:, y, :] = act[:, y * fw : (y + 1) * fw]
+    step = 2 if nout % 2 == 0 else 1
+    for y0 in range(0, nout, step):
+        rows = jnp.concatenate([field[:, (y0 + ky) * fw : (y0 + ky + step) * fw] for ky in range(3)], axis=0)
+        total = dot(w3_ref[...], rows)
+        pre = total[cout : 2 * cout]
+        pre = pre + lane_shift(total[:cout], fw, 1) + lane_shift(total[2 * cout :], fw, -1)
+        pre = pre + b3_ref[...]
+        act = pre / (1.0 + jnp.exp(-pre))
+        for i in range(step):
+            act_ref[:, y0 + i, :] = act[:, i * fw : (i + 1) * fw]
     out_ref[...] = act_ref[...].astype(out_ref.dtype)
 
 

time: 35.4 us -> 35.5 us (level)
  no operation moved by 1% of the time
where the time goes in v18:
time: 35.5 us; the launch traced here: 35 us
  starting transfers between devices  11.8 us (33%)
  waiting for transfers between devices  10.3 us (29%)
  Pallas kernels  9.95 us (28%)
  local copies, waits for them, and re-layouts  1.78 us (5%)
  other arithmetic  1.07 us (3%)
    pallas_call x1, Pallas kernels, decode(): pl.pallas_call(decoder_kernel, out_shape=jax.ShapeDtypeStruct((cout, nfin...  9.95 us
    ppermute x1, waiting for transfers between devices, skip_rows(): before = lax.ppermute(skip[:, -1:], 'row', up)  8.59 us
    all_to_all x1, starting transfers between devices, coarse_windows(): gathered = lax.all_to_all(windows, 'row', 0, 0, tiled=True)  6.55 us
    ppermute x1, starting transfers between devices, skip_rows(): before = lax.ppermute(skip[:, -1:], 'row', up)  3.34 us
    ppermute x1, starting transfers between devices, skip_rows(): after = lax.ppermute(skip[:, :1], 'row', down)  1.92 us
    ppermute x1, waiting for transfers between devices, skip_rows(): after = lax.ppermute(skip[:, :1], 'row', down)  1.67 us
    unnamed x8, local copies, waits for them, and re-layouts  1.43 us
    transpose x1, other arithmetic, coarse_windows(): windows = jnp.transpose(windows, (1, 2, 0, 3))  0.87 us
  transfers between devices with their start and end apart: 3, of which 2 were waited for; matrix products, arithmetic and copies ran while one was open for 2% of the time, Pallas kernels for 0%

profile of v18, /device:TPU:13, one launch (start us, length us, event | category | flops | bytes accessed | tf_op | source)
XLA Modules:
  0.0 35.0 jit_solution(549109771598497948)
XLA Ops:
  0.0 1.3 %copy.17 = bf16[24,64,128]{2,0,1:T(8,128)(2,1)S(1)} copy(bf16[24,64,128]{2,1,0:T(8,128)(2,1)} %param.6) | data formatting | bytes 786432
  1.3 0.0 copy-start
  1.4 0.0 copy-start.1
  1.4 0.0 copy-start.2
  1.4 0.9 %maximum_bitcast_fusion.1 = bf16[16,6,24,128]{3,2,1,0:T(8,128)(2,1)} fusion(bf16[24,16,2,128]{3,0,2,1:T(8,128)(2,1)S(1)} %slice.17, bf16[24,16,4,128]{3,0,2,1:T(8,128)(2,1)S(1)} %slice.16), kind=kLoop, calls=%fused_computation.1 | loop fusion | flops 294912 | bytes 1179648 | tf_op jit(solution)/shard_map/transpose | solution.py:15
  2.3 6.6 %all-to-all-start = ((bf16[16,6,24,128]{3,2,1,0:T(8,128)(2,1)}), bf16[16,6,24,128]{3,2,1,0:T(8,128)(2,1)S(1)}, u32[]{:S(2)}, u32[]{:S(2)}) async-start(bf16[16,6,24,128]{3,2,1,0:T(8,128)(2,1)} %maximum_bitcast_fusion.1), calls=%async_computation | async-start | bytes 1179648 | tf_op jit(solution)/shard_map/all_to_all | solution.py:16
  8.8 0.0 copy-done
  8.8 0.2 copy.12
  9.0 3.3 %collective-permute-start = (bf16[192,1,256]{2,0,1:T(8,128)(2,1)S(1)}, bf16[192,1,256]{2,0,1:T(8,128)(2,1)S(1)}, u32[]{:S(2)}, u32[]{:S(2)}) collective-permute-start(bf16[192,1,256]{2,0,1:T(8,128)(2,1)S(1)} %get-tuple-element.5), channel_id=1, source_target_pairs={{0,1},{1,2},{2,3},{3,4},{4,5},{5,6},{6,7},{7,8},{8,9},{9,10},{10,1... | collective-permute-start | bytes 294920 | tf_op jit(solution)/shard_map/ppermute | solution.py:25
  12.4 1.9 %collective-permute-start.1 = (bf16[192,1,256]{2,0,1:T(8,128)(2,1)S(1)}, bf16[192,1,256]{2,0,1:T(8,128)(2,1)S(1)}, u32[]{:S(2)}, u32[]{:S(2)}) collective-permute-start(bf16[192,1,256]{2,0,1:T(8,128)(2,1)S(1)} %get-tuple-element.6), channel_id=1, source_target_pairs={{1,0},{2,1},{3,2},{4,3},{5,4},{6,5},{7,6},{8,7},{9,8},{10,9},{11,1... | collective-permute-start | bytes 294920 | tf_op jit(solution)/shard_map/ppermute | solution.py:26
  14.3 0.0 copy-done.1
  14.3 0.1 copy.15.bu_ref
  14.5 0.0 copy-done.2
  14.5 0.1 copy.16.b3_ref
  14.6 0.1 add_convert_fusion.flags
  14.7 8.6 %collective-permute-done = bf16[192,1,256]{2,0,1:T(8,128)(2,1)S(1)} collective-permute-done((bf16[192,1,256]{2,0,1:T(8,128)(2,1)S(1)}, bf16[192,1,256]{2,0,1:T(8,128)(2,1)S(1)}, u32[]{:S(2)}, u32[]{:S(2)}) %collective-permute-start) | collective-permute-done | bytes 98336 | tf_op jit(solution)/shard_map/ppermute | solution.py:25
  23.2 1.7 %collective-permute-done.1 = bf16[192,1,256]{2,0,1:T(8,128)(2,1)S(1)} collective-permute-done((bf16[192,1,256]{2,0,1:T(8,128)(2,1)S(1)}, bf16[192,1,256]{2,0,1:T(8,128)(2,1)S(1)}, u32[]{:S(2)}, u32[]{:S(2)}) %collective-permute-start.1) | collective-permute-done | bytes 98336 | tf_op jit(solution)/shard_map/ppermute | solution.py:26
  24.9 0.1 maximum_bitcast_fusion.sk_ref
  25.0 0.0 all-to-all-done.xw_ref
  25.1 10.0 %shard_map.64 = bf16[192,8,256]{2,1,0:T(8,128)(2,1)} custom-call(s32[2]{0:T(128)S(1)} %add_convert_fusion.flags, bf16[16,6,24,128]{3,2,1,0:T(8,128)(2,1)S(1)} %all-to-all-done.xw_ref, bf16[10,192,256]{2,1,0:T(8,128)(2,1)S(1)} %maximum_bitcast_fusion.sk_ref, bf16[4,768,384]{2,1,0:T(8,128)(2,1)} %bitcast.17, f32[192,1]{1,0:T(8,128)S(1)} %copy.15.bu_ref, ...), custom_call_target="tpu_custom_call" | custom-call | tf_op jit(solution)/shard_map/pallas_call | solution.py:112
  (4 shorter events, 0.1 us)
Async XLA Ops:
  1.3 7.6 %copy-start = (bf16[192,8,256]{2,1,0:T(8,128)(2,1)S(1)}, bf16[192,8,256]{2,1,0:T(8,128)(2,1)}, u32[]{:S(2)}) copy-start(bf16[192,8,256]{2,1,0:T(8,128)(2,1)} %param.7) | copy-start | bytes 2359300
  1.4 13.0 %copy-start.1 = (f32[192]{0:T(256)S(1)}, f32[192]{0:T(256)}, u32[]{:S(2)}) copy-start(f32[192]{0:T(256)} %param.9) | copy-start | bytes 2308
  1.4 13.1 %copy-start.2 = (f32[192]{0:T(256)S(1)}, f32[192]{0:T(256)}, u32[]{:S(2)}) copy-start(f32[192]{0:T(256)} %param.11) | copy-start | bytes 2308
  2.3 22.8 %all-to-all-start = ((bf16[16,6,24,128]{3,2,1,0:T(8,128)(2,1)}), bf16[16,6,24,128]{3,2,1,0:T(8,128)(2,1)S(1)}, u32[]{:S(2)}, u32[]{:S(2)}) async-start(bf16[16,6,24,128]{3,2,1,0:T(8,128)(2,1)} %maximum_bitcast_fusion.1), calls=%async_computation | async-start | bytes 1179648 | tf_op jit(solution)/shard_map/all_to_all | solution.py:16
  9.0 14.2 %collective-permute-start = (bf16[192,1,256]{2,0,1:T(8,128)(2,1)S(1)}, bf16[192,1,256]{2,0,1:T(8,128)(2,1)S(1)}, u32[]{:S(2)}, u32[]{:S(2)}) collective-permute-start(bf16[192,1,256]{2,0,1:T(8,128)(2,1)S(1)} %get-tuple-element.5), channel_id=1, source_target_pairs={{0,1},{1,2},{2,3},{3,4},{4,5},{5,6},{6,7},{7,8},{8,9},{9,10},{10,1... | collective-permute-start | bytes 294920 | tf_op jit(solution)/shard_map/ppermute | solution.py:25
  12.4 12.5 %collective-permute-start.1 = (bf16[192,1,256]{2,0,1:T(8,128)(2,1)S(1)}, bf16[192,1,256]{2,0,1:T(8,128)(2,1)S(1)}, u32[]{:S(2)}, u32[]{:S(2)}) collective-permute-start(bf16[192,1,256]{2,0,1:T(8,128)(2,1)S(1)} %get-tuple-element.6), channel_id=1, source_target_pairs={{1,0},{2,1},{3,2},{4,3},{5,4},{6,5},{7,6},{8,7},{9,8},{10,9},{11,1... | collective-permute-start | bytes 294920 | tf_op jit(solution)/shard_map/ppermute | solution.py:26

commit v19 on v11

--- a/solution.py
+++ b/solution.py
@@ -34,7 +34,35 @@
     return jnp.where(lane == edge, 0.0, pltpu.roll(v, step % v.shape[1], 1))
 
 
-def decoder_kernel(flags, xw_ref, sk_ref, wu_hbm, bu_ref, w3_hbm, b3_ref, out_ref, act_ref, wu_ref, w3_ref, sems):
+def half_weights(w3_ref, first, width):
+    cin = w3_ref.shape[1] // 3
+    return jnp.concatenate([w3_ref[:, ky * cin + first : ky * cin + first + width] for ky in range(3)], axis=1)
+
+
+def stacked_rows(field, nout, fw):
+    return jnp.concatenate([field[:, ky * fw : (ky + nout) * fw] for ky in range(3)], axis=0)
+
+
+def combine(total, fw):
+    cout = total.shape[0] // 3
+    return total[cout : 2 * cout] + lane_shift(total[:cout], fw, 1) + lane_shift(total[2 * cout :], fw, -1)
+
+
+def skip_kernel(sk_ref, w3_hbm, b3_ref, out_ref, w3_ref, sems):
+    cin = w3_hbm.shape[2]
+    copies = [pltpu.make_async_copy(w3_hbm.at[ky], w3_ref.at[:, pl.ds(ky * cin, cin)], sems.at[ky]) for ky in range(3)]
+    for copy in copies:
+        copy.start()
+    nfine, skips, fw = sk_ref.shape
+    field = jnp.concatenate([sk_ref[t] for t in range(nfine)], axis=1)
+    rows = stacked_rows(field, nfine - 2, fw)
+    for copy in copies:
+        copy.wait()
+    total = jnp.dot(half_weights(w3_ref, 0, skips), rows, preferred_element_type=jnp.float32)
+    out_ref[...] = combine(total, fw) + b3_ref[...]
+
+
+def decoder_kernel(flags, xw_ref, part_hbm, wu_hbm, bu_ref, w3_hbm, out_ref, act_ref, part_ref, wu_ref, w3_ref, sems):
     cin = wu_hbm.shape[2]
 
     def load(src, dst, k):
@@ -44,9 +72,10 @@
 
     up_loads = [[load(wu_hbm.at[p + 2 * h], wu_ref.at[p, :, pl.ds(h * cin, cin)], 2 * p + h) for h in range(2)] for p in range(2)]
     conv_loads = [load(w3_hbm.at[ky], w3_ref.at[:, pl.ds(ky * cin, cin)], 4 + ky) for ky in range(3)]
+    part_load = load(part_hbm, part_ref, 7)
     peers, nwin, groups, cw = xw_ref.shape
-    nfine, cout, fw = sk_ref.shape
-    nout = nfine - 2
+    cout, nout, fw = out_ref.shape
+    nfine = nout + 2
     span = (nwin - 1) * cw
     f32 = jnp.float32
 
@@ -87,39 +116,61 @@
             row = jnp.where(flags[0] == 1, 0.0, row)
         if t == nfine - 1:
             row = jnp.where(flags[1] == 1, 0.0, row)
-        joined.append(jnp.concatenate([sk_ref[t], row.astype(jnp.bfloat16)], axis=0))
+        joined.append(row.astype(jnp.bfloat16))
     field = jnp.concatenate(joined, axis=1)
     for copy in conv_loads:
         copy.wait()
 
-    rows = jnp.concatenate([field[:, ky * fw : (ky + nout) * fw] for ky in range(3)], axis=0)
-    total = dot(w3_ref[...], rows)
-    pre = total[cout : 2 * cout]
-    pre = pre + lane_shift(total[:cout], fw, 1) + lane_shift(total[2 * cout :], fw, -1)
-    pre = pre + b3_ref[...]
+    skips = w3_ref.shape[1] // 3 - cout
+    total = dot(half_weights(w3_ref, skips, cout), stacked_rows(field, nout, fw))
+    part_load.wait()
+    pre = combine(total, fw) + part_ref[...]
     act = pre / (1.0 + jnp.exp(-pre))
     for y in range(nout):
         act_ref[:, y, :] = act[:, y * fw : (y + 1) * fw]
     out_ref[...] = act_ref[...].astype(out_ref.dtype)
 
 
-def decode(flags, xw, sk, wu, bu, w3, b3):
-    nfine, cout, fw = sk.shape
+def in_hbm(x):
+    return pltpu.with_memory_space_constraint(x, pltpu.HBM)
+
+
+def decode(flags, xw, part, wu, bu, w3, nfine, fw):
+    cout = bu.shape[0]
     vmem = pl.BlockSpec(memory_space=pltpu.VMEM)
     hbm = pl.BlockSpec(memory_space=pltpu.HBM)
     return pl.pallas_call(
         decoder_kernel,
         out_shape=jax.ShapeDtypeStruct((cout, nfine - 2, fw), jnp.bfloat16),
-        in_specs=[pl.BlockSpec(memory_space=pltpu.SMEM), vmem, vmem, hbm, vmem, hbm, vmem],
+        in_specs=[pl.BlockSpec(memory_space=pltpu.SMEM), vmem, hbm, hbm, vmem, hbm],
         out_specs=vmem,
         scratch_shapes=[
             pltpu.VMEM((cout, nfine - 2, fw), jnp.float32),
+            pltpu.VMEM(((cout, (nfine - 2) * fw)), jnp.float32),
             pltpu.VMEM((2, wu.shape[1], 2 * wu.shape[2]), wu.dtype),
             pltpu.VMEM((w3.shape[1], 3 * w3.shape[2]), w3.dtype),
-            pltpu.SemaphoreType.DMA((7,)),
+            pltpu.SemaphoreType.DMA((8,)),
         ],
         compiler_params=pltpu.CompilerParams(vmem_limit_bytes=48 * 1024 * 1024),
-    )(flags, xw, sk, pltpu.with_memory_space_constraint(wu, pltpu.HBM), bu, pltpu.with_memory_space_constraint(w3, pltpu.HBM), b3)
+    )(flags, xw, in_hbm(part), in_hbm(wu), bu, in_hbm(w3))
+
+
+def skip_conv(sk, w3, b3):
+    nfine, cout, fw = sk.shape
+    nout = nfine - 2
+    vmem = pl.BlockSpec(memory_space=pltpu.VMEM)
+    hbm = pl.BlockSpec(memory_space=pltpu.HBM)
+    flops = 2 * w3.shape[1] * 3 * cout * nout * fw
+    moved = sk.size * 2 + w3.size * 2 + cout * nout * fw * 4
+    return pl.pallas_call(
+        skip_kernel,
+        out_shape=jax.ShapeDtypeStruct((cout, nout * fw), jnp.float32),
+        in_specs=[vmem, hbm, vmem],
+        out_specs=vmem,
+        scratch_shapes=[pltpu.VMEM((w3.shape[1], 3 * w3.shape[2]), w3.dtype), pltpu.SemaphoreType.DMA((3,))],
+        compiler_params=pltpu.CompilerParams(vmem_limit_bytes=48 * 1024 * 1024),
+        cost_estimate=pl.CostEstimate(flops=flops, transcendentals=0, bytes_accessed=moved),
+    )(sk, in_hbm(w3), b3)
 
 
 def shards(coarse, skip_field, up_weight, up_bias, conv_weight, conv_bias):
@@ -131,7 +182,8 @@
     cout = up_weight.shape[3]
     wu = jnp.transpose(up_weight, (0, 1, 3, 2)).reshape(4, 4 * cout, -1)
     w3 = jnp.transpose(conv_weight, (0, 1, 3, 2)).reshape(3, 3 * cout, -1)
-    return decode(flags, xw, sk, wu, up_bias[:, None], w3, conv_bias[:, None])
+    part = skip_conv(sk, w3, conv_bias[:, None])
+    return decode(flags, xw, part, wu, up_bias[:, None], w3, sk.shape[0], sk.shape[2])
 
 
 def solution(mesh):

time: 35.4 us -> 39.9 us (1.13)
  Pallas kernels: 9.88 us -> 13.3 us
  local copies, waits for them, and re-layouts: 1.78 us -> 2.91 us
    pallas_call x0 -> x1, Pallas kernels: none -> 3.47 us  [skip_conv(): pl.pallas_call(skip_kernel, out_shape=jax.ShapeDtypeStruct((cout, nout *...]
    unnamed x8 -> x10, local copies, waits for them, and re-layouts: 1.43 us -> 2.56 us
  transfers between devices with their start and end apart: 3 -> 3, of which waited for: 2 -> 2; matrix products, arithmetic and copies ran while one was open for 2% -> 2% of each run, Pallas kernels for 0% -> 9%
where the time goes in v19:
time: 39.9 us; the launch traced here: 39.6 us
  Pallas kernels  13.3 us (33%)
  starting transfers between devices  11.9 us (30%)
  waiting for transfers between devices  10.3 us (26%)
  local copies, waits for them, and re-layouts  2.91 us (7%)
  other arithmetic  1.07 us (3%)
    pallas_call x1, Pallas kernels, decode(): pl.pallas_call(decoder_kernel, out_shape=jax.ShapeDtypeStruct((cout, nfin...  9.79 us
    ppermute x1, waiting for transfers between devices, skip_rows(): before = lax.ppermute(skip[:, -1:], 'row', up)  8.58 us
    all_to_all x1, starting transfers between devices, coarse_windows(): gathered = lax.all_to_all(windows, 'row', 0, 0, tiled=True)  6.69 us
    pallas_call x1, Pallas kernels, skip_conv(): pl.pallas_call(skip_kernel, out_shape=jax.ShapeDtypeStruct((cout, nout *...  3.47 us
    ppermute x1, starting transfers between devices, skip_rows(): before = lax.ppermute(skip[:, -1:], 'row', up)  3.34 us
    unnamed x10, local copies, waits for them, and re-layouts  2.56 us
    ppermute x1, starting transfers between devices, skip_rows(): after = lax.ppermute(skip[:, :1], 'row', down)  1.92 us
    ppermute x1, waiting for transfers between devices, skip_rows(): after = lax.ppermute(skip[:, :1], 'row', down)  1.67 us
  transfers between devices with their start and end apart: 3, of which 2 were waited for; matrix products, arithmetic and copies ran while one was open for 2% of the time, Pallas kernels for 9%

profile of v19, /device:TPU:13, one launch (start us, length us, event | category | flops | bytes accessed | tf_op | source)
XLA Modules:
  0.0 39.6 jit_solution(15904988398512253774)
XLA Ops:
  0.0 1.3 %copy.17 = bf16[24,64,128]{2,0,1:T(8,128)(2,1)S(1)} copy(bf16[24,64,128]{2,1,0:T(8,128)(2,1)} %param.6) | data formatting | bytes 786432
  1.3 0.0 copy-start.1
  1.4 0.9 %maximum_bitcast_fusion.1 = bf16[16,6,24,128]{3,2,1,0:T(8,128)(2,1)} fusion(bf16[24,16,2,128]{3,0,2,1:T(8,128)(2,1)S(1)} %slice.17, bf16[24,16,4,128]{3,0,2,1:T(8,128)(2,1)S(1)} %slice.16), kind=kLoop, calls=%fused_computation.1 | loop fusion | flops 294912 | bytes 1179648 | tf_op jit(solution)/shard_map/transpose | solution.py:15
  2.3 0.0 copy-start.2
  2.3 0.0 copy-start.3
  2.3 6.7 %all-to-all-start = ((bf16[16,6,24,128]{3,2,1,0:T(8,128)(2,1)}), bf16[16,6,24,128]{3,2,1,0:T(8,128)(2,1)S(1)}, u32[]{:S(2)}, u32[]{:S(2)}) async-start(bf16[16,6,24,128]{3,2,1,0:T(8,128)(2,1)} %maximum_bitcast_fusion.1), calls=%async_computation | async-start | bytes 1179648 | tf_op jit(solution)/shard_map/all_to_all | solution.py:16
  9.0 0.0 copy-done.1
  9.0 0.2 copy.12
  9.1 3.3 %collective-permute-start = (bf16[192,1,256]{2,0,1:T(8,128)(2,1)S(1)}, bf16[192,1,256]{2,0,1:T(8,128)(2,1)S(1)}, u32[]{:S(2)}, u32[]{:S(2)}) collective-permute-start(bf16[192,1,256]{2,0,1:T(8,128)(2,1)S(1)} %get-tuple-element.5), channel_id=1, source_target_pairs={{0,1},{1,2},{2,3},{3,4},{4,5},{5,6},{6,7},{7,8},{8,9},{9,10},{10,1... | collective-permute-start | bytes 294920 | tf_op jit(solution)/shard_map/ppermute | solution.py:25
  12.5 1.9 %collective-permute-start.1 = (bf16[192,1,256]{2,0,1:T(8,128)(2,1)S(1)}, bf16[192,1,256]{2,0,1:T(8,128)(2,1)S(1)}, u32[]{:S(2)}, u32[]{:S(2)}) collective-permute-start(bf16[192,1,256]{2,0,1:T(8,128)(2,1)S(1)} %get-tuple-element.6), channel_id=1, source_target_pairs={{1,0},{2,1},{3,2},{4,3},{5,4},{6,5},{7,6},{8,7},{9,8},{10,9},{11,1... | collective-permute-start | bytes 294920 | tf_op jit(solution)/shard_map/ppermute | solution.py:26
  14.4 0.0 copy-done.2
  14.4 0.1 copy.15.b3_ref
  14.6 0.0 copy-done.3
  14.6 0.1 copy.16.bu_ref
  14.7 0.1 add_convert_fusion.flags
  14.8 8.6 %collective-permute-done = bf16[192,1,256]{2,0,1:T(8,128)(2,1)S(1)} collective-permute-done((bf16[192,1,256]{2,0,1:T(8,128)(2,1)S(1)}, bf16[192,1,256]{2,0,1:T(8,128)(2,1)S(1)}, u32[]{:S(2)}, u32[]{:S(2)}) %collective-permute-start) | collective-permute-done | bytes 98336 | tf_op jit(solution)/shard_map/ppermute | solution.py:25
  23.4 1.7 %collective-permute-done.1 = bf16[192,1,256]{2,0,1:T(8,128)(2,1)S(1)} collective-permute-done((bf16[192,1,256]{2,0,1:T(8,128)(2,1)S(1)}, bf16[192,1,256]{2,0,1:T(8,128)(2,1)S(1)}, u32[]{:S(2)}, u32[]{:S(2)}) %collective-permute-start.1) | collective-permute-done | bytes 98336 | tf_op jit(solution)/shard_map/ppermute | solution.py:26
  25.0 0.1 maximum_bitcast_fusion.sk_ref
  25.2 3.5 %shard_map.64.part_hbm = f32[192,2048]{1,0:T(8,128)S(1)} custom-call(bf16[10,192,256]{2,1,0:T(8,128)(2,1)S(1)} %maximum_bitcast_fusion.sk_ref, bf16[3,576,384]{2,1,0:T(8,128)(2,1)} %bitcast.18, f32[192,1]{1,0:T(8,128)S(1)} %copy.15.b3_ref), custom_call_target="tpu_custom_call" | custom-call | flops 1358954496 | bytes 3883008 | tf_op jit(solution)/shard_map/pallas_call | solution.py:165
  28.6 0.0 copy-start
  28.7 1.1 %copy-done = f32[192,2048]{1,0:T(8,128)} copy-done((f32[192,2048]{1,0:T(8,128)}, f32[192,2048]{1,0:T(8,128)S(1)}, u32[]{:S(2)}) %copy-start) | copy-done | bytes 1572888
  29.8 0.0 all-to-all-done.xw_ref
  29.8 9.8 %shard_map.65 = bf16[192,8,256]{2,1,0:T(8,128)(2,1)} custom-call(s32[2]{0:T(128)S(1)} %add_convert_fusion.flags, bf16[16,6,24,128]{3,2,1,0:T(8,128)(2,1)S(1)} %all-to-all-done.xw_ref, f32[192,2048]{1,0:T(8,128)} %copy-done, bf16[4,768,384]{2,1,0:T(8,128)(2,1)} %bitcast.17, f32[192,1]{1,0:T(8,128)S(1)} %copy.16.bu_ref, bf16[3,576,384]{2,1,0:T(8,128)(2,1)} %bitcast.19), custom_call_target="tpu_custom_call" | custom-call | tf_op jit(solution)/shard_map/pallas_call | solution.py:142
  (4 shorter events, 0.1 us)
Async XLA Ops:
  1.3 7.7 %copy-start.1 = (bf16[192,8,256]{2,1,0:T(8,128)(2,1)S(1)}, bf16[192,8,256]{2,1,0:T(8,128)(2,1)}, u32[]{:S(2)}) copy-start(bf16[192,8,256]{2,1,0:T(8,128)(2,1)} %param.7) | copy-start | bytes 2359300
  2.3 12.2 %copy-start.2 = (f32[192]{0:T(256)S(1)}, f32[192]{0:T(256)}, u32[]{:S(2)}) copy-start(f32[192]{0:T(256)} %param.11) | copy-start | bytes 2308
  2.3 12.3 %copy-start.3 = (f32[192]{0:T(256)S(1)}, f32[192]{0:T(256)}, u32[]{:S(2)}) copy-start(f32[192]{0:T(256)} %param.9) | copy-start | bytes 2308
  2.3 27.5 %all-to-all-start = ((bf16[16,6,24,128]{3,2,1,0:T(8,128)(2,1)}), bf16[16,6,24,128]{3,2,1,0:T(8,128)(2,1)S(1)}, u32[]{:S(2)}, u32[]{:S(2)}) async-start(bf16[16,6,24,128]{3,2,1,0:T(8,128)(2,1)} %maximum_bitcast_fusion.1), calls=%async_computation | async-start | bytes 1179648 | tf_op jit(solution)/shard_map/all_to_all | solution.py:16
  9.1 14.2 %collective-permute-start = (bf16[192,1,256]{2,0,1:T(8,128)(2,1)S(1)}, bf16[192,1,256]{2,0,1:T(8,128)(2,1)S(1)}, u32[]{:S(2)}, u32[]{:S(2)}) collective-permute-start(bf16[192,1,256]{2,0,1:T(8,128)(2,1)S(1)} %get-tuple-element.5), channel_id=1, source_target_pairs={{0,1},{1,2},{2,3},{3,4},{4,5},{5,6},{6,7},{7,8},{8,9},{9,10},{10,1... | collective-permute-start | bytes 294920 | tf_op jit(solution)/shard_map/ppermute | solution.py:25
  12.5 12.5 %collective-permute-start.1 = (bf16[192,1,256]{2,0,1:T(8,128)(2,1)S(1)}, bf16[192,1,256]{2,0,1:T(8,128)(2,1)S(1)}, u32[]{:S(2)}, u32[]{:S(2)}) collective-permute-start(bf16[192,1,256]{2,0,1:T(8,128)(2,1)S(1)} %get-tuple-element.6), channel_id=1, source_target_pairs={{1,0},{2,1},{3,2},{4,3},{5,4},{6,5},{7,6},{8,7},{9,8},{10,9},{11,1... | collective-permute-start | bytes 294920 | tf_op jit(solution)/shard_map/ppermute | solution.py:26
  28.6 1.1 %copy-start = (f32[192,2048]{1,0:T(8,128)}, f32[192,2048]{1,0:T(8,128)S(1)}, u32[]{:S(2)}) copy-start(f32[192,2048]{1,0:T(8,128)S(1)} %shard_map.64.part_hbm) | copy-start | bytes 4718596

commit v20 on v11

--- a/solution.py
+++ b/solution.py
@@ -37,13 +37,21 @@
 def decoder_kernel(flags, xw_ref, sk_ref, wu_hbm, bu_ref, w3_hbm, b3_ref, out_ref, act_ref, wu_ref, w3_ref, sems):
     cin = wu_hbm.shape[2]
 
-    def load(src, dst, k):
-        copy = pltpu.make_async_copy(src, dst, sems.at[k])
-        copy.start()
-        return copy
+    count = []
 
-    up_loads = [[load(wu_hbm.at[p + 2 * h], wu_ref.at[p, :, pl.ds(h * cin, cin)], 2 * p + h) for h in range(2)] for p in range(2)]
-    conv_loads = [load(w3_hbm.at[ky], w3_ref.at[:, pl.ds(ky * cin, cin)], 4 + ky) for ky in range(3)]
+    def load(src, dst):
+        rows = src.shape[0]
+        step = rows // 4 if rows % 64 == 0 else rows
+        copies = []
+        for r0 in range(0, rows, step):
+            copy = pltpu.make_async_copy(src.at[pl.ds(r0, step)], dst.at[pl.ds(r0, step)], sems.at[len(count)])
+            count.append(r0)
+            copy.start()
+            copies.append(copy)
+        return copies
+
+    up_loads = [sum([load(wu_hbm.at[p + 2 * h], wu_ref.at[p, :, pl.ds(h * cin, cin)]) for h in range(2)], []) for p in range(2)]
+    conv_loads = sum([load(w3_hbm.at[ky], w3_ref.at[:, pl.ds(ky * cin, cin)]) for ky in range(3)], [])
     peers, nwin, groups, cw = xw_ref.shape
     nfine, cout, fw = sk_ref.shape
     nout = nfine - 2
@@ -116,7 +124,7 @@
             pltpu.VMEM((cout, nfine - 2, fw), jnp.float32),
             pltpu.VMEM((2, wu.shape[1], 2 * wu.shape[2]), wu.dtype),
             pltpu.VMEM((w3.shape[1], 3 * w3.shape[2]), w3.dtype),
-            pltpu.SemaphoreType.DMA((7,)),
+            pltpu.SemaphoreType.DMA((28,)),
         ],
         compiler_params=pltpu.CompilerParams(vmem_limit_bytes=48 * 1024 * 1024),
     )(flags, xw, sk, pltpu.with_memory_space_constraint(wu, pltpu.HBM), bu, pltpu.with_memory_space_constraint(w3, pltpu.HBM), b3)

time: 35.4 us -> 35.7 us (level)
  no operation moved by 1% of the time
where the time goes in v20:
time: 35.7 us; the launch traced here: 35.2 us
  starting transfers between devices  11.8 us (33%)
  waiting for transfers between devices  10.3 us (29%)
  Pallas kernels  10.2 us (29%)
  local copies, waits for them, and re-layouts  1.78 us (5%)
  other arithmetic  1.07 us (3%)
    pallas_call x1, Pallas kernels, decode(): pl.pallas_call(decoder_kernel, out_shape=jax.ShapeDtypeStruct((cout, nfin...  10.2 us
    ppermute x1, waiting for transfers between devices, skip_rows(): before = lax.ppermute(skip[:, -1:], 'row', up)  8.59 us
    all_to_all x1, starting transfers between devices, coarse_windows(): gathered = lax.all_to_all(windows, 'row', 0, 0, tiled=True)  6.55 us
    ppermute x1, starting transfers between devices, skip_rows(): before = lax.ppermute(skip[:, -1:], 'row', up)  3.34 us
    ppermute x1, starting transfers between devices, skip_rows(): after = lax.ppermute(skip[:, :1], 'row', down)  1.92 us
    ppermute x1, waiting for transfers between devices, skip_rows(): after = lax.ppermute(skip[:, :1], 'row', down)  1.67 us
    unnamed x8, local copies, waits for them, and re-layouts  1.43 us
    transpose x1, other arithmetic, coarse_windows(): windows = jnp.transpose(windows, (1, 2, 0, 3))  0.87 us
  transfers between devices with their start and end apart: 3, of which 2 were waited for; matrix products, arithmetic and copies ran while one was open for 2% of the time, Pallas kernels for 0%

profile of v20, /device:TPU:13, one launch (start us, length us, event | category | flops | bytes accessed | tf_op | source)
XLA Modules:
  0.0 35.2 jit_solution(14087885653433072788)
XLA Ops:
  0.0 1.3 %copy.17 = bf16[24,64,128]{2,0,1:T(8,128)(2,1)S(1)} copy(bf16[24,64,128]{2,1,0:T(8,128)(2,1)} %param.6) | data formatting | bytes 786432
  1.3 0.0 copy-start
  1.4 0.0 copy-start.1
  1.4 0.0 copy-start.2
  1.4 0.9 %maximum_bitcast_fusion.1 = bf16[16,6,24,128]{3,2,1,0:T(8,128)(2,1)} fusion(bf16[24,16,2,128]{3,0,2,1:T(8,128)(2,1)S(1)} %slice.17, bf16[24,16,4,128]{3,0,2,1:T(8,128)(2,1)S(1)} %slice.16), kind=kLoop, calls=%fused_computation.1 | loop fusion | flops 294912 | bytes 1179648 | tf_op jit(solution)/shard_map/transpose | solution.py:15
  2.3 6.6 %all-to-all-start = ((bf16[16,6,24,128]{3,2,1,0:T(8,128)(2,1)}), bf16[16,6,24,128]{3,2,1,0:T(8,128)(2,1)S(1)}, u32[]{:S(2)}, u32[]{:S(2)}) async-start(bf16[16,6,24,128]{3,2,1,0:T(8,128)(2,1)} %maximum_bitcast_fusion.1), calls=%async_computation | async-start | bytes 1179648 | tf_op jit(solution)/shard_map/all_to_all | solution.py:16
  8.8 0.0 copy-done
  8.8 0.2 copy.12
  9.0 3.3 %collective-permute-start = (bf16[192,1,256]{2,0,1:T(8,128)(2,1)S(1)}, bf16[192,1,256]{2,0,1:T(8,128)(2,1)S(1)}, u32[]{:S(2)}, u32[]{:S(2)}) collective-permute-start(bf16[192,1,256]{2,0,1:T(8,128)(2,1)S(1)} %get-tuple-element.5), channel_id=1, source_target_pairs={{0,1},{1,2},{2,3},{3,4},{4,5},{5,6},{6,7},{7,8},{8,9},{9,10},{10,1... | collective-permute-start | bytes 294920 | tf_op jit(solution)/shard_map/ppermute | solution.py:25
  12.4 1.9 %collective-permute-start.1 = (bf16[192,1,256]{2,0,1:T(8,128)(2,1)S(1)}, bf16[192,1,256]{2,0,1:T(8,128)(2,1)S(1)}, u32[]{:S(2)}, u32[]{:S(2)}) collective-permute-start(bf16[192,1,256]{2,0,1:T(8,128)(2,1)S(1)} %get-tuple-element.6), channel_id=1, source_target_pairs={{1,0},{2,1},{3,2},{4,3},{5,4},{6,5},{7,6},{8,7},{9,8},{10,9},{11,1... | collective-permute-start | bytes 294920 | tf_op jit(solution)/shard_map/ppermute | solution.py:26
  14.3 0.0 copy-done.1
  14.3 0.1 copy.15.bu_ref
  14.5 0.0 copy-done.2
  14.5 0.1 copy.16.b3_ref
  14.6 0.1 add_convert_fusion.flags
  14.7 8.6 %collective-permute-done = bf16[192,1,256]{2,0,1:T(8,128)(2,1)S(1)} collective-permute-done((bf16[192,1,256]{2,0,1:T(8,128)(2,1)S(1)}, bf16[192,1,256]{2,0,1:T(8,128)(2,1)S(1)}, u32[]{:S(2)}, u32[]{:S(2)}) %collective-permute-start) | collective-permute-done | bytes 98336 | tf_op jit(solution)/shard_map/ppermute | solution.py:25
  23.2 1.7 %collective-permute-done.1 = bf16[192,1,256]{2,0,1:T(8,128)(2,1)S(1)} collective-permute-done((bf16[192,1,256]{2,0,1:T(8,128)(2,1)S(1)}, bf16[192,1,256]{2,0,1:T(8,128)(2,1)S(1)}, u32[]{:S(2)}, u32[]{:S(2)}) %collective-permute-start.1) | collective-permute-done | bytes 98336 | tf_op jit(solution)/shard_map/ppermute | solution.py:26
  24.9 0.1 maximum_bitcast_fusion.sk_ref
  25.0 0.0 all-to-all-done.xw_ref
  25.1 10.2 %shard_map.64 = bf16[192,8,256]{2,1,0:T(8,128)(2,1)} custom-call(s32[2]{0:T(128)S(1)} %add_convert_fusion.flags, bf16[16,6,24,128]{3,2,1,0:T(8,128)(2,1)S(1)} %all-to-all-done.xw_ref, bf16[10,192,256]{2,1,0:T(8,128)(2,1)S(1)} %maximum_bitcast_fusion.sk_ref, bf16[4,768,384]{2,1,0:T(8,128)(2,1)} %bitcast.17, f32[192,1]{1,0:T(8,128)S(1)} %copy.15.bu_ref, ...), custom_call_target="tpu_custom_call" | custom-call | tf_op jit(solution)/shard_map/pallas_call | solution.py:118
  (4 shorter events, 0.1 us)
Async XLA Ops:
  1.3 7.6 %copy-start = (bf16[192,8,256]{2,1,0:T(8,128)(2,1)S(1)}, bf16[192,8,256]{2,1,0:T(8,128)(2,1)}, u32[]{:S(2)}) copy-start(bf16[192,8,256]{2,1,0:T(8,128)(2,1)} %param.7) | copy-start | bytes 2359300
  1.4 13.0 %copy-start.1 = (f32[192]{0:T(256)S(1)}, f32[192]{0:T(256)}, u32[]{:S(2)}) copy-start(f32[192]{0:T(256)} %param.9) | copy-start | bytes 2308
  1.4 13.1 %copy-start.2 = (f32[192]{0:T(256)S(1)}, f32[192]{0:T(256)}, u32[]{:S(2)}) copy-start(f32[192]{0:T(256)} %param.11) | copy-start | bytes 2308
  2.3 22.8 %all-to-all-start = ((bf16[16,6,24,128]{3,2,1,0:T(8,128)(2,1)}), bf16[16,6,24,128]{3,2,1,0:T(8,128)(2,1)S(1)}, u32[]{:S(2)}, u32[]{:S(2)}) async-start(bf16[16,6,24,128]{3,2,1,0:T(8,128)(2,1)} %maximum_bitcast_fusion.1), calls=%async_computation | async-start | bytes 1179648 | tf_op jit(solution)/shard_map/all_to_all | solution.py:16
  9.0 14.2 %collective-permute-start = (bf16[192,1,256]{2,0,1:T(8,128)(2,1)S(1)}, bf16[192,1,256]{2,0,1:T(8,128)(2,1)S(1)}, u32[]{:S(2)}, u32[]{:S(2)}) collective-permute-start(bf16[192,1,256]{2,0,1:T(8,128)(2,1)S(1)} %get-tuple-element.5), channel_id=1, source_target_pairs={{0,1},{1,2},{2,3},{3,4},{4,5},{5,6},{6,7},{7,8},{8,9},{9,10},{10,1... | collective-permute-start | bytes 294920 | tf_op jit(solution)/shard_map/ppermute | solution.py:25
  12.4 12.5 %collective-permute-start.1 = (bf16[192,1,256]{2,0,1:T(8,128)(2,1)S(1)}, bf16[192,1,256]{2,0,1:T(8,128)(2,1)S(1)}, u32[]{:S(2)}, u32[]{:S(2)}) collective-permute-start(bf16[192,1,256]{2,0,1:T(8,128)(2,1)S(1)} %get-tuple-element.6), channel_id=1, source_target_pairs={{1,0},{2,1},{3,2},{4,3},{5,4},{6,5},{7,6},{8,7},{9,8},{10,9},{11,1... | collective-permute-start | bytes 294920 | tf_op jit(solution)/shard_map/ppermute | solution.py:26

commit v21 on v11

--- a/solution.py
+++ b/solution.py
@@ -56,8 +56,7 @@
     def window_row(i):
         if peers == 1:
             return xw_ref[0, i]
-        pieces = [xw_ref[s, i].astype(f32) for s in range(peers)]
-        return jnp.concatenate(pieces, axis=0).astype(jnp.bfloat16)
+        return jnp.concatenate([xw_ref[s, i] for s in range(peers)], axis=0)
 
     wide = jnp.concatenate([window_row(i) for i in range(nwin)], axis=1)
     stacked = jnp.concatenate([wide[:, cw:], wide[:, :span]], axis=0)

time: 35.4 us -> 35.4 us (level)
  no operation moved by 1% of the time
where the time goes in v21:
time: 35.4 us; the launch traced here: 34.9 us
  starting transfers between devices  11.8 us (33%)
  waiting for transfers between devices  10.3 us (29%)
  Pallas kernels  9.88 us (28%)
  local copies, waits for them, and re-layouts  1.78 us (5%)
  other arithmetic  1.07 us (3%)
    pallas_call x1, Pallas kernels, decode(): pl.pallas_call(decoder_kernel, out_shape=jax.ShapeDtypeStruct((cout, nfin...  9.88 us
    ppermute x1, waiting for transfers between devices, skip_rows(): before = lax.ppermute(skip[:, -1:], 'row', up)  8.59 us
    all_to_all x1, starting transfers between devices, coarse_windows(): gathered = lax.all_to_all(windows, 'row', 0, 0, tiled=True)  6.55 us
    ppermute x1, starting transfers between devices, skip_rows(): before = lax.ppermute(skip[:, -1:], 'row', up)  3.34 us
    ppermute x1, starting transfers between devices, skip_rows(): after = lax.ppermute(skip[:, :1], 'row', down)  1.92 us
    ppermute x1, waiting for transfers between devices, skip_rows(): after = lax.ppermute(skip[:, :1], 'row', down)  1.67 us
    unnamed x8, local copies, waits for them, and re-layouts  1.43 us
    transpose x1, other arithmetic, coarse_windows(): windows = jnp.transpose(windows, (1, 2, 0, 3))  0.87 us
  transfers between devices with their start and end apart: 3, of which 2 were waited for; matrix products, arithmetic and copies ran while one was open for 2% of the time, Pallas kernels for 0%

profile of v21, /device:TPU:13, one launch (start us, length us, event | category | flops | bytes accessed | tf_op | source)
XLA Modules:
  0.0 34.9 jit_solution(5463010380299356892)
XLA Ops:
  0.0 1.3 %copy.17 = bf16[24,64,128]{2,0,1:T(8,128)(2,1)S(1)} copy(bf16[24,64,128]{2,1,0:T(8,128)(2,1)} %param.6) | data formatting | bytes 786432
  1.3 0.0 copy-start
  1.4 0.0 copy-start.1
  1.4 0.0 copy-start.2
  1.4 0.9 %maximum_bitcast_fusion.1 = bf16[16,6,24,128]{3,2,1,0:T(8,128)(2,1)} fusion(bf16[24,16,2,128]{3,0,2,1:T(8,128)(2,1)S(1)} %slice.17, bf16[24,16,4,128]{3,0,2,1:T(8,128)(2,1)S(1)} %slice.16), kind=kLoop, calls=%fused_computation.1 | loop fusion | flops 294912 | bytes 1179648 | tf_op jit(solution)/shard_map/transpose | solution.py:15
  2.3 6.6 %all-to-all-start = ((bf16[16,6,24,128]{3,2,1,0:T(8,128)(2,1)}), bf16[16,6,24,128]{3,2,1,0:T(8,128)(2,1)S(1)}, u32[]{:S(2)}, u32[]{:S(2)}) async-start(bf16[16,6,24,128]{3,2,1,0:T(8,128)(2,1)} %maximum_bitcast_fusion.1), calls=%async_computation | async-start | bytes 1179648 | tf_op jit(solution)/shard_map/all_to_all | solution.py:16
  8.8 0.0 copy-done
  8.8 0.2 copy.12
  9.0 3.3 %collective-permute-start = (bf16[192,1,256]{2,0,1:T(8,128)(2,1)S(1)}, bf16[192,1,256]{2,0,1:T(8,128)(2,1)S(1)}, u32[]{:S(2)}, u32[]{:S(2)}) collective-permute-start(bf16[192,1,256]{2,0,1:T(8,128)(2,1)S(1)} %get-tuple-element.5), channel_id=1, source_target_pairs={{0,1},{1,2},{2,3},{3,4},{4,5},{5,6},{6,7},{7,8},{8,9},{9,10},{10,1... | collective-permute-start | bytes 294920 | tf_op jit(solution)/shard_map/ppermute | solution.py:25
  12.4 1.9 %collective-permute-start.1 = (bf16[192,1,256]{2,0,1:T(8,128)(2,1)S(1)}, bf16[192,1,256]{2,0,1:T(8,128)(2,1)S(1)}, u32[]{:S(2)}, u32[]{:S(2)}) collective-permute-start(bf16[192,1,256]{2,0,1:T(8,128)(2,1)S(1)} %get-tuple-element.6), channel_id=1, source_target_pairs={{1,0},{2,1},{3,2},{4,3},{5,4},{6,5},{7,6},{8,7},{9,8},{10,9},{11,1... | collective-permute-start | bytes 294920 | tf_op jit(solution)/shard_map/ppermute | solution.py:26
  14.3 0.0 copy-done.1
  14.3 0.1 copy.15.bu_ref
  14.5 0.0 copy-done.2
  14.5 0.1 copy.16.b3_ref
  14.6 0.1 add_convert_fusion.flags
  14.7 8.6 %collective-permute-done = bf16[192,1,256]{2,0,1:T(8,128)(2,1)S(1)} collective-permute-done((bf16[192,1,256]{2,0,1:T(8,128)(2,1)S(1)}, bf16[192,1,256]{2,0,1:T(8,128)(2,1)S(1)}, u32[]{:S(2)}, u32[]{:S(2)}) %collective-permute-start) | collective-permute-done | bytes 98336 | tf_op jit(solution)/shard_map/ppermute | solution.py:25
  23.2 1.7 %collective-permute-done.1 = bf16[192,1,256]{2,0,1:T(8,128)(2,1)S(1)} collective-permute-done((bf16[192,1,256]{2,0,1:T(8,128)(2,1)S(1)}, bf16[192,1,256]{2,0,1:T(8,128)(2,1)S(1)}, u32[]{:S(2)}, u32[]{:S(2)}) %collective-permute-start.1) | collective-permute-done | bytes 98336 | tf_op jit(solution)/shard_map/ppermute | solution.py:26
  24.9 0.1 maximum_bitcast_fusion.sk_ref
  25.0 0.0 all-to-all-done.xw_ref
  25.1 9.9 %shard_map.64 = bf16[192,8,256]{2,1,0:T(8,128)(2,1)} custom-call(s32[2]{0:T(128)S(1)} %add_convert_fusion.flags, bf16[16,6,24,128]{3,2,1,0:T(8,128)(2,1)S(1)} %all-to-all-done.xw_ref, bf16[10,192,256]{2,1,0:T(8,128)(2,1)S(1)} %maximum_bitcast_fusion.sk_ref, bf16[4,768,384]{2,1,0:T(8,128)(2,1)} %bitcast.17, f32[192,1]{1,0:T(8,128)S(1)} %copy.15.bu_ref, ...), custom_call_target="tpu_custom_call" | custom-call | tf_op jit(solution)/shard_map/pallas_call | solution.py:109
  (4 shorter events, 0.1 us)
Async XLA Ops:
  1.3 7.6 %copy-start = (bf16[192,8,256]{2,1,0:T(8,128)(2,1)S(1)}, bf16[192,8,256]{2,1,0:T(8,128)(2,1)}, u32[]{:S(2)}) copy-start(bf16[192,8,256]{2,1,0:T(8,128)(2,1)} %param.7) | copy-start | bytes 2359300
  1.4 13.0 %copy-start.1 = (f32[192]{0:T(256)S(1)}, f32[192]{0:T(256)}, u32[]{:S(2)}) copy-start(f32[192]{0:T(256)} %param.9) | copy-start | bytes 2308
  1.4 13.1 %copy-start.2 = (f32[192]{0:T(256)S(1)}, f32[192]{0:T(256)}, u32[]{:S(2)}) copy-start(f32[192]{0:T(256)} %param.11) | copy-start | bytes 2308
  2.3 22.8 %all-to-all-start = ((bf16[16,6,24,128]{3,2,1,0:T(8,128)(2,1)}), bf16[16,6,24,128]{3,2,1,0:T(8,128)(2,1)S(1)}, u32[]{:S(2)}, u32[]{:S(2)}) async-start(bf16[16,6,24,128]{3,2,1,0:T(8,128)(2,1)} %maximum_bitcast_fusion.1), calls=%async_computation | async-start | bytes 1179648 | tf_op jit(solution)/shard_map/all_to_all | solution.py:16
  9.0 14.2 %collective-permute-start = (bf16[192,1,256]{2,0,1:T(8,128)(2,1)S(1)}, bf16[192,1,256]{2,0,1:T(8,128)(2,1)S(1)}, u32[]{:S(2)}, u32[]{:S(2)}) collective-permute-start(bf16[192,1,256]{2,0,1:T(8,128)(2,1)S(1)} %get-tuple-element.5), channel_id=1, source_target_pairs={{0,1},{1,2},{2,3},{3,4},{4,5},{5,6},{6,7},{7,8},{8,9},{9,10},{10,1... | collective-permute-start | bytes 294920 | tf_op jit(solution)/shard_map/ppermute | solution.py:25
  12.4 12.5 %collective-permute-start.1 = (bf16[192,1,256]{2,0,1:T(8,128)(2,1)S(1)}, bf16[192,1,256]{2,0,1:T(8,128)(2,1)S(1)}, u32[]{:S(2)}, u32[]{:S(2)}) collective-permute-start(bf16[192,1,256]{2,0,1:T(8,128)(2,1)S(1)} %get-tuple-element.6), channel_id=1, source_target_pairs={{1,0},{2,1},{3,2},{4,3},{5,4},{6,5},{7,6},{8,7},{9,8},{10,9},{11,1... | collective-permute-start | bytes 294920 | tf_op jit(solution)/shard_map/ppermute | solution.py:26

commit v22 on v11

--- a/solution.py
+++ b/solution.py
@@ -97,7 +97,7 @@
     pre = total[cout : 2 * cout]
     pre = pre + lane_shift(total[:cout], fw, 1) + lane_shift(total[2 * cout :], fw, -1)
     pre = pre + b3_ref[...]
-    act = pre / (1.0 + jnp.exp(-pre))
+    act = pre * jax.nn.sigmoid(pre)
     for y in range(nout):
         act_ref[:, y, :] = act[:, y * fw : (y + 1) * fw]
     out_ref[...] = act_ref[...].astype(out_ref.dtype)

time: 35.4 us -> 35.4 us (level)
  no operation moved by 1% of the time
where the time goes in v22:
time: 35.4 us; the launch traced here: 34.9 us
  starting transfers between devices  11.8 us (33%)
  waiting for transfers between devices  10.3 us (29%)
  Pallas kernels  9.87 us (28%)
  local copies, waits for them, and re-layouts  1.78 us (5%)
  other arithmetic  1.07 us (3%)
    pallas_call x1, Pallas kernels, decode(): pl.pallas_call(decoder_kernel, out_shape=jax.ShapeDtypeStruct((cout, nfin...  9.87 us
    ppermute x1, waiting for transfers between devices, skip_rows(): before = lax.ppermute(skip[:, -1:], 'row', up)  8.59 us
    all_to_all x1, starting transfers between devices, coarse_windows(): gathered = lax.all_to_all(windows, 'row', 0, 0, tiled=True)  6.55 us
    ppermute x1, starting transfers between devices, skip_rows(): before = lax.ppermute(skip[:, -1:], 'row', up)  3.34 us
    ppermute x1, starting transfers between devices, skip_rows(): after = lax.ppermute(skip[:, :1], 'row', down)  1.92 us
    ppermute x1, waiting for transfers between devices, skip_rows(): after = lax.ppermute(skip[:, :1], 'row', down)  1.67 us
    unnamed x8, local copies, waits for them, and re-layouts  1.43 us
    transpose x1, other arithmetic, coarse_windows(): windows = jnp.transpose(windows, (1, 2, 0, 3))  0.87 us
  transfers between devices with their start and end apart: 3, of which 2 were waited for; matrix products, arithmetic and copies ran while one was open for 2% of the time, Pallas kernels for 0%

profile of v22, /device:TPU:13, one launch (start us, length us, event | category | flops | bytes accessed | tf_op | source)
XLA Modules:
  0.0 34.9 jit_solution(5173372487776288383)
XLA Ops:
  0.0 1.3 %copy.17 = bf16[24,64,128]{2,0,1:T(8,128)(2,1)S(1)} copy(bf16[24,64,128]{2,1,0:T(8,128)(2,1)} %param.6) | data formatting | bytes 786432
  1.3 0.0 copy-start
  1.4 0.0 copy-start.1
  1.4 0.0 copy-start.2
  1.4 0.9 %maximum_bitcast_fusion.1 = bf16[16,6,24,128]{3,2,1,0:T(8,128)(2,1)} fusion(bf16[24,16,2,128]{3,0,2,1:T(8,128)(2,1)S(1)} %slice.17, bf16[24,16,4,128]{3,0,2,1:T(8,128)(2,1)S(1)} %slice.16), kind=kLoop, calls=%fused_computation.1 | loop fusion | flops 294912 | bytes 1179648 | tf_op jit(solution)/shard_map/transpose | solution.py:15
  2.3 6.6 %all-to-all-start = ((bf16[16,6,24,128]{3,2,1,0:T(8,128)(2,1)}), bf16[16,6,24,128]{3,2,1,0:T(8,128)(2,1)S(1)}, u32[]{:S(2)}, u32[]{:S(2)}) async-start(bf16[16,6,24,128]{3,2,1,0:T(8,128)(2,1)} %maximum_bitcast_fusion.1), calls=%async_computation | async-start | bytes 1179648 | tf_op jit(solution)/shard_map/all_to_all | solution.py:16
  8.8 0.0 copy-done
  8.8 0.2 copy.12
  9.0 3.3 %collective-permute-start = (bf16[192,1,256]{2,0,1:T(8,128)(2,1)S(1)}, bf16[192,1,256]{2,0,1:T(8,128)(2,1)S(1)}, u32[]{:S(2)}, u32[]{:S(2)}) collective-permute-start(bf16[192,1,256]{2,0,1:T(8,128)(2,1)S(1)} %get-tuple-element.5), channel_id=1, source_target_pairs={{0,1},{1,2},{2,3},{3,4},{4,5},{5,6},{6,7},{7,8},{8,9},{9,10},{10,1... | collective-permute-start | bytes 294920 | tf_op jit(solution)/shard_map/ppermute | solution.py:25
  12.4 1.9 %collective-permute-start.1 = (bf16[192,1,256]{2,0,1:T(8,128)(2,1)S(1)}, bf16[192,1,256]{2,0,1:T(8,128)(2,1)S(1)}, u32[]{:S(2)}, u32[]{:S(2)}) collective-permute-start(bf16[192,1,256]{2,0,1:T(8,128)(2,1)S(1)} %get-tuple-element.6), channel_id=1, source_target_pairs={{1,0},{2,1},{3,2},{4,3},{5,4},{6,5},{7,6},{8,7},{9,8},{10,9},{11,1... | collective-permute-start | bytes 294920 | tf_op jit(solution)/shard_map/ppermute | solution.py:26
  14.3 0.0 copy-done.1
  14.3 0.1 copy.15.bu_ref
  14.5 0.0 copy-done.2
  14.5 0.1 copy.16.b3_ref
  14.6 0.1 add_convert_fusion.flags
  14.7 8.6 %collective-permute-done = bf16[192,1,256]{2,0,1:T(8,128)(2,1)S(1)} collective-permute-done((bf16[192,1,256]{2,0,1:T(8,128)(2,1)S(1)}, bf16[192,1,256]{2,0,1:T(8,128)(2,1)S(1)}, u32[]{:S(2)}, u32[]{:S(2)}) %collective-permute-start) | collective-permute-done | bytes 98336 | tf_op jit(solution)/shard_map/ppermute | solution.py:25
  23.2 1.7 %collective-permute-done.1 = bf16[192,1,256]{2,0,1:T(8,128)(2,1)S(1)} collective-permute-done((bf16[192,1,256]{2,0,1:T(8,128)(2,1)S(1)}, bf16[192,1,256]{2,0,1:T(8,128)(2,1)S(1)}, u32[]{:S(2)}, u32[]{:S(2)}) %collective-permute-start.1) | collective-permute-done | bytes 98336 | tf_op jit(solution)/shard_map/ppermute | solution.py:26
  24.9 0.1 maximum_bitcast_fusion.sk_ref
  25.0 0.0 all-to-all-done.xw_ref
  25.1 9.9 %shard_map.64 = bf16[192,8,256]{2,1,0:T(8,128)(2,1)} custom-call(s32[2]{0:T(128)S(1)} %add_convert_fusion.flags, bf16[16,6,24,128]{3,2,1,0:T(8,128)(2,1)S(1)} %all-to-all-done.xw_ref, bf16[10,192,256]{2,1,0:T(8,128)(2,1)S(1)} %maximum_bitcast_fusion.sk_ref, bf16[4,768,384]{2,1,0:T(8,128)(2,1)} %bitcast.17, f32[192,1]{1,0:T(8,128)S(1)} %copy.15.bu_ref, ...), custom_call_target="tpu_custom_call" | custom-call | tf_op jit(solution)/shard_map/pallas_call | solution.py:110
  (4 shorter events, 0.1 us)
Async XLA Ops:
  1.3 7.6 %copy-start = (bf16[192,8,256]{2,1,0:T(8,128)(2,1)S(1)}, bf16[192,8,256]{2,1,0:T(8,128)(2,1)}, u32[]{:S(2)}) copy-start(bf16[192,8,256]{2,1,0:T(8,128)(2,1)} %param.7) | copy-start | bytes 2359300
  1.4 13.0 %copy-start.1 = (f32[192]{0:T(256)S(1)}, f32[192]{0:T(256)}, u32[]{:S(2)}) copy-start(f32[192]{0:T(256)} %param.9) | copy-start | bytes 2308
  1.4 13.1 %copy-start.2 = (f32[192]{0:T(256)S(1)}, f32[192]{0:T(256)}, u32[]{:S(2)}) copy-start(f32[192]{0:T(256)} %param.11) | copy-start | bytes 2308
  2.3 22.8 %all-to-all-start = ((bf16[16,6,24,128]{3,2,1,0:T(8,128)(2,1)}), bf16[16,6,24,128]{3,2,1,0:T(8,128)(2,1)S(1)}, u32[]{:S(2)}, u32[]{:S(2)}) async-start(bf16[16,6,24,128]{3,2,1,0:T(8,128)(2,1)} %maximum_bitcast_fusion.1), calls=%async_computation | async-start | bytes 1179648 | tf_op jit(solution)/shard_map/all_to_all | solution.py:16
  9.0 14.2 %collective-permute-start = (bf16[192,1,256]{2,0,1:T(8,128)(2,1)S(1)}, bf16[192,1,256]{2,0,1:T(8,128)(2,1)S(1)}, u32[]{:S(2)}, u32[]{:S(2)}) collective-permute-start(bf16[192,1,256]{2,0,1:T(8,128)(2,1)S(1)} %get-tuple-element.5), channel_id=1, source_target_pairs={{0,1},{1,2},{2,3},{3,4},{4,5},{5,6},{6,7},{7,8},{8,9},{9,10},{10,1... | collective-permute-start | bytes 294920 | tf_op jit(solution)/shard_map/ppermute | solution.py:25
  12.4 12.5 %collective-permute-start.1 = (bf16[192,1,256]{2,0,1:T(8,128)(2,1)S(1)}, bf16[192,1,256]{2,0,1:T(8,128)(2,1)S(1)}, u32[]{:S(2)}, u32[]{:S(2)}) collective-permute-start(bf16[192,1,256]{2,0,1:T(8,128)(2,1)S(1)} %get-tuple-element.6), channel_id=1, source_target_pairs={{1,0},{2,1},{3,2},{4,3},{5,4},{6,5},{7,6},{8,7},{9,8},{10,9},{11,1... | collective-permute-start | bytes 294920 | tf_op jit(solution)/shard_map/ppermute | solution.py:26
